TPU v7x, 512 devices: a whole 4x4x16 slice. The times are simulated.
512 devices in a mesh: req: 64 (over z, x_lo, core), tp: 8 (over x_hi, y).
Axes of the slice: x: 4 (x_hi: 2, x_lo: 2; x = x_hi * 2 + x_lo), y: 4, z: 16, core: 2. Of those that a mesh axis runs over, the one named last changes fastest.
Arguments:
- queries: bfloat16 [8192, 8192], P('req', 'tp'), may hold values from -16 to 16
- span_rotated_keys: bfloat16 [8192, 1024], P('req', 'tp'), may hold values from -6 to 6
- span_token_values: bfloat16 [8192, 1024], P('req', 'tp'), may hold values from -6 to 6
- cache_keys: bfloat16 [65536, 1024], P('req', 'tp'), may hold values from -6 to 6
- prompt_cache_values: bfloat16 [65536, 1024], P('req', 'tp'), may hold values from -6 to 6
- lengths: int32 [8], replicated, may hold values from 2 to 8192, as said below
Outputs:
- attention: bfloat16 [8192, 8192], P(('req', 'tp'))
Inputs may be any that keep to these rules, and one draw needn't show every extreme that they name: `lengths`: each group's cached prompt length; one group's is exactly 8192.
All inputs are finite; a program needn't handle non-finite values.
Results may differ from a plain program's by a relative error of at most 0.0045.
Values may be sent and summed in bfloat16 or wider, within the bound.
No kernel may reach another device: no remote copies, remote signals or barrier semaphores. Data moves between devices by JAX's collectives and lax.ppermute only.
A program may use at most 64 MiB of HBM per device.

v0:
```python
import math

import jax
import jax.numpy as jnp
from jax import lax
from jax.sharding import PartitionSpec as P

HEAD_SIZE = 128
GROUP_DEVS = 8


NEG_FILL = -1e30


def partner(value, axis, distance):
    mask = 2**distance
    pairs = [(source, source ^ mask) for source in range(lax.axis_size(axis))]
    return lax.ppermute(value, axis, pairs)


def heads_first(matrix, kv_heads):
    row_count = matrix.shape[0]
    return matrix.reshape(row_count, kv_heads, HEAD_SIZE).transpose(1, 0, 2)


def query_layout(query_block, kv_heads):
    token_count = query_block.shape[0]
    heads_per_group = query_block.shape[1] // (kv_heads * HEAD_SIZE)
    shaped = query_block.reshape(token_count, kv_heads, heads_per_group, HEAD_SIZE).transpose(
        1, 2, 0, 3
    )
    return shaped.reshape(kv_heads, heads_per_group * token_count, HEAD_SIZE)


def empty_state(kv_heads, row_count):
    return (
        jnp.full((kv_heads, row_count), NEG_FILL, jnp.float32),
        jnp.zeros((kv_heads, row_count), jnp.float32),
        jnp.zeros((kv_heads, row_count, HEAD_SIZE), jnp.float32),
    )


def absorb(online, query_rows, key_block, value_block, allowed):
    run_max, run_sum, run_acc = online
    scores = jnp.einsum(
        "jqd,jkd->jqk", query_rows, key_block, preferred_element_type=jnp.float32
    ) * (1.0 / math.sqrt(HEAD_SIZE))
    scores = jnp.where(allowed[None], scores, NEG_FILL)
    new_max = jnp.maximum(run_max, jnp.max(scores, axis=-1))
    weights = jnp.where(allowed[None], jnp.exp(scores - new_max[..., None]), 0.0)
    factor = jnp.exp(run_max - new_max)
    run_sum = run_sum * factor + jnp.sum(weights, axis=-1)
    run_acc = run_acc * factor[..., None] + jnp.einsum(
        "jqk,jkd->jqd",
        weights.astype(jnp.bfloat16),
        value_block,
        preferred_element_type=jnp.float32,
    )
    return (new_max, run_sum, run_acc)


def sweep(online, query_rows, key_rows, value_rows, live_rows, allowed_at):
    kv_heads = query_rows.shape[0]
    block_rows = math.gcd(key_rows.shape[0], 512)
    block_count = (live_rows + block_rows - 1) // block_rows

    def advance(block_index, inner_state):
        offset = block_index * block_rows
        key_block = heads_first(lax.dynamic_slice_in_dim(key_rows, offset, block_rows, 0), kv_heads)
        value_block = heads_first(
            lax.dynamic_slice_in_dim(value_rows, offset, block_rows, 0), kv_heads
        )
        return absorb(
            inner_state,
            query_rows,
            key_block,
            value_block,
            allowed_at(offset + jnp.arange(block_rows, dtype=jnp.int32)),
        )

    return lax.fori_loop(0, block_count, advance, online)


def cache_mask(first_row, group_length):

    def allowed_at(offsets):
        return (first_row + offsets < group_length)[None, :]

    return allowed_at


def span_mask(first_pos, query_pos):

    def allowed_at(offsets):
        return (first_pos + offsets)[None, :] <= query_pos[:, None]

    return allowed_at


def merge_parts(first_part, second_part):
    new_max = jnp.maximum(first_part[0], second_part[0])
    scale_one = jnp.exp(first_part[0] - new_max)
    scale_two = jnp.exp(second_part[0] - new_max)
    return (
        new_max,
        first_part[1] * scale_one + second_part[1] * scale_two,
        first_part[2] * scale_one[..., None] + second_part[2] * scale_two[..., None],
    )


def finish(online, token_count):
    run_max, run_sum, run_acc = online
    kv_heads = run_acc.shape[0]
    heads_per_group = run_acc.shape[1] // token_count
    output = run_acc / run_sum[..., None]
    output = output.reshape(kv_heads, heads_per_group, token_count, HEAD_SIZE).transpose(2, 0, 1, 3)
    return output.reshape(token_count, kv_heads * heads_per_group * HEAD_SIZE).astype(jnp.bfloat16)


def body(queries, span_rotated_keys, span_token_values, cache_keys, prompt_cache_values, lengths):
    kv_heads = span_rotated_keys.shape[1] // HEAD_SIZE
    tok_rows = queries.shape[0]
    cache_rows = cache_keys.shape[0]
    heads_per_group = queries.shape[1] // (kv_heads * HEAD_SIZE)
    bit_count = GROUP_DEVS.bit_length() - 1
    device = lax.axis_index("req")
    position = device % GROUP_DEVS
    group_length = lax.dynamic_index_in_dim(lengths, device // GROUP_DEVS, 0, keepdims=False)
    own_sets = queries
    for level in range(bit_count):
        peer_part = partner(own_sets, "req", level)
        mine_first = position >> level & 1 == 0
        own_sets = jnp.where(
            mine_first,
            jnp.concatenate([own_sets, peer_part], 0),
            jnp.concatenate([peer_part, own_sets], 0),
        )
    stacked = own_sets.reshape(GROUP_DEVS, tok_rows, own_sets.shape[1])
    first_row = position * cache_rows
    live_rows = jnp.clip(group_length - first_row, 0, cache_rows)

    def one_block(inputs):
        query_block, block_index = inputs
        query_rows = query_layout(query_block, kv_heads)
        query_pos = (
            block_index * tok_rows
            + jnp.arange(heads_per_group * tok_rows, dtype=jnp.int32) % tok_rows
        )
        online = empty_state(kv_heads, heads_per_group * tok_rows)
        online = sweep(
            online,
            query_rows,
            cache_keys,
            prompt_cache_values,
            live_rows,
            cache_mask(first_row, group_length),
        )
        return sweep(
            online,
            query_rows,
            span_rotated_keys,
            span_token_values,
            tok_rows,
            span_mask(position * tok_rows, query_pos),
        )

    partials = lax.map(one_block, (stacked, jnp.arange(GROUP_DEVS, dtype=jnp.int32)))
    for level in reversed(range(bit_count)):
        half_size = 1 << level
        upper_half = position >> level & 1 == 1
        kept_part = tuple(
            (jnp.where(upper_half, member[half_size:], member[:half_size]) for member in partials)
        )
        sent_part = tuple(
            (jnp.where(upper_half, member[:half_size], member[half_size:]) for member in partials)
        )
        gotten = partner(sent_part, "req", level)
        partials = merge_parts(kept_part, gotten)
    attended = finish(tuple((member[0] for member in partials)), tok_rows)
    return lax.all_to_all(attended, "tp", split_axis=0, concat_axis=1, tiled=True)


def solution(mesh):
    in_specs = (P("req", "tp"), P("req", "tp"), P("req", "tp"), P("req", "tp"), P("req", "tp"), P())
    out_specs = P(("req", "tp"), None)
    return jax.shard_map(body, mesh=mesh, in_specs=in_specs, out_specs=out_specs, check_vma=False)
```

profile of v0, /device:TPU:1, one launch (start us, length us, event | category | flops | bytes accessed | tf_op | source)
XLA Modules:
  0.0 240.2 jit_solution(3304796626245086845)
XLA Ops:
  0.0 8.9 %collective-permute-start = (bf16[128,1024]{1,0:T(8,128)(2,1)}, bf16[128,1024]{1,0:T(8,128)(2,1)S(1)}, u32[]{:S(2)}, u32[]{:S(2)}) collective-permute-start(bf16[128,1024]{1,0:T(8,128)(2,1)} %param.10), channel_id=1, source_target_pairs={{0,8},{8,0},{16,24},{24,16},{32,40},{40,32},{48,56},{56,48},{64,72... | collective-permute-start | bytes 786440 | tf_op jit(solution)/shard_map/ppermute | solution.py:18
  8.9 1.3 collective-permute-done
  10.2 1.2 maximum_select_fusion.2
  11.4 1.9 collective-permute-start.1
  13.4 13.1 %collective-permute-done.1 = bf16[256,1024]{1,0:T(8,128)(2,1)S(1)} collective-permute-done((bf16[256,1024]{1,0:T(8,128)(2,1)S(1)}, bf16[256,1024]{1,0:T(8,128)(2,1)S(1)}, u32[]{:S(2)}, u32[]{:S(2)}) %collective-permute-start.1) | collective-permute-done | bytes 524320 | tf_op jit(solution)/shard_map/ppermute | solution.py:18
  26.9 1.9 collective-permute-start.2
  30.3 22.1 %collective-permute-done.2 = bf16[512,1024]{1,0:T(8,128)(2,1)S(1)} collective-permute-done((bf16[512,1024]{1,0:T(8,128)(2,1)S(1)}, bf16[512,1024]{1,0:T(8,128)(2,1)S(1)}, u32[]{:S(2)}, u32[]{:S(2)}) %collective-permute-start.2) | collective-permute-done | bytes 1048608 | tf_op jit(solution)/shard_map/ppermute | solution.py:18
  52.3 2.4 maximum_select_fusion
  54.7 80.4 %while.47 = (s32[]{:T(128)}, f32[8,1,1024]{2,1,0:T(1,128)S(1)}, f32[8,1,1024]{2,1,0:T(1,128)S(1)}, f32[8,1,1024,128]{3,2,1,0:T(8,128)}, bf16[8,128,1024]{2,1,0:T...) while((s32[]{:T(128)}, f32[8,1,1024]{2,1,0:T(1,128)S(1)}, ...), condition=%wide.region_7.8_spmd, body=%wide.region_0.7_spmd.sunk | while | flops 344470144 | bytes 13067348 | solution.py:167
  57.7 5.6 %while.48 = (s32[]{:T(128)}, f32[1,1024]{1,0:T(1,128)S(1)}, f32[1,1024]{1,0:T(1,128)S(1)}, f32[1,1024,128]{2,1,0:T(8,128)S(1)}, s32[]{:T(128)}, /*index=5*/s32[]...) while((s32[]{:T(128)}, f32[1,1024]{1,0:T(1,128)S(1)}, ...), condition=%wide.region_4.4_spmd, body=%wide.region_1.3_spmd.sunk | while | flops 275516928 | bytes 7932103 | solution.py:81
  67.8 5.6 %while.48 = (s32[]{:T(128)}, f32[1,1024]{1,0:T(1,128)S(1)}, f32[1,1024]{1,0:T(1,128)S(1)}, f32[1,1024,128]{2,1,0:T(8,128)S(1)}, s32[]{:T(128)}, /*index=5*/s32[]...) while((s32[]{:T(128)}, f32[1,1024]{1,0:T(1,128)S(1)}, ...), condition=%wide.region_4.4_spmd, body=%wide.region_1.3_spmd.sunk | while | flops 275516928 | bytes 7932103 | solution.py:81
  77.8 5.6 %while.48 = (s32[]{:T(128)}, f32[1,1024]{1,0:T(1,128)S(1)}, f32[1,1024]{1,0:T(1,128)S(1)}, f32[1,1024,128]{2,1,0:T(8,128)S(1)}, s32[]{:T(128)}, /*index=5*/s32[]...) while((s32[]{:T(128)}, f32[1,1024]{1,0:T(1,128)S(1)}, ...), condition=%wide.region_4.4_spmd, body=%wide.region_1.3_spmd.sunk | while | flops 275516928 | bytes 7932103 | solution.py:81
  87.9 5.6 %while.48 = (s32[]{:T(128)}, f32[1,1024]{1,0:T(1,128)S(1)}, f32[1,1024]{1,0:T(1,128)S(1)}, f32[1,1024,128]{2,1,0:T(8,128)S(1)}, s32[]{:T(128)}, /*index=5*/s32[]...) while((s32[]{:T(128)}, f32[1,1024]{1,0:T(1,128)S(1)}, ...), condition=%wide.region_4.4_spmd, body=%wide.region_1.3_spmd.sunk | while | flops 275516928 | bytes 7932103 | solution.py:81
  97.9 5.6 %while.48 = (s32[]{:T(128)}, f32[1,1024]{1,0:T(1,128)S(1)}, f32[1,1024]{1,0:T(1,128)S(1)}, f32[1,1024,128]{2,1,0:T(8,128)S(1)}, s32[]{:T(128)}, /*index=5*/s32[]...) while((s32[]{:T(128)}, f32[1,1024]{1,0:T(1,128)S(1)}, ...), condition=%wide.region_4.4_spmd, body=%wide.region_1.3_spmd.sunk | while | flops 275516928 | bytes 7932103 | solution.py:81
  108.0 5.6 %while.48 = (s32[]{:T(128)}, f32[1,1024]{1,0:T(1,128)S(1)}, f32[1,1024]{1,0:T(1,128)S(1)}, f32[1,1024,128]{2,1,0:T(8,128)S(1)}, s32[]{:T(128)}, /*index=5*/s32[]...) while((s32[]{:T(128)}, f32[1,1024]{1,0:T(1,128)S(1)}, ...), condition=%wide.region_4.4_spmd, body=%wide.region_1.3_spmd.sunk | while | flops 275516928 | bytes 7932103 | solution.py:81
  118.0 5.6 %while.48 = (s32[]{:T(128)}, f32[1,1024]{1,0:T(1,128)S(1)}, f32[1,1024]{1,0:T(1,128)S(1)}, f32[1,1024,128]{2,1,0:T(8,128)S(1)}, s32[]{:T(128)}, /*index=5*/s32[]...) while((s32[]{:T(128)}, f32[1,1024]{1,0:T(1,128)S(1)}, ...), condition=%wide.region_4.4_spmd, body=%wide.region_1.3_spmd.sunk | while | flops 275516928 | bytes 7932103 | solution.py:81
  128.1 5.6 %while.48 = (s32[]{:T(128)}, f32[1,1024]{1,0:T(1,128)S(1)}, f32[1,1024]{1,0:T(1,128)S(1)}, f32[1,1024,128]{2,1,0:T(8,128)S(1)}, s32[]{:T(128)}, /*index=5*/s32[]...) while((s32[]{:T(128)}, f32[1,1024]{1,0:T(1,128)S(1)}, ...), condition=%wide.region_4.4_spmd, body=%wide.region_1.3_spmd.sunk | while | flops 275516928 | bytes 7932103 | solution.py:81
  135.1 2.4 %slice_select_fusion = f32[4,1,1024,128]{3,2,1,0:T(8,128)S(1)} fusion(f32[8,1,1024,128]{3,2,1,0:T(8,128)} %get-tuple-element.830, pred[]{:T(512)S(6)} %eq.26), kind=kLoop, calls=%fused_computation.50 | loop fusion | flops 524288 | bytes 6291457 | tf_op jit(solution)/shard_map/jit(_where)/select_n | solution.py:175
  137.5 1.9 collective-permute-start.4
  139.5 3.4 %collective-permute-start.3 = (f32[4,1,1024]{2,1,0:T(1,128)S(1)}, f32[4,1,1024]{2,1,0:T(1,128)S(1)}, u32[]{:S(2)}, u32[]{:S(2)}) collective-permute-start(f32[4,1,1024]{2,1,0:T(1,128)S(1)} %broadcast_select_fusion.2), channel_id=1, source_target_pairs={{0,32},{8,40},{16,48},{24,56},{32,0},{40,8},{48,16},{56,24},{64,96... | collective-permute-start | bytes 49160 | tf_op jit(solution)/shard_map/ppermute | solution.py:18
  142.9 1.9 collective-permute-start.9
  144.8 40.2 %collective-permute-done.3 = f32[4,1,1024]{2,1,0:T(1,128)S(1)} collective-permute-done((f32[4,1,1024]{2,1,0:T(1,128)S(1)}, f32[4,1,1024]{2,1,0:T(1,128)S(1)}, u32[]{:S(2)}, u32[]{:S(2)}) %collective-permute-start.3) | collective-permute-done | bytes 16416 | tf_op jit(solution)/shard_map/ppermute | solution.py:18
  185.4 4.0 %multiply_add_fusion.1 = f32[4,1,1024,128]{3,2,1,0:T(8,128)S(1)} fusion(f32[4,1,1024,128]{3,2,1,0:T(8,128)} %collective-permute-done.4, f32[8,1,1024,128]{3,2,1,0:T(8,128)} %get-tuple-element.830, f32[4,1024]{1,0:T(4,128)S(1)} %get-tuple-element.471, f32[4,1024]{1,0:T(4,128)S(1)} %get-tuple-element.472, pred[]{:T(512)S(6)} %eq.26), kind=kLoop, calls=%fused_computation.49 | loop fusion | flops 2097152 | bytes 8421377 | tf_op jit(solution)/shard_map/add | solution.py:107
  190.6 2.8 %collective-permute-start.6 = (f32[2,1,1024,128]{3,2,1,0:T(8,128)}, f32[2,1,1024,128]{3,2,1,0:T(8,128)S(1)}, u32[]{:S(2)}, u32[]{:S(2)}) collective-permute-start(f32[2,1,1024,128]{3,2,1,0:T(8,128)} %slice_select_fusion.1), channel_id=1, source_target_pairs={{0,16},{8,24},{16,0},{24,8},{32,48},{40,56},{48,32},{56,40},{64,80... | collective-permute-start | bytes 3145736 | tf_op jit(solution)/shard_map/ppermute | solution.py:18
  193.4 2.5 %collective-permute-start.5 = (f32[2,1,1024]{2,1,0:T(1,128)S(1)}, f32[2,1,1024]{2,1,0:T(1,128)S(1)}, u32[]{:S(2)}, u32[]{:S(2)}) collective-permute-start(f32[2,1,1024]{2,1,0:T(1,128)S(1)} %broadcast_select_fusion.6), channel_id=1, source_target_pairs={{0,16},{8,24},{16,0},{24,8},{32,48},{40,56},{48,32},{56,40},{64,80... | collective-permute-start | bytes 24584 | tf_op jit(solution)/shard_map/ppermute | solution.py:18
  195.9 2.8 %collective-permute-start.10 = (f32[2,1,1024]{2,1,0:T(1,128)S(1)}, f32[2,1,1024]{2,1,0:T(1,128)S(1)}, u32[]{:S(2)}, u32[]{:S(2)}) collective-permute-start(f32[2,1,1024]{2,1,0:T(1,128)S(1)} %broadcast_select_fusion.4), channel_id=1, source_target_pairs={{0,16},{8,24},{16,0},{24,8},{32,48},{40,56},{48,32},{56,40},{64,80... | collective-permute-start | bytes 24584 | tf_op jit(solution)/shard_map/ppermute | solution.py:18
  198.7 16.0 %collective-permute-done.5 = f32[2,1,1024]{2,1,0:T(1,128)S(1)} collective-permute-done((f32[2,1,1024]{2,1,0:T(1,128)S(1)}, f32[2,1,1024]{2,1,0:T(1,128)S(1)}, u32[]{:S(2)}, u32[]{:S(2)}) %collective-permute-start.5) | collective-permute-done | bytes 8224 | tf_op jit(solution)/shard_map/ppermute | solution.py:18
  215.9 1.8 multiply_add_fusion.2
  217.8 5.6 %collective-permute-start.8 = (f32[1,1,1024,128]{3,2,1,0:T(8,128)S(1)}, f32[1,1,1024,128]{3,2,1,0:T(8,128)S(1)}, u32[]{:S(2)}, u32[]{:S(2)}) collective-permute-start(f32[1,1,1024,128]{3,2,1,0:T(8,128)S(1)} %slice_select_fusion.2), channel_id=1, source_target_pairs={{0,8},{8,0},{16,24},{24,16},{32,40},{40,32},{48,56},{56,48},{64,72... | collective-permute-start | bytes 1572872 | tf_op jit(solution)/shard_map/ppermute | solution.py:18
  223.4 1.9 collective-permute-start.7
  225.3 2.4 %collective-permute-start.11 = (f32[1,1,1024]{2,1,0:T(1,128)S(1)}, f32[1,1,1024]{2,1,0:T(1,128)S(1)}, u32[]{:S(2)}, u32[]{:S(2)}) collective-permute-start(f32[1,1,1024]{2,1,0:T(1,128)S(1)} %broadcast_select_fusion.8), channel_id=1, source_target_pairs={{0,8},{8,0},{16,24},{24,16},{32,40},{40,32},{48,56},{56,48},{64,72... | collective-permute-start | bytes 12296 | tf_op jit(solution)/shard_map/ppermute | solution.py:18
  229.5 10.0 %all_to_all.16 = bf16[8,16,1024]{2,1,0:T(8,128)(2,1)S(1)} all-to-all(bf16[8,16,1024]{2,1,0:T(8,128)(2,1)S(1)} %convert_element_type.25), channel_id=1, replica_groups=mesh['req'=64,'tp'=8] {'tp'}, dimensions={0} | all-to-all | bytes 524288 | tf_op jit(solution)/shard_map/all_to_all | solution.py:180
  (267 shorter events, 79.5 us)
Async XLA Ops:
  0.0 28.9 %copy-start.5 = (s32[8]{0:T(128)S(1)}, s32[8]{0:T(128)}, u32[]{:S(2)}) copy-start(s32[8]{0:T(128)} %param.15) | copy-start | bytes 100
  0.0 10.2 %collective-permute-start = (bf16[128,1024]{1,0:T(8,128)(2,1)}, bf16[128,1024]{1,0:T(8,128)(2,1)S(1)}, u32[]{:S(2)}, u32[]{:S(2)}) collective-permute-start(bf16[128,1024]{1,0:T(8,128)(2,1)} %param.10), channel_id=1, source_target_pairs={{0,8},{8,0},{16,24},{24,16},{32,40},{40,32},{48,56},{56,48},{64,72... | collective-permute-start | bytes 786440 | tf_op jit(solution)/shard_map/ppermute | solution.py:18
  11.4 15.0 %collective-permute-start.1 = (bf16[256,1024]{1,0:T(8,128)(2,1)S(1)}, bf16[256,1024]{1,0:T(8,128)(2,1)S(1)}, u32[]{:S(2)}, u32[]{:S(2)}) collective-permute-start(bf16[256,1024]{1,0:T(8,128)(2,1)S(1)} %maximum_select_fusion.2), channel_id=1, source_target_pairs={{0,16},{8,24},{16,0},{24,8},{32,48},{40,56},{48,32},{56,40},{64,80... | collective-permute-start | bytes 1572872 | tf_op jit(solution)/shard_map/ppermute | solution.py:18
  26.9 25.4 %collective-permute-start.2 = (bf16[512,1024]{1,0:T(8,128)(2,1)S(1)}, bf16[512,1024]{1,0:T(8,128)(2,1)S(1)}, u32[]{:S(2)}, u32[]{:S(2)}) collective-permute-start(bf16[512,1024]{1,0:T(8,128)(2,1)S(1)} %maximum_select_fusion.1), channel_id=1, source_target_pairs={{0,32},{8,40},{16,48},{24,56},{32,0},{40,8},{48,16},{56,24},{64,96... | collective-permute-start | bytes 3145736 | tf_op jit(solution)/shard_map/ppermute | solution.py:18
  30.2 24.5 %copy-start = (bf16[1024,128]{1,0:T(8,128)(2,1)S(1)}, bf16[1024,128]{1,0:T(8,128)(2,1)}, u32[]{:S(2)}) copy-start(bf16[1024,128]{1,0:T(8,128)(2,1)} %param.13) | copy-start | bytes 786436
  30.2 24.5 %copy-start.2 = (bf16[128,128]{1,0:T(8,128)(2,1)S(1)}, bf16[128,128]{1,0:T(8,128)(2,1)}, u32[]{:S(2)}) copy-start(bf16[128,128]{1,0:T(8,128)(2,1)} %param.12) | copy-start | bytes 98308
  30.2 24.5 %copy-start.3 = (bf16[1024,128]{1,0:T(8,128)(2,1)S(1)}, bf16[1024,128]{1,0:T(8,128)(2,1)}, u32[]{:S(2)}) copy-start(bf16[1024,128]{1,0:T(8,128)(2,1)} %param.14) | copy-start | bytes 786436
  30.2 24.5 %copy-start.4 = (bf16[128,128]{1,0:T(8,128)(2,1)S(1)}, bf16[128,128]{1,0:T(8,128)(2,1)}, u32[]{:S(2)}) copy-start(bf16[128,128]{1,0:T(8,128)(2,1)} %param.11) | copy-start | bytes 98308
  137.5 47.9 %collective-permute-start.4 = (f32[4,1,1024,128]{3,2,1,0:T(8,128)S(1)}, f32[4,1,1024,128]{3,2,1,0:T(8,128)}, u32[]{:S(2)}, u32[]{:S(2)}) collective-permute-start(f32[4,1,1024,128]{3,2,1,0:T(8,128)S(1)} %slice_select_fusion), channel_id=1, source_target_pairs={{0,32},{8,40},{16,48},{24,56},{32,0},{40,8},{48,16},{56,24},{64,96... | collective-permute-start | bytes 6291464 | tf_op jit(solution)/shard_map/ppermute | solution.py:18
  139.5 45.5 %collective-permute-start.3 = (f32[4,1,1024]{2,1,0:T(1,128)S(1)}, f32[4,1,1024]{2,1,0:T(1,128)S(1)}, u32[]{:S(2)}, u32[]{:S(2)}) collective-permute-start(f32[4,1,1024]{2,1,0:T(1,128)S(1)} %broadcast_select_fusion.2), channel_id=1, source_target_pairs={{0,32},{8,40},{16,48},{24,56},{32,0},{40,8},{48,16},{56,24},{64,96... | collective-permute-start | bytes 49160 | tf_op jit(solution)/shard_map/ppermute | solution.py:18
  142.9 42.4 %collective-permute-start.9 = (f32[4,1,1024]{2,1,0:T(1,128)S(1)}, f32[4,1,1024]{2,1,0:T(1,128)S(1)}, u32[]{:S(2)}, u32[]{:S(2)}) collective-permute-start(f32[4,1,1024]{2,1,0:T(1,128)S(1)} %broadcast_select_fusion), channel_id=1, source_target_pairs={{0,32},{8,40},{16,48},{24,56},{32,0},{40,8},{48,16},{56,24},{64,96... | collective-permute-start | bytes 49160 | tf_op jit(solution)/shard_map/ppermute | solution.py:18
  190.6 24.4 %collective-permute-start.6 = (f32[2,1,1024,128]{3,2,1,0:T(8,128)}, f32[2,1,1024,128]{3,2,1,0:T(8,128)S(1)}, u32[]{:S(2)}, u32[]{:S(2)}) collective-permute-start(f32[2,1,1024,128]{3,2,1,0:T(8,128)} %slice_select_fusion.1), channel_id=1, source_target_pairs={{0,16},{8,24},{16,0},{24,8},{32,48},{40,56},{48,32},{56,40},{64,80... | collective-permute-start | bytes 3145736 | tf_op jit(solution)/shard_map/ppermute | solution.py:18
  193.4 21.4 %collective-permute-start.5 = (f32[2,1,1024]{2,1,0:T(1,128)S(1)}, f32[2,1,1024]{2,1,0:T(1,128)S(1)}, u32[]{:S(2)}, u32[]{:S(2)}) collective-permute-start(f32[2,1,1024]{2,1,0:T(1,128)S(1)} %broadcast_select_fusion.6), channel_id=1, source_target_pairs={{0,16},{8,24},{16,0},{24,8},{32,48},{40,56},{48,32},{56,40},{64,80... | collective-permute-start | bytes 24584 | tf_op jit(solution)/shard_map/ppermute | solution.py:18
  195.9 19.0 %collective-permute-start.10 = (f32[2,1,1024]{2,1,0:T(1,128)S(1)}, f32[2,1,1024]{2,1,0:T(1,128)S(1)}, u32[]{:S(2)}, u32[]{:S(2)}) collective-permute-start(f32[2,1,1024]{2,1,0:T(1,128)S(1)} %broadcast_select_fusion.4), channel_id=1, source_target_pairs={{0,16},{8,24},{16,0},{24,8},{32,48},{40,56},{48,32},{56,40},{64,80... | collective-permute-start | bytes 24584 | tf_op jit(solution)/shard_map/ppermute | solution.py:18
  215.0 1.0 copy-start.1
  217.8 10.9 %collective-permute-start.8 = (f32[1,1,1024,128]{3,2,1,0:T(8,128)S(1)}, f32[1,1,1024,128]{3,2,1,0:T(8,128)S(1)}, u32[]{:S(2)}, u32[]{:S(2)}) collective-permute-start(f32[1,1,1024,128]{3,2,1,0:T(8,128)S(1)} %slice_select_fusion.2), channel_id=1, source_target_pairs={{0,8},{8,0},{16,24},{24,16},{32,40},{40,32},{48,56},{56,48},{64,72... | collective-permute-start | bytes 1572872 | tf_op jit(solution)/shard_map/ppermute | solution.py:18
  223.4 4.4 %collective-permute-start.7 = (f32[1,1,1024]{2,1,0:T(1,128)S(1)}, f32[1,1,1024]{2,1,0:T(1,128)S(1)}, u32[]{:S(2)}, u32[]{:S(2)}) collective-permute-start(f32[1,1,1024]{2,1,0:T(1,128)S(1)} %broadcast_select_fusion.10), channel_id=1, source_target_pairs={{0,8},{8,0},{16,24},{24,16},{32,40},{40,32},{48,56},{56,48},{64,72... | collective-permute-start | bytes 12296 | tf_op jit(solution)/shard_map/ppermute | solution.py:18
  225.3 3.2 %collective-permute-start.11 = (f32[1,1,1024]{2,1,0:T(1,128)S(1)}, f32[1,1,1024]{2,1,0:T(1,128)S(1)}, u32[]{:S(2)}, u32[]{:S(2)}) collective-permute-start(f32[1,1,1024]{2,1,0:T(1,128)S(1)} %broadcast_select_fusion.8), channel_id=1, source_target_pairs={{0,8},{8,0},{16,24},{24,16},{32,40},{40,32},{48,56},{56,48},{64,72... | collective-permute-start | bytes 12296 | tf_op jit(solution)/shard_map/ppermute | solution.py:18
where the time goes:
time: 241 us; the launch traced here: 240 us
  waiting for transfers between devices  94 us (39%)
  starting transfers between devices  37.9 us (16%)
  other arithmetic  35.6 us (15%)
  matrix products  35.6 us (15%)
  local copies, waits for them, and re-layouts  18.8 us (8%)
  blocking collectives  9.99 us (4%)
  loops' own time  7.33 us (3%)
    ppermute x12, waiting for transfers between devices, partner(): return lax.ppermute(value, axis, pairs)  94 us
    ppermute x12, starting transfers between devices, partner(): return lax.ppermute(value, axis, pairs)  37.9 us
    dot_general x24, matrix products, absorb(): jnp.einsum('jqk,jkd->jqd', weights.astype(jnp.bfloat16), value_block, pre...  26.3 us
    dynamic_slice x24, local copies, waits for them, and re-layouts, body(): lax.map(one_block, (stacked, jnp.arange(GROUP_DEVS, dtype=jnp.int32)))  14.4 us
    lt x16, other arithmetic, allowed_at(): return (first_row + offsets < group_length)[None, :]  10.3 us
    reduce_sum x24, other arithmetic, absorb(): run_sum = run_sum * factor + jnp.sum(weights, axis=-1)  10 us
    all_to_all x1, blocking collectives, body(): lax.all_to_all(attended, 'tp', split_axis=0, concat_axis=1, tiled=True)  9.99 us
    dot_general x24, matrix products, absorb(): jnp.einsum('jqd,jkd->jqk', query_rows, key_block, preferred_element_type=...  9.28 us
  transfers between devices with their start and end apart: 12, of which 8 were waited for; matrix products, arithmetic and copies ran while one was open for 0% of the time, Pallas kernels for 0%

commit v1 on v0

v1 whole, which is shorter than its diff:
```python
import functools
import math

import jax
import jax.numpy as jnp
from jax import lax
from jax.experimental import pallas as pl
from jax.experimental.pallas import tpu as pltpu
from jax.sharding import PartitionSpec as P

HEAD_SIZE = 128
GROUP_DEVS = 8
NEG_FILL = -1e30
SCALE = 1.0 / math.sqrt(HEAD_SIZE)


def exchange(value, axis, mask):
    pairs = [(source, source ^ mask) for source in range(lax.axis_size(axis))]
    return lax.ppermute(value, axis, pairs)


def gather_group(own):
    half = [member.shape[0] // 2 for member in own]
    from_x = exchange(own, "req", 2)
    from_z = exchange(own, "req", 4)
    diag_lo = exchange(tuple(m[:n] for m, n in zip(from_z, half)), "req", 2)
    diag_hi = exchange(tuple(m[n:] for m, n in zip(from_x, half)), "req", 4)
    diag = tuple(jnp.concatenate([lo, hi], 0) for lo, hi in zip(diag_lo, diag_hi))
    chip = (own, from_x, from_z, diag)
    other = exchange(chip, "req", 1)
    return [own, other[0], from_x, other[1], from_z, other[2], diag, other[3]]


def attn_kernel(info_ref, q_ref, kc_ref, vc_ref, ks_ref, vs_ref, o_ref, m_sc, l_sc, acc_sc):
    step = pl.program_id(0)
    last = pl.num_programs(0) - 1
    n_slots = last
    heads = q_ref.shape[1] // HEAD_SIZE
    tokens = q_ref.shape[0]
    block = kc_ref.shape[0]
    span_block = ks_ref.shape[0]
    length = info_ref[0]
    first_token = info_ref[1]

    @pl.when(step == 0)
    def _init():
        m_sc[...] = jnp.full(m_sc.shape, NEG_FILL, jnp.float32)
        l_sc[...] = jnp.zeros(l_sc.shape, jnp.float32)
        acc_sc[...] = jnp.zeros(acc_sc.shape, jnp.float32)

    def process(k_ref, v_ref, allowed_fn):
        keys = k_ref[...]
        values = v_ref[...]
        allowed = None if allowed_fn is None else allowed_fn()

        def one_head(h, carry):
            col = pl.multiple_of(h * HEAD_SIZE, HEAD_SIZE)
            qh = q_ref[:, pl.ds(col, HEAD_SIZE)]
            s = lax.dot_general(
                qh, keys, (((1,), (1,)), ((), ())), preferred_element_type=jnp.float32
            )
            if allowed is not None:
                s = jnp.where(allowed, s, NEG_FILL)
            m_prev = m_sc[h]
            m_new = jnp.maximum(m_prev, jnp.max(s, axis=1, keepdims=True))
            alpha = jnp.exp((m_prev - m_new) * SCALE)
            p = jnp.exp((s - m_new) * SCALE)
            l_sc[h] = alpha * l_sc[h] + jnp.sum(p, axis=1, keepdims=True)
            pv = jnp.dot(p.astype(jnp.bfloat16), values, preferred_element_type=jnp.float32)
            acc_sc[h] = alpha * acc_sc[h] + pv
            m_sc[h] = m_new
            return carry

        lax.fori_loop(0, heads, one_head, 0)

    @pl.when(step < n_slots)
    def _cache():
        start = info_ref[2 + jnp.minimum(step, n_slots - 1)]
        full = start + block <= length
        partial = jnp.logical_and(start < length, jnp.logical_not(full))

        @pl.when(full)
        def _():
            process(kc_ref, vc_ref, None)

        @pl.when(partial)
        def _():
            def allowed_fn():
                rows = start + lax.broadcasted_iota(jnp.int32, (tokens, block), 1)
                return rows < length

            process(kc_ref, vc_ref, allowed_fn)

    @pl.when(step == n_slots)
    def _span():
        def allowed_fn():
            key_pos = lax.broadcasted_iota(jnp.int32, (tokens, span_block), 1)
            query_pos = first_token + lax.broadcasted_iota(jnp.int32, (tokens, span_block), 0)
            return key_pos <= query_pos

        process(ks_ref, vs_ref, allowed_fn)

    @pl.when(step == last)
    def _finish():
        for h in range(heads):
            o_ref[:, h * HEAD_SIZE:(h + 1) * HEAD_SIZE] = (acc_sc[h] / l_sc[h]).astype(o_ref.dtype)


def attention(info, queries, cache_k, cache_v, span_k, span_v, block):
    tokens, width = queries.shape
    heads = width // HEAD_SIZE
    n_slots = cache_k.shape[0] // block
    span_rows = span_k.shape[0]
    cache_spec = pl.BlockSpec((block, HEAD_SIZE), lambda k, info: (jnp.minimum(k, n_slots - 1), 0))
    span_spec = pl.BlockSpec((span_rows, HEAD_SIZE), lambda k, info: (0, 0))
    whole = pl.BlockSpec((tokens, width), lambda k, info: (0, 0))
    return pl.pallas_call(
        attn_kernel,
        out_shape=jax.ShapeDtypeStruct((tokens, width), jnp.bfloat16),
        grid_spec=pltpu.PrefetchScalarGridSpec(
            num_scalar_prefetch=1,
            grid=(n_slots + 1,),
            in_specs=[whole, cache_spec, cache_spec, span_spec, span_spec],
            out_specs=whole,
            scratch_shapes=[
                pltpu.VMEM((heads, tokens, 1), jnp.float32),
                pltpu.VMEM((heads, tokens, 1), jnp.float32),
                pltpu.VMEM((heads, tokens, HEAD_SIZE), jnp.float32),
            ],
        ),
        compiler_params=pltpu.CompilerParams(
            dimension_semantics=("arbitrary",), vmem_limit_bytes=48 * 1024 * 1024
        ),
    )(info, queries, cache_k, cache_v, span_k, span_v)


def body(queries, span_rotated_keys, span_token_values, cache_keys, prompt_cache_values, lengths):
    tok_rows = queries.shape[0]
    cache_rows = cache_keys.shape[0]
    group_devs = lax.axis_size("req") // lengths.shape[0]
    assert group_devs == GROUP_DEVS
    device = lax.axis_index("req")
    position = device % GROUP_DEVS
    group_length = lax.dynamic_index_in_dim(lengths, device // GROUP_DEVS, 0, keepdims=False)

    slots = gather_group((cache_keys, prompt_cache_values, span_rotated_keys, span_token_values))
    cache_k = jnp.concatenate([slot[0] for slot in slots], 0)
    cache_v = jnp.concatenate([slot[1] for slot in slots], 0)
    order = jnp.arange(GROUP_DEVS, dtype=jnp.int32) ^ position
    span_k = jnp.stack([slot[2] for slot in slots])[order].reshape(-1, HEAD_SIZE)
    span_v = jnp.stack([slot[3] for slot in slots])[order].reshape(-1, HEAD_SIZE)
    starts = (jnp.arange(GROUP_DEVS, dtype=jnp.int32) ^ position) * cache_rows
    info = jnp.concatenate(
        [jnp.stack([group_length, position * tok_rows]).astype(jnp.int32), starts.astype(jnp.int32)]
    )
    attended = attention(info, queries, cache_k, cache_v, span_k, span_v, cache_rows)
    return lax.all_to_all(attended, "tp", split_axis=0, concat_axis=1, tiled=True)


def solution(mesh):
    in_specs = (P("req", "tp"), P("req", "tp"), P("req", "tp"), P("req", "tp"), P("req", "tp"), P())
    out_specs = P(("req", "tp"), None)
    return jax.shard_map(body, mesh=mesh, in_specs=in_specs, out_specs=out_specs, check_vma=False)
```

time: 241 us -> 172 us (0.71)
  waiting for transfers between devices: 94 us -> 5.05 us
  starting transfers between devices: 37.9 us -> 87 us
  Pallas kernels: 0 us -> 47.9 us
  matrix products: 35.6 us -> 0 us
  other arithmetic: 35.6 us -> 0.76 us
  loops' own time: 7.33 us -> 0 us
    ppermute x12 -> x32, waiting for transfers between devices: 94 us -> 5.05 us  [exchange(): return lax.ppermute(value, axis, pairs)]
    ppermute x12 -> x32, starting transfers between devices: 37.9 us -> 87 us  [exchange(): return lax.ppermute(value, axis, pairs)]
    pallas_call x0 -> x1, Pallas kernels: none -> 47.9 us  [attention(): pl.pallas_call(attn_kernel, out_shape=jax.ShapeDtypeStruct((tokens, width...]
    dot_general x48 -> x0, matrix products: 35.6 us -> none  [the longest x24 26.3 us: absorb(): jnp.einsum('jqk,jkd->jqd', weights.astype(jnp.bfloat16), value_block, pre...]
    dynamic_slice x24 -> x0, local copies, waits for them, and re-layouts: 14.4 us -> none  [body(): lax.map(one_block, (stacked, jnp.arange(GROUP_DEVS, dtype=jnp.int32)))]
    unnamed x14 -> x36, local copies, waits for them, and re-layouts: 1.02 us -> 13.2 us
    lt x16 -> x0, other arithmetic: 10.3 us -> none  [allowed_at(): return (first_row + offsets < group_length)[None, :]]
    reduce_sum x24 -> x0, other arithmetic: 10 us -> none  [absorb(): run_sum = run_sum * factor + jnp.sum(weights, axis=-1)]
  transfers between devices with their start and end apart: 12 -> 32, of which waited for: 8 -> 4; matrix products, arithmetic and copies ran while one was open for 0% -> 11% of each run, Pallas kernels for 0% -> 0%
where the time goes in v1:
time: 172 us; the launch traced here: 170 us
  starting transfers between devices  87 us (51%)
  Pallas kernels  47.9 us (28%)
  local copies, waits for them, and re-layouts  19 us (11%)
  blocking collectives  9.99 us (6%)
  waiting for transfers between devices  5.05 us (3%)
    ppermute x32, starting transfers between devices, exchange(): return lax.ppermute(value, axis, pairs)  87 us
    pallas_call x1, Pallas kernels, attention(): pl.pallas_call(attn_kernel, out_shape=jax.ShapeDtypeStruct((tokens, width...  47.9 us
    unnamed x36, local copies, waits for them, and re-layouts  13.2 us
    all_to_all x1, blocking collectives, body(): lax.all_to_all(attended, 'tp', split_axis=0, concat_axis=1, tiled=True)  9.99 us
    ppermute x32, waiting for transfers between devices, exchange(): return lax.ppermute(value, axis, pairs)  5.05 us
  transfers between devices with their start and end apart: 32, of which 4 were waited for; matrix products, arithmetic and copies ran while one was open for 11% of the time, Pallas kernels for 0%

profile of v1, /device:TPU:1, one launch (start us, length us, event | category | flops | bytes accessed | tf_op | source)
XLA Modules:
  0.0 170.5 jit_solution(6462386704354632480)
XLA Ops:
  0.0 8.7 %collective-permute-start = (bf16[1024,128]{1,0:T(8,128)(2,1)}, bf16[1024,128]{1,0:T(8,128)(2,1)}, u32[]{:S(2)}, u32[]{:S(2)}) collective-permute-start(bf16[1024,128]{1,0:T(8,128)(2,1)} %param.9), channel_id=1, source_target_pairs={{0,8},{8,0},{16,24},{24,16},{32,40},{40,32},{48,56},{56,48},{64,72... | collective-permute-start | bytes 786440 | tf_op jit(solution)/shard_map/ppermute | solution.py:19
  8.7 1.9 %collective-permute-start.1 = (bf16[1024,128]{1,0:T(8,128)(2,1)}, bf16[1024,128]{1,0:T(8,128)(2,1)S(1)}, u32[]{:S(2)}, u32[]{:S(2)}) collective-permute-start(bf16[1024,128]{1,0:T(8,128)(2,1)} %param.9), channel_id=1, source_target_pairs={{0,16},{8,24},{16,0},{24,8},{32,48},{40,56},{48,32},{56,40},{64,80... | collective-permute-start | bytes 786440 | tf_op jit(solution)/shard_map/ppermute | solution.py:19
  10.7 1.9 %collective-permute-start.3 = (bf16[1024,128]{1,0:T(8,128)(2,1)}, bf16[1024,128]{1,0:T(8,128)(2,1)S(1)}, u32[]{:S(2)}, u32[]{:S(2)}) collective-permute-start(bf16[1024,128]{1,0:T(8,128)(2,1)} %param.9), channel_id=1, source_target_pairs={{0,32},{8,40},{16,48},{24,56},{32,0},{40,8},{48,16},{56,24},{64,96... | collective-permute-start | bytes 786440 | tf_op jit(solution)/shard_map/ppermute | solution.py:19
  12.6 1.9 %collective-permute-start.16 = (bf16[128,128]{1,0:T(8,128)(2,1)}, bf16[128,128]{1,0:T(8,128)(2,1)S(1)}, u32[]{:S(2)}, u32[]{:S(2)}) collective-permute-start(bf16[128,128]{1,0:T(8,128)(2,1)} %param.7), channel_id=1, source_target_pairs={{0,8},{8,0},{16,24},{24,16},{32,40},{40,32},{48,56},{56,48},{64,72... | collective-permute-start | bytes 98312 | tf_op jit(solution)/shard_map/ppermute | solution.py:19
  14.5 3.6 %collective-permute-start.17 = (bf16[128,128]{1,0:T(8,128)(2,1)}, bf16[128,128]{1,0:T(8,128)(2,1)S(1)}, u32[]{:S(2)}, u32[]{:S(2)}) collective-permute-start(bf16[128,128]{1,0:T(8,128)(2,1)} %param.7), channel_id=1, source_target_pairs={{0,16},{8,24},{16,0},{24,8},{32,48},{40,56},{48,32},{56,40},{64,80... | collective-permute-start | bytes 98312 | tf_op jit(solution)/shard_map/ppermute | solution.py:19
  25.0 3.6 %collective-permute-start.19 = (bf16[128,128]{1,0:T(8,128)(2,1)}, bf16[128,128]{1,0:T(8,128)(2,1)S(1)}, u32[]{:S(2)}, u32[]{:S(2)}) collective-permute-start(bf16[128,128]{1,0:T(8,128)(2,1)} %param.7), channel_id=1, source_target_pairs={{0,32},{8,40},{16,48},{24,56},{32,0},{40,8},{48,16},{56,24},{64,96... | collective-permute-start | bytes 98312 | tf_op jit(solution)/shard_map/ppermute | solution.py:19
  28.6 2.5 %collective-permute-start.24 = (bf16[128,128]{1,0:T(8,128)(2,1)}, bf16[128,128]{1,0:T(8,128)(2,1)S(1)}, u32[]{:S(2)}, u32[]{:S(2)}) collective-permute-start(bf16[128,128]{1,0:T(8,128)(2,1)} %param.8), channel_id=1, source_target_pairs={{0,8},{8,0},{16,24},{24,16},{32,40},{40,32},{48,56},{56,48},{64,72... | collective-permute-start | bytes 98312 | tf_op jit(solution)/shard_map/ppermute | solution.py:19
  37.0 3.0 %collective-permute-start.21 = (bf16[64,128]{1,0:T(8,128)(2,1)S(1)}, bf16[64,128]{1,0:T(8,128)(2,1)S(1)}, u32[]{:S(2)}, u32[]{:S(2)}) collective-permute-start(bf16[64,128]{1,0:T(8,128)(2,1)S(1)} %slice.40), channel_id=1, source_target_pairs={{0,16},{8,24},{16,0},{24,8},{32,48},{40,56},{48,32},{56,40},{64,80... | collective-permute-start | bytes 49160 | tf_op jit(solution)/shard_map/ppermute | solution.py:19
  40.6 3.4 %collective-permute-start.22 = (bf16[64,128]{1,0:T(8,128)(2,1)S(1)}, bf16[64,128]{1,0:T(8,128)(2,1)S(1)}, u32[]{:S(2)}, u32[]{:S(2)}) collective-permute-start(bf16[64,128]{1,0:T(8,128)(2,1)S(1)} %slice.41), channel_id=1, source_target_pairs={{0,32},{8,40},{16,48},{24,56},{32,0},{40,8},{48,16},{56,24},{64,96... | collective-permute-start | bytes 49160 | tf_op jit(solution)/shard_map/ppermute | solution.py:19
  44.0 1.9 %collective-permute-start.29 = (bf16[64,128]{1,0:T(8,128)(2,1)S(1)}, bf16[64,128]{1,0:T(8,128)(2,1)S(1)}, u32[]{:S(2)}, u32[]{:S(2)}) collective-permute-start(bf16[64,128]{1,0:T(8,128)(2,1)S(1)} %slice.42), channel_id=1, source_target_pairs={{0,16},{8,24},{16,0},{24,8},{32,48},{40,56},{48,32},{56,40},{64,80... | collective-permute-start | bytes 49160 | tf_op jit(solution)/shard_map/ppermute | solution.py:19
  46.0 2.5 %collective-permute-done.29 = bf16[64,128]{1,0:T(8,128)(2,1)S(1)} collective-permute-done((bf16[64,128]{1,0:T(8,128)(2,1)S(1)}, bf16[64,128]{1,0:T(8,128)(2,1)S(1)}, u32[]{:S(2)}, u32[]{:S(2)}) %collective-permute-start.29) | collective-permute-done | bytes 16416 | tf_op jit(solution)/shard_map/ppermute | solution.py:19
  50.5 4.7 %collective-permute-start.18 = (bf16[128,128]{1,0:T(8,128)(2,1)S(1)}, bf16[128,128]{1,0:T(8,128)(2,1)S(1)}, u32[]{:S(2)}, u32[]{:S(2)}) collective-permute-start(bf16[128,128]{1,0:T(8,128)(2,1)S(1)} %collective-permute-done.17), channel_id=1, source_target_pairs={{0,8},{8,0},{16,24},{24,16},{32,40},{40,32},{48,56},{56,48},{64,72... | collective-permute-start | bytes 98312 | tf_op jit(solution)/shard_map/ppermute | solution.py:19
  55.2 3.4 %collective-permute-start.20 = (bf16[128,128]{1,0:T(8,128)(2,1)S(1)}, bf16[128,128]{1,0:T(8,128)(2,1)S(1)}, u32[]{:S(2)}, u32[]{:S(2)}) collective-permute-start(bf16[128,128]{1,0:T(8,128)(2,1)S(1)} %collective-permute-done.19), channel_id=1, source_target_pairs={{0,8},{8,0},{16,24},{24,16},{32,40},{40,32},{48,56},{56,48},{64,72... | collective-permute-start | bytes 98312 | tf_op jit(solution)/shard_map/ppermute | solution.py:19
  58.7 1.9 %collective-permute-start.26 = (bf16[128,128]{1,0:T(8,128)(2,1)S(1)}, bf16[128,128]{1,0:T(8,128)(2,1)S(1)}, u32[]{:S(2)}, u32[]{:S(2)}) collective-permute-start(bf16[128,128]{1,0:T(8,128)(2,1)S(1)} %collective-permute-done.25), channel_id=1, source_target_pairs={{0,8},{8,0},{16,24},{24,16},{32,40},{40,32},{48,56},{56,48},{64,72... | collective-permute-start | bytes 98312 | tf_op jit(solution)/shard_map/ppermute | solution.py:19
  60.7 2.4 %collective-permute-start.28 = (bf16[128,128]{1,0:T(8,128)(2,1)S(1)}, bf16[128,128]{1,0:T(8,128)(2,1)S(1)}, u32[]{:S(2)}, u32[]{:S(2)}) collective-permute-start(bf16[128,128]{1,0:T(8,128)(2,1)S(1)} %collective-permute-done.27), channel_id=1, source_target_pairs={{0,8},{8,0},{16,24},{24,16},{32,40},{40,32},{48,56},{56,48},{64,72... | collective-permute-start | bytes 98312 | tf_op jit(solution)/shard_map/ppermute | solution.py:19
  63.1 1.9 %collective-permute-start.23 = (bf16[128,128]{1,0:T(8,128)(2,1)S(1)}, bf16[128,128]{1,0:T(8,128)(2,1)S(1)}, u32[]{:S(2)}, u32[]{:S(2)}) collective-permute-start(bf16[128,128]{1,0:T(8,128)(2,1)S(1)} %constant_dynamic-update-slice_fusion.18), channel_id=1, source_target_pairs={{0,8},{8,0},{16,24},{24,16},{32,40},{40,32},{48,56},{56,48},{64,72... | collective-permute-start | bytes 98312 | tf_op jit(solution)/shard_map/ppermute | solution.py:19
  66.3 2.4 %collective-permute-start.31 = (bf16[128,128]{1,0:T(8,128)(2,1)S(1)}, bf16[128,128]{1,0:T(8,128)(2,1)S(1)}, u32[]{:S(2)}, u32[]{:S(2)}) collective-permute-start(bf16[128,128]{1,0:T(8,128)(2,1)S(1)} %constant_dynamic-update-slice_fusion.28), channel_id=1, source_target_pairs={{0,8},{8,0},{16,24},{24,16},{32,40},{40,32},{48,56},{56,48},{64,72... | collective-permute-start | bytes 98312 | tf_op jit(solution)/shard_map/ppermute | solution.py:19
  69.9 1.9 %collective-permute-start.9 = (bf16[1024,128]{1,0:T(8,128)(2,1)}, bf16[1024,128]{1,0:T(8,128)(2,1)}, u32[]{:S(2)}, u32[]{:S(2)}) collective-permute-start(bf16[1024,128]{1,0:T(8,128)(2,1)} %param.10), channel_id=1, source_target_pairs={{0,16},{8,24},{16,0},{24,8},{32,48},{40,56},{48,32},{56,40},{64,80... | collective-permute-start | bytes 786440 | tf_op jit(solution)/shard_map/ppermute | solution.py:19
  71.9 2.9 %collective-permute-start.11 = (bf16[1024,128]{1,0:T(8,128)(2,1)}, bf16[1024,128]{1,0:T(8,128)(2,1)S(1)}, u32[]{:S(2)}, u32[]{:S(2)}) collective-permute-start(bf16[1024,128]{1,0:T(8,128)(2,1)} %param.10), channel_id=1, source_target_pairs={{0,32},{8,40},{16,48},{24,56},{32,0},{40,8},{48,16},{56,24},{64,96... | collective-permute-start | bytes 786440 | tf_op jit(solution)/shard_map/ppermute | solution.py:19
  74.8 2.5 %collective-permute-start.8 = (bf16[1024,128]{1,0:T(8,128)(2,1)}, bf16[1024,128]{1,0:T(8,128)(2,1)}, u32[]{:S(2)}, u32[]{:S(2)}) collective-permute-start(bf16[1024,128]{1,0:T(8,128)(2,1)} %param.10), channel_id=1, source_target_pairs={{0,8},{8,0},{16,24},{24,16},{32,40},{40,32},{48,56},{56,48},{64,72... | collective-permute-start | bytes 786440 | tf_op jit(solution)/shard_map/ppermute | solution.py:19
  80.1 2.9 %collective-permute-start.5 = (bf16[512,128]{1,0:T(8,128)(2,1)S(1)}, bf16[512,128]{1,0:T(8,128)(2,1)S(1)}, u32[]{:S(2)}, u32[]{:S(2)}) collective-permute-start(bf16[512,128]{1,0:T(8,128)(2,1)S(1)} %slice.36), channel_id=1, source_target_pairs={{0,16},{8,24},{16,0},{24,8},{32,48},{40,56},{48,32},{56,40},{64,80... | collective-permute-start | bytes 393224 | tf_op jit(solution)/shard_map/ppermute | solution.py:19
  83.0 2.9 %collective-permute-start.6 = (bf16[512,128]{1,0:T(8,128)(2,1)S(1)}, bf16[512,128]{1,0:T(8,128)(2,1)S(1)}, u32[]{:S(2)}, u32[]{:S(2)}) collective-permute-start(bf16[512,128]{1,0:T(8,128)(2,1)S(1)} %slice.37), channel_id=1, source_target_pairs={{0,32},{8,40},{16,48},{24,56},{32,0},{40,8},{48,16},{56,24},{64,96... | collective-permute-start | bytes 393224 | tf_op jit(solution)/shard_map/ppermute | solution.py:19
  85.9 1.9 %collective-permute-start.13 = (bf16[512,128]{1,0:T(8,128)(2,1)S(1)}, bf16[512,128]{1,0:T(8,128)(2,1)S(1)}, u32[]{:S(2)}, u32[]{:S(2)}) collective-permute-start(bf16[512,128]{1,0:T(8,128)(2,1)S(1)} %slice.38), channel_id=1, source_target_pairs={{0,16},{8,24},{16,0},{24,8},{32,48},{40,56},{48,32},{56,40},{64,80... | collective-permute-start | bytes 393224 | tf_op jit(solution)/shard_map/ppermute | solution.py:19
  88.8 2.9 %collective-permute-start.14 = (bf16[512,128]{1,0:T(8,128)(2,1)S(1)}, bf16[512,128]{1,0:T(8,128)(2,1)S(1)}, u32[]{:S(2)}, u32[]{:S(2)}) collective-permute-start(bf16[512,128]{1,0:T(8,128)(2,1)S(1)} %slice.39), channel_id=1, source_target_pairs={{0,32},{8,40},{16,48},{24,56},{32,0},{40,8},{48,16},{56,24},{64,96... | collective-permute-start | bytes 393224 | tf_op jit(solution)/shard_map/ppermute | solution.py:19
  92.7 3.4 %collective-permute-start.2 = (bf16[1024,128]{1,0:T(8,128)(2,1)S(1)}, bf16[1024,128]{1,0:T(8,128)(2,1)S(1)}, u32[]{:S(2)}, u32[]{:S(2)}) collective-permute-start(bf16[1024,128]{1,0:T(8,128)(2,1)S(1)} %collective-permute-done.1), channel_id=1, source_target_pairs={{0,8},{8,0},{16,24},{24,16},{32,40},{40,32},{48,56},{56,48},{64,72... | collective-permute-start | bytes 786440 | tf_op jit(solution)/shard_map/ppermute | solution.py:19
  99.5 2.0 %collective-permute-start.4 = (bf16[1024,128]{1,0:T(8,128)(2,1)S(1)}, bf16[1024,128]{1,0:T(8,128)(2,1)S(1)}, u32[]{:S(2)}, u32[]{:S(2)}) collective-permute-start(bf16[1024,128]{1,0:T(8,128)(2,1)S(1)} %collective-permute-done.3), channel_id=1, source_target_pairs={{0,8},{8,0},{16,24},{24,16},{32,40},{40,32},{48,56},{56,48},{64,72... | collective-permute-start | bytes 786440 | tf_op jit(solution)/shard_map/ppermute | solution.py:19
  101.5 2.4 %collective-permute-start.10 = (bf16[1024,128]{1,0:T(8,128)(2,1)}, bf16[1024,128]{1,0:T(8,128)(2,1)S(1)}, u32[]{:S(2)}, u32[]{:S(2)}) collective-permute-start(bf16[1024,128]{1,0:T(8,128)(2,1)} %collective-permute-done.9), channel_id=1, source_target_pairs={{0,8},{8,0},{16,24},{24,16},{32,40},{40,32},{48,56},{56,48},{64,72... | collective-permute-start | bytes 786440 | tf_op jit(solution)/shard_map/ppermute | solution.py:19
  104.0 1.9 %collective-permute-start.12 = (bf16[1024,128]{1,0:T(8,128)(2,1)S(1)}, bf16[1024,128]{1,0:T(8,128)(2,1)S(1)}, u32[]{:S(2)}, u32[]{:S(2)}) collective-permute-start(bf16[1024,128]{1,0:T(8,128)(2,1)S(1)} %collective-permute-done.11), channel_id=1, source_target_pairs={{0,8},{8,0},{16,24},{24,16},{32,40},{40,32},{48,56},{56,48},{64,72... | collective-permute-start | bytes 786440 | tf_op jit(solution)/shard_map/ppermute | solution.py:19
  105.9 2.4 %collective-permute-start.7 = (bf16[1024,128]{1,0:T(8,128)(2,1)S(1)}, bf16[1024,128]{1,0:T(8,128)(2,1)S(1)}, u32[]{:S(2)}, u32[]{:S(2)}) collective-permute-start(bf16[1024,128]{1,0:T(8,128)(2,1)S(1)} %pad_maximum_fusion), channel_id=1, source_target_pairs={{0,8},{8,0},{16,24},{24,16},{32,40},{40,32},{48,56},{56,48},{64,72... | collective-permute-start | bytes 786440 | tf_op jit(solution)/shard_map/ppermute | solution.py:19
  108.4 1.9 %collective-permute-start.15 = (bf16[1024,128]{1,0:T(8,128)(2,1)S(1)}, bf16[1024,128]{1,0:T(8,128)(2,1)S(1)}, u32[]{:S(2)}, u32[]{:S(2)}) collective-permute-start(bf16[1024,128]{1,0:T(8,128)(2,1)S(1)} %pad_maximum_fusion.1), channel_id=1, source_target_pairs={{0,8},{8,0},{16,24},{24,16},{32,40},{40,32},{48,56},{56,48},{64,72... | collective-permute-start | bytes 786440 | tf_op jit(solution)/shard_map/ppermute | solution.py:19
  111.8 47.9 %shard_map.64 = bf16[128,1024]{1,0:T(8,128)(2,1)S(1)} custom-call(s32[10]{0:T(128)S(1)} %pad_add_fusion.info_ref, bf16[128,1024]{1,0:T(8,128)(2,1)S(1)} %copy-done.1, bf16[8192,128]{1,0:T(8,128)(2,1)S(1)} %constant_dynamic-update-slice_fusion.kc_ref, bf16[8192,128]{1,0:T(8,128)(2,1)S(1)} %constant_dynamic-update-slice_fusion.9.vc_ref, ...), custom_call_target="tpu_custom_call" | custom-call | tf_op jit(solution)/shard_map/pallas_call | solution.py:117
  159.8 10.0 %all_to_all.19 = bf16[8,16,1024]{2,1,0:T(8,128)(2,1)S(1)} all-to-all(bf16[8,16,1024]{2,1,0:T(8,128)(2,1)S(1)} %bitcast.43), channel_id=1, replica_groups=mesh['req'=64,'tp'=8] {'tp'}, dimensions={0} | all-to-all | bytes 524288 | tf_op jit(solution)/shard_map/all_to_all | solution.py:157
  (94 shorter events, 28.0 us)
Async XLA Ops:
  0.0 88.8 %collective-permute-start = (bf16[1024,128]{1,0:T(8,128)(2,1)}, bf16[1024,128]{1,0:T(8,128)(2,1)}, u32[]{:S(2)}, u32[]{:S(2)}) collective-permute-start(bf16[1024,128]{1,0:T(8,128)(2,1)} %param.9), channel_id=1, source_target_pairs={{0,8},{8,0},{16,24},{24,16},{32,40},{40,32},{48,56},{56,48},{64,72... | collective-permute-start | bytes 786440 | tf_op jit(solution)/shard_map/ppermute | solution.py:19
  8.7 71.3 %collective-permute-start.1 = (bf16[1024,128]{1,0:T(8,128)(2,1)}, bf16[1024,128]{1,0:T(8,128)(2,1)S(1)}, u32[]{:S(2)}, u32[]{:S(2)}) collective-permute-start(bf16[1024,128]{1,0:T(8,128)(2,1)} %param.9), channel_id=1, source_target_pairs={{0,16},{8,24},{16,0},{24,8},{32,48},{40,56},{48,32},{56,40},{64,80... | collective-permute-start | bytes 786440 | tf_op jit(solution)/shard_map/ppermute | solution.py:19
  10.7 64.1 %collective-permute-start.3 = (bf16[1024,128]{1,0:T(8,128)(2,1)}, bf16[1024,128]{1,0:T(8,128)(2,1)S(1)}, u32[]{:S(2)}, u32[]{:S(2)}) collective-permute-start(bf16[1024,128]{1,0:T(8,128)(2,1)} %param.9), channel_id=1, source_target_pairs={{0,32},{8,40},{16,48},{24,56},{32,0},{40,8},{48,16},{56,24},{64,96... | collective-permute-start | bytes 786440 | tf_op jit(solution)/shard_map/ppermute | solution.py:19
  12.6 12.4 %collective-permute-start.16 = (bf16[128,128]{1,0:T(8,128)(2,1)}, bf16[128,128]{1,0:T(8,128)(2,1)S(1)}, u32[]{:S(2)}, u32[]{:S(2)}) collective-permute-start(bf16[128,128]{1,0:T(8,128)(2,1)} %param.7), channel_id=1, source_target_pairs={{0,8},{8,0},{16,24},{24,16},{32,40},{40,32},{48,56},{56,48},{64,72... | collective-permute-start | bytes 98312 | tf_op jit(solution)/shard_map/ppermute | solution.py:19
  14.5 14.1 %collective-permute-start.17 = (bf16[128,128]{1,0:T(8,128)(2,1)}, bf16[128,128]{1,0:T(8,128)(2,1)S(1)}, u32[]{:S(2)}, u32[]{:S(2)}) collective-permute-start(bf16[128,128]{1,0:T(8,128)(2,1)} %param.7), channel_id=1, source_target_pairs={{0,16},{8,24},{16,0},{24,8},{32,48},{40,56},{48,32},{56,40},{64,80... | collective-permute-start | bytes 98312 | tf_op jit(solution)/shard_map/ppermute | solution.py:19
  25.0 9.8 %collective-permute-start.19 = (bf16[128,128]{1,0:T(8,128)(2,1)}, bf16[128,128]{1,0:T(8,128)(2,1)S(1)}, u32[]{:S(2)}, u32[]{:S(2)}) collective-permute-start(bf16[128,128]{1,0:T(8,128)(2,1)} %param.7), channel_id=1, source_target_pairs={{0,32},{8,40},{16,48},{24,56},{32,0},{40,8},{48,16},{56,24},{64,96... | collective-permute-start | bytes 98312 | tf_op jit(solution)/shard_map/ppermute | solution.py:19
  28.6 3.5 %collective-permute-start.24 = (bf16[128,128]{1,0:T(8,128)(2,1)}, bf16[128,128]{1,0:T(8,128)(2,1)S(1)}, u32[]{:S(2)}, u32[]{:S(2)}) collective-permute-start(bf16[128,128]{1,0:T(8,128)(2,1)} %param.8), channel_id=1, source_target_pairs={{0,8},{8,0},{16,24},{24,16},{32,40},{40,32},{48,56},{56,48},{64,72... | collective-permute-start | bytes 98312 | tf_op jit(solution)/shard_map/ppermute | solution.py:19
  32.2 4.9 %collective-permute-start.25 = (bf16[128,128]{1,0:T(8,128)(2,1)}, bf16[128,128]{1,0:T(8,128)(2,1)S(1)}, u32[]{:S(2)}, u32[]{:S(2)}) collective-permute-start(bf16[128,128]{1,0:T(8,128)(2,1)} %param.8), channel_id=1, source_target_pairs={{0,16},{8,24},{16,0},{24,8},{32,48},{40,56},{48,32},{56,40},{64,80... | collective-permute-start | bytes 98312 | tf_op jit(solution)/shard_map/ppermute | solution.py:19
  34.7 5.9 %collective-permute-start.27 = (bf16[128,128]{1,0:T(8,128)(2,1)}, bf16[128,128]{1,0:T(8,128)(2,1)S(1)}, u32[]{:S(2)}, u32[]{:S(2)}) collective-permute-start(bf16[128,128]{1,0:T(8,128)(2,1)} %param.8), channel_id=1, source_target_pairs={{0,32},{8,40},{16,48},{24,56},{32,0},{40,8},{48,16},{56,24},{64,96... | collective-permute-start | bytes 98312 | tf_op jit(solution)/shard_map/ppermute | solution.py:19
  37.0 7.0 %collective-permute-start.21 = (bf16[64,128]{1,0:T(8,128)(2,1)S(1)}, bf16[64,128]{1,0:T(8,128)(2,1)S(1)}, u32[]{:S(2)}, u32[]{:S(2)}) collective-permute-start(bf16[64,128]{1,0:T(8,128)(2,1)S(1)} %slice.40), channel_id=1, source_target_pairs={{0,16},{8,24},{16,0},{24,8},{32,48},{40,56},{48,32},{56,40},{64,80... | collective-permute-start | bytes 49160 | tf_op jit(solution)/shard_map/ppermute | solution.py:19
  40.6 9.8 %collective-permute-start.22 = (bf16[64,128]{1,0:T(8,128)(2,1)S(1)}, bf16[64,128]{1,0:T(8,128)(2,1)S(1)}, u32[]{:S(2)}, u32[]{:S(2)}) collective-permute-start(bf16[64,128]{1,0:T(8,128)(2,1)S(1)} %slice.41), channel_id=1, source_target_pairs={{0,32},{8,40},{16,48},{24,56},{32,0},{40,8},{48,16},{56,24},{64,96... | collective-permute-start | bytes 49160 | tf_op jit(solution)/shard_map/ppermute | solution.py:19
  44.0 4.5 %collective-permute-start.29 = (bf16[64,128]{1,0:T(8,128)(2,1)S(1)}, bf16[64,128]{1,0:T(8,128)(2,1)S(1)}, u32[]{:S(2)}, u32[]{:S(2)}) collective-permute-start(bf16[64,128]{1,0:T(8,128)(2,1)S(1)} %slice.42), channel_id=1, source_target_pairs={{0,16},{8,24},{16,0},{24,8},{32,48},{40,56},{48,32},{56,40},{64,80... | collective-permute-start | bytes 49160 | tf_op jit(solution)/shard_map/ppermute | solution.py:19
  48.5 6.7 %collective-permute-start.30 = (bf16[64,128]{1,0:T(8,128)(2,1)S(1)}, bf16[64,128]{1,0:T(8,128)(2,1)S(1)}, u32[]{:S(2)}, u32[]{:S(2)}) collective-permute-start(bf16[64,128]{1,0:T(8,128)(2,1)S(1)} %slice.43), channel_id=1, source_target_pairs={{0,32},{8,40},{16,48},{24,56},{32,0},{40,8},{48,16},{56,24},{64,96... | collective-permute-start | bytes 49160 | tf_op jit(solution)/shard_map/ppermute | solution.py:19
  50.5 8.2 %collective-permute-start.18 = (bf16[128,128]{1,0:T(8,128)(2,1)S(1)}, bf16[128,128]{1,0:T(8,128)(2,1)S(1)}, u32[]{:S(2)}, u32[]{:S(2)}) collective-permute-start(bf16[128,128]{1,0:T(8,128)(2,1)S(1)} %collective-permute-done.17), channel_id=1, source_target_pairs={{0,8},{8,0},{16,24},{24,16},{32,40},{40,32},{48,56},{56,48},{64,72... | collective-permute-start | bytes 98312 | tf_op jit(solution)/shard_map/ppermute | solution.py:19
  55.2 5.4 %collective-permute-start.20 = (bf16[128,128]{1,0:T(8,128)(2,1)S(1)}, bf16[128,128]{1,0:T(8,128)(2,1)S(1)}, u32[]{:S(2)}, u32[]{:S(2)}) collective-permute-start(bf16[128,128]{1,0:T(8,128)(2,1)S(1)} %collective-permute-done.19), channel_id=1, source_target_pairs={{0,8},{8,0},{16,24},{24,16},{32,40},{40,32},{48,56},{56,48},{64,72... | collective-permute-start | bytes 98312 | tf_op jit(solution)/shard_map/ppermute | solution.py:19
  58.7 4.4 %collective-permute-start.26 = (bf16[128,128]{1,0:T(8,128)(2,1)S(1)}, bf16[128,128]{1,0:T(8,128)(2,1)S(1)}, u32[]{:S(2)}, u32[]{:S(2)}) collective-permute-start(bf16[128,128]{1,0:T(8,128)(2,1)S(1)} %collective-permute-done.25), channel_id=1, source_target_pairs={{0,8},{8,0},{16,24},{24,16},{32,40},{40,32},{48,56},{56,48},{64,72... | collective-permute-start | bytes 98312 | tf_op jit(solution)/shard_map/ppermute | solution.py:19
  60.7 5.6 %collective-permute-start.28 = (bf16[128,128]{1,0:T(8,128)(2,1)S(1)}, bf16[128,128]{1,0:T(8,128)(2,1)S(1)}, u32[]{:S(2)}, u32[]{:S(2)}) collective-permute-start(bf16[128,128]{1,0:T(8,128)(2,1)S(1)} %collective-permute-done.27), channel_id=1, source_target_pairs={{0,8},{8,0},{16,24},{24,16},{32,40},{40,32},{48,56},{56,48},{64,72... | collective-permute-start | bytes 98312 | tf_op jit(solution)/shard_map/ppermute | solution.py:19
  63.1 6.8 %collective-permute-start.23 = (bf16[128,128]{1,0:T(8,128)(2,1)S(1)}, bf16[128,128]{1,0:T(8,128)(2,1)S(1)}, u32[]{:S(2)}, u32[]{:S(2)}) collective-permute-start(bf16[128,128]{1,0:T(8,128)(2,1)S(1)} %constant_dynamic-update-slice_fusion.18), channel_id=1, source_target_pairs={{0,8},{8,0},{16,24},{24,16},{32,40},{40,32},{48,56},{56,48},{64,72... | collective-permute-start | bytes 98312 | tf_op jit(solution)/shard_map/ppermute | solution.py:19
  66.3 5.6 %collective-permute-start.31 = (bf16[128,128]{1,0:T(8,128)(2,1)S(1)}, bf16[128,128]{1,0:T(8,128)(2,1)S(1)}, u32[]{:S(2)}, u32[]{:S(2)}) collective-permute-start(bf16[128,128]{1,0:T(8,128)(2,1)S(1)} %constant_dynamic-update-slice_fusion.28), channel_id=1, source_target_pairs={{0,8},{8,0},{16,24},{24,16},{32,40},{40,32},{48,56},{56,48},{64,72... | collective-permute-start | bytes 98312 | tf_op jit(solution)/shard_map/ppermute | solution.py:19
  69.9 16.0 %collective-permute-start.9 = (bf16[1024,128]{1,0:T(8,128)(2,1)}, bf16[1024,128]{1,0:T(8,128)(2,1)}, u32[]{:S(2)}, u32[]{:S(2)}) collective-permute-start(bf16[1024,128]{1,0:T(8,128)(2,1)} %param.10), channel_id=1, source_target_pairs={{0,16},{8,24},{16,0},{24,8},{32,48},{40,56},{48,32},{56,40},{64,80... | collective-permute-start | bytes 786440 | tf_op jit(solution)/shard_map/ppermute | solution.py:19
  71.9 11.1 %collective-permute-start.11 = (bf16[1024,128]{1,0:T(8,128)(2,1)}, bf16[1024,128]{1,0:T(8,128)(2,1)S(1)}, u32[]{:S(2)}, u32[]{:S(2)}) collective-permute-start(bf16[1024,128]{1,0:T(8,128)(2,1)} %param.10), channel_id=1, source_target_pairs={{0,32},{8,40},{16,48},{24,56},{32,0},{40,8},{48,16},{56,24},{64,96... | collective-permute-start | bytes 786440 | tf_op jit(solution)/shard_map/ppermute | solution.py:19
  74.8 17.9 %collective-permute-start.8 = (bf16[1024,128]{1,0:T(8,128)(2,1)}, bf16[1024,128]{1,0:T(8,128)(2,1)}, u32[]{:S(2)}, u32[]{:S(2)}) collective-permute-start(bf16[1024,128]{1,0:T(8,128)(2,1)} %param.10), channel_id=1, source_target_pairs={{0,8},{8,0},{16,24},{24,16},{32,40},{40,32},{48,56},{56,48},{64,72... | collective-permute-start | bytes 786440 | tf_op jit(solution)/shard_map/ppermute | solution.py:19
  80.1 19.4 %collective-permute-start.5 = (bf16[512,128]{1,0:T(8,128)(2,1)S(1)}, bf16[512,128]{1,0:T(8,128)(2,1)S(1)}, u32[]{:S(2)}, u32[]{:S(2)}) collective-permute-start(bf16[512,128]{1,0:T(8,128)(2,1)S(1)} %slice.36), channel_id=1, source_target_pairs={{0,16},{8,24},{16,0},{24,8},{32,48},{40,56},{48,32},{56,40},{64,80... | collective-permute-start | bytes 393224 | tf_op jit(solution)/shard_map/ppermute | solution.py:19
  83.0 18.5 %collective-permute-start.6 = (bf16[512,128]{1,0:T(8,128)(2,1)S(1)}, bf16[512,128]{1,0:T(8,128)(2,1)S(1)}, u32[]{:S(2)}, u32[]{:S(2)}) collective-permute-start(bf16[512,128]{1,0:T(8,128)(2,1)S(1)} %slice.37), channel_id=1, source_target_pairs={{0,32},{8,40},{16,48},{24,56},{32,0},{40,8},{48,16},{56,24},{64,96... | collective-permute-start | bytes 393224 | tf_op jit(solution)/shard_map/ppermute | solution.py:19
  85.9 18.1 %collective-permute-start.13 = (bf16[512,128]{1,0:T(8,128)(2,1)S(1)}, bf16[512,128]{1,0:T(8,128)(2,1)S(1)}, u32[]{:S(2)}, u32[]{:S(2)}) collective-permute-start(bf16[512,128]{1,0:T(8,128)(2,1)S(1)} %slice.38), channel_id=1, source_target_pairs={{0,16},{8,24},{16,0},{24,8},{32,48},{40,56},{48,32},{56,40},{64,80... | collective-permute-start | bytes 393224 | tf_op jit(solution)/shard_map/ppermute | solution.py:19
  88.8 17.1 %collective-permute-start.14 = (bf16[512,128]{1,0:T(8,128)(2,1)S(1)}, bf16[512,128]{1,0:T(8,128)(2,1)S(1)}, u32[]{:S(2)}, u32[]{:S(2)}) collective-permute-start(bf16[512,128]{1,0:T(8,128)(2,1)S(1)} %slice.39), channel_id=1, source_target_pairs={{0,32},{8,40},{16,48},{24,56},{32,0},{40,8},{48,16},{56,24},{64,96... | collective-permute-start | bytes 393224 | tf_op jit(solution)/shard_map/ppermute | solution.py:19
  92.7 15.7 %collective-permute-start.2 = (bf16[1024,128]{1,0:T(8,128)(2,1)S(1)}, bf16[1024,128]{1,0:T(8,128)(2,1)S(1)}, u32[]{:S(2)}, u32[]{:S(2)}) collective-permute-start(bf16[1024,128]{1,0:T(8,128)(2,1)S(1)} %collective-permute-done.1), channel_id=1, source_target_pairs={{0,8},{8,0},{16,24},{24,16},{32,40},{40,32},{48,56},{56,48},{64,72... | collective-permute-start | bytes 786440 | tf_op jit(solution)/shard_map/ppermute | solution.py:19
  99.5 10.9 %collective-permute-start.4 = (bf16[1024,128]{1,0:T(8,128)(2,1)S(1)}, bf16[1024,128]{1,0:T(8,128)(2,1)S(1)}, u32[]{:S(2)}, u32[]{:S(2)}) collective-permute-start(bf16[1024,128]{1,0:T(8,128)(2,1)S(1)} %collective-permute-done.3), channel_id=1, source_target_pairs={{0,8},{8,0},{16,24},{24,16},{32,40},{40,32},{48,56},{56,48},{64,72... | collective-permute-start | bytes 786440 | tf_op jit(solution)/shard_map/ppermute | solution.py:19
  101.5 9.0 %collective-permute-start.10 = (bf16[1024,128]{1,0:T(8,128)(2,1)}, bf16[1024,128]{1,0:T(8,128)(2,1)S(1)}, u32[]{:S(2)}, u32[]{:S(2)}) collective-permute-start(bf16[1024,128]{1,0:T(8,128)(2,1)} %collective-permute-done.9), channel_id=1, source_target_pairs={{0,8},{8,0},{16,24},{24,16},{32,40},{40,32},{48,56},{56,48},{64,72... | collective-permute-start | bytes 786440 | tf_op jit(solution)/shard_map/ppermute | solution.py:19
  104.0 6.6 %collective-permute-start.12 = (bf16[1024,128]{1,0:T(8,128)(2,1)S(1)}, bf16[1024,128]{1,0:T(8,128)(2,1)S(1)}, u32[]{:S(2)}, u32[]{:S(2)}) collective-permute-start(bf16[1024,128]{1,0:T(8,128)(2,1)S(1)} %collective-permute-done.11), channel_id=1, source_target_pairs={{0,8},{8,0},{16,24},{24,16},{32,40},{40,32},{48,56},{56,48},{64,72... | collective-permute-start | bytes 786440 | tf_op jit(solution)/shard_map/ppermute | solution.py:19
  105.9 4.8 %collective-permute-start.7 = (bf16[1024,128]{1,0:T(8,128)(2,1)S(1)}, bf16[1024,128]{1,0:T(8,128)(2,1)S(1)}, u32[]{:S(2)}, u32[]{:S(2)}) collective-permute-start(bf16[1024,128]{1,0:T(8,128)(2,1)S(1)} %pad_maximum_fusion), channel_id=1, source_target_pairs={{0,8},{8,0},{16,24},{24,16},{32,40},{40,32},{48,56},{56,48},{64,72... | collective-permute-start | bytes 786440 | tf_op jit(solution)/shard_map/ppermute | solution.py:19
  108.4 3.4 %collective-permute-start.15 = (bf16[1024,128]{1,0:T(8,128)(2,1)S(1)}, bf16[1024,128]{1,0:T(8,128)(2,1)S(1)}, u32[]{:S(2)}, u32[]{:S(2)}) collective-permute-start(bf16[1024,128]{1,0:T(8,128)(2,1)S(1)} %pad_maximum_fusion.1), channel_id=1, source_target_pairs={{0,8},{8,0},{16,24},{24,16},{32,40},{40,32},{48,56},{56,48},{64,72... | collective-permute-start | bytes 786440 | tf_op jit(solution)/shard_map/ppermute | solution.py:19
  (2 other events, 12.5 us)

commit v2 on v1

v2 whole, which is shorter than its diff:
```python
import math

import jax
import jax.numpy as jnp
from jax import lax
from jax.experimental import pallas as pl
from jax.experimental.pallas import tpu as pltpu
from jax.sharding import PartitionSpec as P

HEAD_SIZE = 128
GROUP_DEVS = 8
NEG_FILL = -1e30
SCALE = 1.0 / math.sqrt(HEAD_SIZE)


def exchange(value, axis, mask):
    pairs = [(source, source ^ mask) for source in range(lax.axis_size(axis))]
    return lax.ppermute(value, axis, pairs)


def gather_group(pack):
    half = pack.shape[0] // 2
    from_x = exchange(pack, "req", 2)
    from_z = exchange(pack, "req", 4)
    diag_lo = exchange(from_z[:half], "req", 2)
    diag_hi = exchange(from_x[half:], "req", 4)
    diag = jnp.concatenate([diag_lo, diag_hi], 0)
    local = jnp.stack([pack, from_x, from_z, diag])
    other = exchange(local, "req", 1)
    return local, other


def attn_kernel(info_ref, q_ref, lk_ref, lv_ref, ls_ref, ok_ref, ov_ref, os_ref, o_ref,
                m_sc, l_sc, acc_sc):
    step = pl.program_id(0)
    last = pl.num_programs(0) - 1
    heads = q_ref.shape[1] // HEAD_SIZE
    tokens = q_ref.shape[0]
    block = lk_ref.shape[0]
    span = ls_ref.shape[0] // 2
    length = info_ref[0]
    first_token = info_ref[1]
    start = info_ref[2 + step]
    span_start = info_ref[2 + GROUP_DEVS + step]

    @pl.when(step == 0)
    def _init():
        m_sc[...] = jnp.full(m_sc.shape, NEG_FILL, jnp.float32)
        l_sc[...] = jnp.zeros(l_sc.shape, jnp.float32)
        acc_sc[...] = jnp.zeros(acc_sc.shape, jnp.float32)

    def process(keys, values, allowed):
        def one_head(h, carry):
            col = pl.multiple_of(h * HEAD_SIZE, HEAD_SIZE)
            qh = q_ref[:, pl.ds(col, HEAD_SIZE)]
            s = lax.dot_general(
                qh, keys, (((1,), (1,)), ((), ())), preferred_element_type=jnp.float32
            )
            if allowed is not None:
                s = jnp.where(allowed, s, NEG_FILL)
            m_prev = m_sc[h]
            m_new = jnp.maximum(m_prev, jnp.max(s, axis=1, keepdims=True))
            alpha = jnp.exp((m_prev - m_new) * SCALE)
            p = jnp.exp((s - m_new) * SCALE)
            l_sc[h] = alpha * l_sc[h] + jnp.sum(p, axis=1, keepdims=True)
            pv = jnp.dot(p.astype(jnp.bfloat16), values, preferred_element_type=jnp.float32)
            acc_sc[h] = alpha * acc_sc[h] + pv
            m_sc[h] = m_new
            return carry

        lax.fori_loop(0, heads, one_head, 0)

    def slot(k_ref, v_ref, s_ref):
        full = start + block <= length
        partial = jnp.logical_and(start < length, jnp.logical_not(full))

        @pl.when(full)
        def _():
            process(k_ref[...], v_ref[...], None)

        @pl.when(partial)
        def _():
            rows = start + lax.broadcasted_iota(jnp.int32, (tokens, block), 1)
            process(k_ref[...], v_ref[...], rows < length)

        @pl.when(span_start < first_token)
        def _():
            process(s_ref[:span], s_ref[span:], None)

        @pl.when(span_start == first_token)
        def _():
            key_pos = lax.broadcasted_iota(jnp.int32, (tokens, span), 1)
            query_pos = lax.broadcasted_iota(jnp.int32, (tokens, span), 0)
            process(s_ref[:span], s_ref[span:], key_pos <= query_pos)

    @pl.when(step % 2 == 0)
    def _local():
        slot(lk_ref, lv_ref, ls_ref)

    @pl.when(step % 2 == 1)
    def _other():
        slot(ok_ref, ov_ref, os_ref)

    @pl.when(step == last)
    def _finish():
        for h in range(heads):
            o_ref[:, h * HEAD_SIZE:(h + 1) * HEAD_SIZE] = (acc_sc[h] / l_sc[h]).astype(o_ref.dtype)


def attention(info, queries, local, other, block, span):
    tokens, width = queries.shape
    heads = width // HEAD_SIZE
    steps = 2 * local.shape[0]
    span_index = 2 * block // (2 * span)

    def views(pick):
        return [
            pl.BlockSpec((None, block, HEAD_SIZE), lambda k, info: (pick(k), 0, 0)),
            pl.BlockSpec((None, block, HEAD_SIZE), lambda k, info: (pick(k), 1, 0)),
            pl.BlockSpec((None, 2 * span, HEAD_SIZE), lambda k, info: (pick(k), span_index, 0)),
        ]

    whole = pl.BlockSpec((tokens, width), lambda k, info: (0, 0))
    in_specs = (
        [whole]
        + views(lambda k: k // 2)
        + views(lambda k: jnp.maximum(k - 1, 0) // 2)
    )
    return pl.pallas_call(
        attn_kernel,
        out_shape=jax.ShapeDtypeStruct((tokens, width), jnp.bfloat16),
        grid_spec=pltpu.PrefetchScalarGridSpec(
            num_scalar_prefetch=1,
            grid=(steps,),
            in_specs=in_specs,
            out_specs=whole,
            scratch_shapes=[
                pltpu.VMEM((heads, tokens, 1), jnp.float32),
                pltpu.VMEM((heads, tokens, 1), jnp.float32),
                pltpu.VMEM((heads, tokens, HEAD_SIZE), jnp.float32),
            ],
        ),
        compiler_params=pltpu.CompilerParams(
            dimension_semantics=("arbitrary",), vmem_limit_bytes=48 * 1024 * 1024
        ),
    )(info, queries, local, local, local, other, other, other)


def body(queries, span_rotated_keys, span_token_values, cache_keys, prompt_cache_values, lengths):
    tok_rows = queries.shape[0]
    cache_rows = cache_keys.shape[0]
    group_devs = lax.axis_size("req") // lengths.shape[0]
    assert group_devs == GROUP_DEVS
    assert span_rotated_keys.shape[0] * 2 * 4 == cache_rows
    device = lax.axis_index("req")
    position = device % GROUP_DEVS
    group_length = lax.dynamic_index_in_dim(lengths, device // GROUP_DEVS, 0, keepdims=False)

    pack = jnp.concatenate(
        [cache_keys, prompt_cache_values, span_rotated_keys, span_token_values], 0
    )
    local, other = gather_group(pack)
    slot_pos = jnp.arange(GROUP_DEVS, dtype=jnp.int32) ^ position
    info = jnp.concatenate(
        [
            jnp.stack([group_length, position * tok_rows]).astype(jnp.int32),
            (slot_pos * cache_rows).astype(jnp.int32),
            (slot_pos * tok_rows).astype(jnp.int32),
        ]
    )
    attended = attention(info, queries, local, other, cache_rows, span_rotated_keys.shape[0])
    return lax.all_to_all(attended, "tp", split_axis=0, concat_axis=1, tiled=True)


def solution(mesh):
    in_specs = (P("req", "tp"), P("req", "tp"), P("req", "tp"), P("req", "tp"), P("req", "tp"), P())
    out_specs = P(("req", "tp"), None)
    return jax.shard_map(body, mesh=mesh, in_specs=in_specs, out_specs=out_specs, check_vma=False)
```

time: 172 us -> 127 us (0.74)
  the two profiles are of different devices: /device:TPU:1 before, /device:TPU:355 now
where the time goes in v2:
time: 127 us; the launch traced here: 126 us
  Pallas kernels  72.6 us (57%)
  waiting for transfers between devices  20.3 us (16%)
  starting transfers between devices  14.2 us (11%)
  blocking collectives  13.3 us (10%)
  local copies, waits for them, and re-layouts  4.9 us (4%)
    pallas_call x1, Pallas kernels, attention(): pl.pallas_call(attn_kernel, out_shape=jax.ShapeDtypeStruct((tokens, width...  72.6 us
    ppermute x5, waiting for transfers between devices, exchange(): return lax.ppermute(value, axis, pairs)  20.3 us
    ppermute x5, starting transfers between devices, exchange(): return lax.ppermute(value, axis, pairs)  14.2 us
    all_to_all x1, blocking collectives, body(): lax.all_to_all(attended, 'tp', split_axis=0, concat_axis=1, tiled=True)  13.3 us
    unnamed x7, local copies, waits for them, and re-layouts  2.74 us
  transfers between devices with their start and end apart: 5, of which 5 were waited for; matrix products, arithmetic and copies ran while one was open for 1% of the time, Pallas kernels for 0%

profile of v2, /device:TPU:355, one launch (start us, length us, event | category | flops | bytes accessed | tf_op | source)
XLA Modules:
  0.0 126.4 jit_solution(4307408921401076498)
XLA Ops:
  0.0 1.0 constant_dynamic-update-slice_fusion.3
  1.0 1.0 constant_dynamic-update-slice_fusion.2
  2.0 0.8 constant_dynamic-update-slice_fusion.1
  2.7 0.8 constant_dynamic-update-slice_fusion
  3.5 2.6 %collective-permute-start.1 = (bf16[2304,128]{1,0:T(8,128)(2,1)S(1)}, bf16[2304,128]{1,0:T(8,128)(2,1)S(1)}, u32[]{:S(2)}, u32[]{:S(2)}) collective-permute-start(bf16[2304,128]{1,0:T(8,128)(2,1)S(1)} %constant_dynamic-update-slice_fusion), channel_id=1, source_target_pairs={{0,32},{8,40},{16,48},{24,56},{32,0},{40,8},{48,16},{56,24},{64,96... | collective-permute-start | bytes 1769480 | tf_op jit(solution)/shard_map/ppermute | solution.py:18
  6.1 2.2 %collective-permute-start = (bf16[2304,128]{1,0:T(8,128)(2,1)S(1)}, bf16[2304,128]{1,0:T(8,128)(2,1)S(1)}, u32[]{:S(2)}, u32[]{:S(2)}) collective-permute-start(bf16[2304,128]{1,0:T(8,128)(2,1)S(1)} %constant_dynamic-update-slice_fusion), channel_id=1, source_target_pairs={{0,16},{8,24},{16,0},{24,8},{32,48},{40,56},{48,32},{56,40},{64,80... | collective-permute-start | bytes 1769480 | tf_op jit(solution)/shard_map/ppermute | solution.py:18
  8.3 11.3 %collective-permute-done.1 = bf16[2304,128]{1,0:T(8,128)(2,1)S(1)} collective-permute-done((bf16[2304,128]{1,0:T(8,128)(2,1)S(1)}, bf16[2304,128]{1,0:T(8,128)(2,1)S(1)}, u32[]{:S(2)}, u32[]{:S(2)}) %collective-permute-start.1) | collective-permute-done | bytes 589856 | tf_op jit(solution)/shard_map/ppermute | solution.py:18
  19.6 2.2 %collective-permute-start.2 = (bf16[1152,128]{1,0:T(8,128)(2,1)S(1)}, bf16[1152,128]{1,0:T(8,128)(2,1)S(1)}, u32[]{:S(2)}, u32[]{:S(2)}) collective-permute-start(bf16[1152,128]{1,0:T(8,128)(2,1)S(1)} %slice.8), channel_id=1, source_target_pairs={{0,16},{8,24},{16,0},{24,8},{32,48},{40,56},{48,32},{56,40},{64,80... | collective-permute-start | bytes 884744 | tf_op jit(solution)/shard_map/ppermute | solution.py:18
  21.8 0.2 collective-permute-done
  22.0 2.6 %collective-permute-start.3 = (bf16[1152,128]{1,0:T(8,128)(2,1)S(1)}, bf16[1152,128]{1,0:T(8,128)(2,1)S(1)}, u32[]{:S(2)}, u32[]{:S(2)}) collective-permute-start(bf16[1152,128]{1,0:T(8,128)(2,1)S(1)} %slice.9), channel_id=1, source_target_pairs={{0,32},{8,40},{16,48},{24,56},{32,0},{40,8},{48,16},{56,24},{64,96... | collective-permute-start | bytes 884744 | tf_op jit(solution)/shard_map/ppermute | solution.py:18
  24.6 3.9 %collective-permute-done.2 = bf16[1152,128]{1,0:T(8,128)(2,1)S(1)} collective-permute-done((bf16[1152,128]{1,0:T(8,128)(2,1)S(1)}, bf16[1152,128]{1,0:T(8,128)(2,1)S(1)}, u32[]{:S(2)}, u32[]{:S(2)}) %collective-permute-start.2) | collective-permute-done | bytes 294944 | tf_op jit(solution)/shard_map/ppermute | solution.py:18
  28.5 2.1 %collective-permute-done.3 = bf16[1152,128]{1,0:T(8,128)(2,1)S(1)} collective-permute-done((bf16[1152,128]{1,0:T(8,128)(2,1)S(1)}, bf16[1152,128]{1,0:T(8,128)(2,1)S(1)}, u32[]{:S(2)}, u32[]{:S(2)}) %collective-permute-start.3) | collective-permute-done | bytes 294944 | tf_op jit(solution)/shard_map/ppermute | solution.py:18
  30.7 0.0 copy-start.1
  30.7 0.0 copy-start
  30.7 0.3 pad_maximum_fusion.lk_ref.lv_ref.ls_ref
  31.0 4.6 %collective-permute-start.4 = (bf16[4,2304,128]{2,1,0:T(8,128)(2,1)S(1)}, bf16[4,2304,128]{2,1,0:T(8,128)(2,1)}, u32[]{:S(2)}, u32[]{:S(2)}) collective-permute-start(bf16[4,2304,128]{2,1,0:T(8,128)(2,1)S(1)} %pad_maximum_fusion.lk_ref.lv_ref.ls_ref), channel_id=1, source_target_pairs={{0,8},{8,0},{16,24},{24,16},{32,40},{40,32},{48,56},{56,48},{64,72... | collective-permute-start | bytes 7077896 | tf_op jit(solution)/shard_map/ppermute | solution.py:18
  35.6 0.0 copy-done.1
  35.6 0.6 dynamic_slice.4
  36.3 0.7 pad_add_fusion.info_ref
  37.0 2.9 %collective-permute-done.4.ok_ref.ov_ref.os_ref = bf16[4,2304,128]{2,1,0:T(8,128)(2,1)} collective-permute-done((bf16[4,2304,128]{2,1,0:T(8,128)(2,1)S(1)}, bf16[4,2304,128]{2,1,0:T(8,128)(2,1)}, u32[]{:S(2)}, u32[]{:S(2)}) %collective-permute-start.4) | collective-permute-done | bytes 2359328 | tf_op jit(solution)/shard_map/ppermute | solution.py:18
  39.9 0.0 copy-done
  39.9 72.6 %shard_map.64 = bf16[128,1024]{1,0:T(8,128)(2,1)S(1)} custom-call(s32[18]{0:T(128)S(1)} %pad_add_fusion.info_ref, bf16[128,1024]{1,0:T(8,128)(2,1)S(1)} %copy-done, bf16[4,2304,128]{2,1,0:T(8,128)(2,1)S(1)} %pad_maximum_fusion.lk_ref.lv_ref.ls_ref, bf16[4,2304,128]{2,1,0:T(8,128)(2,1)S(1)} %pad_maximum_fusion.lk_ref.lv_ref.ls_ref, ...), custom_call_target="tpu_custom_call" | custom-call | tf_op jit(solution)/shard_map/pallas_call | solution.py:129
  112.4 13.3 %all_to_all.19 = bf16[8,16,1024]{2,1,0:T(8,128)(2,1)S(1)} all-to-all(bf16[8,16,1024]{2,1,0:T(8,128)(2,1)S(1)} %bitcast.10), channel_id=1, replica_groups=mesh['req'=64,'tp'=8] {'tp'}, dimensions={0} | all-to-all | bytes 524288 | tf_op jit(solution)/shard_map/all_to_all | solution.py:172
  125.7 0.7 copy.8
  (4 shorter events, 0.1 us)
Async XLA Ops:
  3.5 16.1 %collective-permute-start.1 = (bf16[2304,128]{1,0:T(8,128)(2,1)S(1)}, bf16[2304,128]{1,0:T(8,128)(2,1)S(1)}, u32[]{:S(2)}, u32[]{:S(2)}) collective-permute-start(bf16[2304,128]{1,0:T(8,128)(2,1)S(1)} %constant_dynamic-update-slice_fusion), channel_id=1, source_target_pairs={{0,32},{8,40},{16,48},{24,56},{32,0},{40,8},{48,16},{56,24},{64,96... | collective-permute-start | bytes 1769480 | tf_op jit(solution)/shard_map/ppermute | solution.py:18
  6.1 15.8 %collective-permute-start = (bf16[2304,128]{1,0:T(8,128)(2,1)S(1)}, bf16[2304,128]{1,0:T(8,128)(2,1)S(1)}, u32[]{:S(2)}, u32[]{:S(2)}) collective-permute-start(bf16[2304,128]{1,0:T(8,128)(2,1)S(1)} %constant_dynamic-update-slice_fusion), channel_id=1, source_target_pairs={{0,16},{8,24},{16,0},{24,8},{32,48},{40,56},{48,32},{56,40},{64,80... | collective-permute-start | bytes 1769480 | tf_op jit(solution)/shard_map/ppermute | solution.py:18
  19.6 8.9 %collective-permute-start.2 = (bf16[1152,128]{1,0:T(8,128)(2,1)S(1)}, bf16[1152,128]{1,0:T(8,128)(2,1)S(1)}, u32[]{:S(2)}, u32[]{:S(2)}) collective-permute-start(bf16[1152,128]{1,0:T(8,128)(2,1)S(1)} %slice.8), channel_id=1, source_target_pairs={{0,16},{8,24},{16,0},{24,8},{32,48},{40,56},{48,32},{56,40},{64,80... | collective-permute-start | bytes 884744 | tf_op jit(solution)/shard_map/ppermute | solution.py:18
  22.0 8.7 %collective-permute-start.3 = (bf16[1152,128]{1,0:T(8,128)(2,1)S(1)}, bf16[1152,128]{1,0:T(8,128)(2,1)S(1)}, u32[]{:S(2)}, u32[]{:S(2)}) collective-permute-start(bf16[1152,128]{1,0:T(8,128)(2,1)S(1)} %slice.9), channel_id=1, source_target_pairs={{0,32},{8,40},{16,48},{24,56},{32,0},{40,8},{48,16},{56,24},{64,96... | collective-permute-start | bytes 884744 | tf_op jit(solution)/shard_map/ppermute | solution.py:18
  30.7 4.9 %copy-start.1 = (s32[8]{0:T(128)S(1)}, s32[8]{0:T(128)}, u32[]{:S(2)}) copy-start(s32[8]{0:T(128)} %param.11) | copy-start | bytes 100
  30.7 9.2 %copy-start = (bf16[128,1024]{1,0:T(8,128)(2,1)S(1)}, bf16[128,1024]{1,0:T(8,128)(2,1)}, u32[]{:S(2)}) copy-start(bf16[128,1024]{1,0:T(8,128)(2,1)} %q_ref.1) | copy-start | bytes 786436
  31.0 8.9 %collective-permute-start.4 = (bf16[4,2304,128]{2,1,0:T(8,128)(2,1)S(1)}, bf16[4,2304,128]{2,1,0:T(8,128)(2,1)}, u32[]{:S(2)}, u32[]{:S(2)}) collective-permute-start(bf16[4,2304,128]{2,1,0:T(8,128)(2,1)S(1)} %pad_maximum_fusion.lk_ref.lv_ref.ls_ref), channel_id=1, source_target_pairs={{0,8},{8,0},{16,24},{24,16},{32,40},{40,32},{48,56},{56,48},{64,72... | collective-permute-start | bytes 7077896 | tf_op jit(solution)/shard_map/ppermute | solution.py:18

commit v3 on v2

v3 whole, which is shorter than its diff:
```python
import math

import jax
import jax.numpy as jnp
from jax import lax
from jax.experimental import pallas as pl
from jax.experimental.pallas import tpu as pltpu
from jax.sharding import PartitionSpec as P

HEAD_SIZE = 128
GROUP_DEVS = 8
NEG_FILL = -1e30
SCALE = 1.0 / math.sqrt(HEAD_SIZE)


def exchange(value, axis, mask):
    pairs = [(source, source ^ mask) for source in range(lax.axis_size(axis))]
    return lax.ppermute(value, axis, pairs)


def gather_group(pack):
    half = pack.shape[0] // 2
    from_x = exchange(pack, "req", 2)
    from_z = exchange(pack, "req", 4)
    diag_lo = exchange(from_z[:half], "req", 2)
    diag_hi = exchange(from_x[half:], "req", 4)
    diag = jnp.concatenate([diag_lo, diag_hi], 0)
    local = jnp.stack([pack, from_x, from_z, diag])
    other = exchange(local, "req", 1)
    return local, other


def attn_kernel(info_ref, q_ref, lk_ref, lv_ref, ok_ref, ov_ref, sk_ref, sv_ref, o_ref,
                m_sc, l_sc, acc_sc):
    step = pl.program_id(0)
    last = pl.num_programs(0) - 1
    rows = q_ref.shape[0]
    tokens = o_ref.shape[0]
    heads = rows // tokens
    block = lk_ref.shape[0]
    span = sk_ref.shape[0]
    length = info_ref[0]
    first_token = info_ref[1]
    start = info_ref[2 + jnp.minimum(step, last - 1)]

    @pl.when(step == 0)
    def _init():
        m_sc[...] = jnp.full(m_sc.shape, NEG_FILL, jnp.float32)
        l_sc[...] = jnp.zeros(l_sc.shape, jnp.float32)
        acc_sc[...] = jnp.zeros(acc_sc.shape, jnp.float32)

    def process(keys, values, allowed):
        s = lax.dot_general(
            q_ref[...], keys, (((1,), (1,)), ((), ())), preferred_element_type=jnp.float32
        )
        if allowed is not None:
            s = jnp.where(allowed, s, NEG_FILL)
        m_prev = m_sc[...]
        m_new = jnp.maximum(m_prev, jnp.max(s, axis=1, keepdims=True))
        alpha = jnp.exp((m_prev - m_new) * SCALE)
        p = jnp.exp((s - m_new) * SCALE)
        l_sc[...] = alpha * l_sc[...] + jnp.sum(p, axis=1, keepdims=True)
        pv = jnp.dot(p.astype(jnp.bfloat16), values, preferred_element_type=jnp.float32)
        acc_sc[...] = alpha * acc_sc[...] + pv
        m_sc[...] = m_new

    def slot(k_ref, v_ref):
        full = start + block <= length
        partial = jnp.logical_and(start < length, jnp.logical_not(full))

        @pl.when(full)
        def _():
            process(k_ref[...], v_ref[...], None)

        @pl.when(partial)
        def _():
            key_rows = start + lax.broadcasted_iota(jnp.int32, (rows, block), 1)
            process(k_ref[...], v_ref[...], key_rows < length)

    @pl.when(jnp.logical_and(step < last, step % 2 == 0))
    def _local():
        slot(lk_ref, lv_ref)

    @pl.when(jnp.logical_and(step < last, step % 2 == 1))
    def _other():
        slot(ok_ref, ov_ref)

    @pl.when(step == last)
    def _span():
        key_pos = lax.broadcasted_iota(jnp.int32, (rows, span), 1)
        query_pos = first_token + lax.rem(lax.broadcasted_iota(jnp.int32, (rows, span), 0), tokens)
        process(sk_ref[...], sv_ref[...], key_pos <= query_pos)

    @pl.when(step == last)
    def _finish():
        for h in range(heads):
            rows_h = slice(h * tokens, (h + 1) * tokens)
            o_ref[:, h * HEAD_SIZE:(h + 1) * HEAD_SIZE] = (
                acc_sc[rows_h, :] / l_sc[rows_h, :]
            ).astype(o_ref.dtype)


def attention(info, q_rows, local, other, span_k, span_v, block, tokens):
    rows = q_rows.shape[0]
    heads = rows // tokens
    width = heads * HEAD_SIZE
    slots = 2 * local.shape[0]
    span = span_k.shape[0]

    def views(pick):
        return [
            pl.BlockSpec((None, block, HEAD_SIZE), lambda k, info: (pick(jnp.minimum(k, slots - 1)), 0, 0)),
            pl.BlockSpec((None, block, HEAD_SIZE), lambda k, info: (pick(jnp.minimum(k, slots - 1)), 1, 0)),
        ]

    fixed = lambda k, info: (0, 0)
    in_specs = (
        [pl.BlockSpec((rows, HEAD_SIZE), fixed)]
        + views(lambda k: k // 2)
        + views(lambda k: jnp.maximum(k - 1, 0) // 2)
        + [pl.BlockSpec((span, HEAD_SIZE), fixed), pl.BlockSpec((span, HEAD_SIZE), fixed)]
    )
    return pl.pallas_call(
        attn_kernel,
        out_shape=jax.ShapeDtypeStruct((tokens, width), jnp.bfloat16),
        grid_spec=pltpu.PrefetchScalarGridSpec(
            num_scalar_prefetch=1,
            grid=(slots + 1,),
            in_specs=in_specs,
            out_specs=pl.BlockSpec((tokens, width), fixed),
            scratch_shapes=[
                pltpu.VMEM((rows, 1), jnp.float32),
                pltpu.VMEM((rows, 1), jnp.float32),
                pltpu.VMEM((rows, HEAD_SIZE), jnp.float32),
            ],
        ),
        compiler_params=pltpu.CompilerParams(
            dimension_semantics=("arbitrary",), vmem_limit_bytes=56 * 1024 * 1024
        ),
    )(info, q_rows, local, local, other, other, span_k, span_v)


def heads_as_rows(queries):
    tokens, width = queries.shape
    heads = width // HEAD_SIZE
    return queries.reshape(tokens, heads, HEAD_SIZE).transpose(1, 0, 2).reshape(heads * tokens, HEAD_SIZE)


def body(queries, span_rotated_keys, span_token_values, cache_keys, prompt_cache_values, lengths):
    tok_rows = queries.shape[0]
    cache_rows = cache_keys.shape[0]
    group_devs = lax.axis_size("req") // lengths.shape[0]
    assert group_devs == GROUP_DEVS
    device = lax.axis_index("req")
    position = device % GROUP_DEVS
    group_length = lax.dynamic_index_in_dim(lengths, device // GROUP_DEVS, 0, keepdims=False)

    pack = jnp.concatenate(
        [cache_keys, prompt_cache_values, span_rotated_keys, span_token_values], 0
    )
    local, other = gather_group(pack)
    slot_pos = jnp.arange(GROUP_DEVS, dtype=jnp.int32) ^ position
    info = jnp.concatenate(
        [
            jnp.stack([group_length, position * tok_rows]).astype(jnp.int32),
            (slot_pos * cache_rows).astype(jnp.int32),
        ]
    )
    span_rows = span_rotated_keys.shape[0]
    span_cut = 2 * cache_rows
    by_slot = jnp.stack([local[:, span_cut:], other[:, span_cut:]], 1)
    by_position = by_slot.reshape(GROUP_DEVS, 2 * span_rows, HEAD_SIZE)[slot_pos]
    span_k = by_position[:, :span_rows].reshape(-1, HEAD_SIZE)
    span_v = by_position[:, span_rows:].reshape(-1, HEAD_SIZE)
    attended = attention(
        info, heads_as_rows(queries), local, other, span_k, span_v, cache_rows, tok_rows
    )
    return lax.all_to_all(attended, "tp", split_axis=0, concat_axis=1, tiled=True)


def solution(mesh):
    in_specs = (P("req", "tp"), P("req", "tp"), P("req", "tp"), P("req", "tp"), P("req", "tp"), P())
    out_specs = P(("req", "tp"), None)
    return jax.shard_map(body, mesh=mesh, in_specs=in_specs, out_specs=out_specs, check_vma=False)
```

time: 127 us -> 89.9 us (0.71)
  the two profiles are of different devices: /device:TPU:355 before, /device:TPU:320 now
where the time goes in v3:
time: 89.9 us; the launch traced here: 89.2 us
  Pallas kernels  28 us (31%)
  waiting for transfers between devices  19.1 us (21%)
  blocking collectives  15.7 us (17%)
  starting transfers between devices  14.6 us (16%)
  local copies, waits for them, and re-layouts  10.1 us (11%)
  other arithmetic  1.67 us (2%)
    pallas_call x1, Pallas kernels, attention(): pl.pallas_call(attn_kernel, out_shape=jax.ShapeDtypeStruct((tokens, width...  28 us
    ppermute x5, waiting for transfers between devices, exchange(): return lax.ppermute(value, axis, pairs)  19.1 us
    all_to_all x1, blocking collectives, body(): lax.all_to_all(attended, 'tp', split_axis=0, concat_axis=1, tiled=True)  15.7 us
    ppermute x5, starting transfers between devices, exchange(): return lax.ppermute(value, axis, pairs)  14.6 us
    unnamed x9, local copies, waits for them, and re-layouts  2.78 us
    another operation x3, local copies, waits for them, and re-layouts, body(): by_slot = jnp.stack([local[:, span_cut:], other[:, span_cut:]], 1)  1.82 us
  transfers between devices with their start and end apart: 5, of which 4 were waited for; matrix products, arithmetic and copies ran while one was open for 3% of the time, Pallas kernels for 0%

profile of v3, /device:TPU:320, one launch (start us, length us, event | category | flops | bytes accessed | tf_op | source)
XLA Modules:
  0.0 89.2 jit_solution(1780134177157147712)
XLA Ops:
  0.0 0.0 copy-start
  0.0 1.0 %constant_dynamic-update-slice_fusion.3 = bf16[2304,128]{1,0:T(8,128)(2,1)S(1)} fusion(bf16[1024,128]{1,0:T(8,128)(2,1)} %param.9), kind=kLoop, calls=%fused_computation.10 | loop fusion | bytes 524288
  1.0 1.0 %constant_dynamic-update-slice_fusion.2 = bf16[2304,128]{1,0:T(8,128)(2,1)S(1)} fusion(bf16[2304,128]{1,0:T(8,128)(2,1)S(1)} %constant_dynamic-update-slice_fusion.3, bf16[1024,128]{1,0:T(8,128)(2,1)} %param.10), kind=kLoop, calls=%fused_computation.9 | loop fusion | bytes 524288
  2.0 0.8 constant_dynamic-update-slice_fusion.1
  2.8 0.8 constant_dynamic-update-slice_fusion
  3.5 2.9 %collective-permute-start.1 = (bf16[2304,128]{1,0:T(8,128)(2,1)S(1)}, bf16[2304,128]{1,0:T(8,128)(2,1)S(1)}, u32[]{:S(2)}, u32[]{:S(2)}) collective-permute-start(bf16[2304,128]{1,0:T(8,128)(2,1)S(1)} %constant_dynamic-update-slice_fusion), channel_id=1, source_target_pairs={{0,32},{8,40},{16,48},{24,56},{32,0},{40,8},{48,16},{56,24},{64,96... | collective-permute-start | bytes 1769480 | tf_op jit(solution)/shard_map/ppermute | solution.py:18
  6.5 3.4 %collective-permute-start = (bf16[2304,128]{1,0:T(8,128)(2,1)S(1)}, bf16[2304,128]{1,0:T(8,128)(2,1)S(1)}, u32[]{:S(2)}, u32[]{:S(2)}) collective-permute-start(bf16[2304,128]{1,0:T(8,128)(2,1)S(1)} %constant_dynamic-update-slice_fusion), channel_id=1, source_target_pairs={{0,16},{8,24},{16,0},{24,8},{32,48},{40,56},{48,32},{56,40},{64,80... | collective-permute-start | bytes 1769480 | tf_op jit(solution)/shard_map/ppermute | solution.py:18
  9.9 10.6 %collective-permute-done.1 = bf16[2304,128]{1,0:T(8,128)(2,1)S(1)} collective-permute-done((bf16[2304,128]{1,0:T(8,128)(2,1)S(1)}, bf16[2304,128]{1,0:T(8,128)(2,1)S(1)}, u32[]{:S(2)}, u32[]{:S(2)}) %collective-permute-start.1) | collective-permute-done | bytes 589856 | tf_op jit(solution)/shard_map/ppermute | solution.py:18
  20.5 3.4 %collective-permute-start.2 = (bf16[1152,128]{1,0:T(8,128)(2,1)S(1)}, bf16[1152,128]{1,0:T(8,128)(2,1)S(1)}, u32[]{:S(2)}, u32[]{:S(2)}) collective-permute-start(bf16[1152,128]{1,0:T(8,128)(2,1)S(1)} %slice.26), channel_id=1, source_target_pairs={{0,16},{8,24},{16,0},{24,8},{32,48},{40,56},{48,32},{56,40},{64,80... | collective-permute-start | bytes 884744 | tf_op jit(solution)/shard_map/ppermute | solution.py:18
  23.9 0.0 collective-permute-done
  24.0 2.9 %collective-permute-start.3 = (bf16[1152,128]{1,0:T(8,128)(2,1)S(1)}, bf16[1152,128]{1,0:T(8,128)(2,1)S(1)}, u32[]{:S(2)}, u32[]{:S(2)}) collective-permute-start(bf16[1152,128]{1,0:T(8,128)(2,1)S(1)} %slice.27), channel_id=1, source_target_pairs={{0,32},{8,40},{16,48},{24,56},{32,0},{40,8},{48,16},{56,24},{64,96... | collective-permute-start | bytes 884744 | tf_op jit(solution)/shard_map/ppermute | solution.py:18
  26.9 3.4 %collective-permute-done.2 = bf16[1152,128]{1,0:T(8,128)(2,1)S(1)} collective-permute-done((bf16[1152,128]{1,0:T(8,128)(2,1)S(1)}, bf16[1152,128]{1,0:T(8,128)(2,1)S(1)}, u32[]{:S(2)}, u32[]{:S(2)}) %collective-permute-start.2) | collective-permute-done | bytes 294944 | tf_op jit(solution)/shard_map/ppermute | solution.py:18
  30.3 3.2 %collective-permute-done.3 = bf16[1152,128]{1,0:T(8,128)(2,1)S(1)} collective-permute-done((bf16[1152,128]{1,0:T(8,128)(2,1)S(1)}, bf16[1152,128]{1,0:T(8,128)(2,1)S(1)}, u32[]{:S(2)}, u32[]{:S(2)}) %collective-permute-start.3) | collective-permute-done | bytes 294944 | tf_op jit(solution)/shard_map/ppermute | solution.py:18
  33.5 0.0 copy-start.2
  33.5 0.3 pad_maximum_fusion.lk_ref.lv_ref
  33.8 0.0 copy-start.1
  33.8 1.9 %collective-permute-start.4 = (bf16[4,2304,128]{2,1,0:T(8,128)(2,1)S(1)}, bf16[4,2304,128]{2,1,0:T(8,128)(2,1)}, u32[]{:S(2)}, u32[]{:S(2)}) collective-permute-start(bf16[4,2304,128]{2,1,0:T(8,128)(2,1)S(1)} %pad_maximum_fusion.lk_ref.lv_ref), channel_id=1, source_target_pairs={{0,8},{8,0},{16,24},{24,16},{32,40},{40,32},{48,56},{56,48},{64,72... | collective-permute-start | bytes 7077896 | tf_op jit(solution)/shard_map/ppermute | solution.py:18
  35.8 0.0 copy-done.2
  35.8 0.7 dynamic_slice.4
  36.5 1.3 %pad_add_fusion.info_ref = s32[10]{0:T(128)} fusion(s32[8]{0:T(128)S(1)} %xor_multiply_fusion, s32[1]{0:T(128)} %bitcast, s32[1]{0:T(128)} %dynamic_slice.4), kind=kLoop, calls=%fused_computation.14 | loop fusion | flops 20 | bytes 80 | tf_op jit(solution)/shard_map/concatenate | solution.py:163
  37.8 0.0 copy-done
  37.8 0.8 copy_bitcast_fusion
  38.5 1.9 %collective-permute-done.4.ok_ref.ov_ref = bf16[4,2304,128]{2,1,0:T(8,128)(2,1)} collective-permute-done((bf16[4,2304,128]{2,1,0:T(8,128)(2,1)S(1)}, bf16[4,2304,128]{2,1,0:T(8,128)(2,1)}, u32[]{:S(2)}, u32[]{:S(2)}) %collective-permute-start.4) | collective-permute-done | bytes 2359328 | tf_op jit(solution)/shard_map/ppermute | solution.py:18
  40.4 1.0 %slice_bitcast_fusion = bf16[4,1,256,128]{3,2,0,1:T(8,128)(2,1)S(1)} fusion(bf16[4,2304,128]{2,1,0:T(8,128)(2,1)} %collective-permute-done.4.ok_ref.ov_ref), kind=kLoop, calls=%fused_computation.5 | loop fusion | bytes 524288 | tf_op jit(solution)/shard_map/stack | solution.py:171
  41.4 0.1 pad_maximum_fusion.1
  41.4 0.8 copy.10
  42.3 1.7 %gather_fusion = bf16[8,256,128]{2,1,0:T(8,128)(2,1)S(1)} fusion(bf16[8,256,128]{2,1,0:T(8,128)(2,1)} %bitcast.27, s32[1024]{0:T(1024)S(1)} %pad_clamp_fusion), kind=kCustom, calls=%fused_computation | custom fusion | bytes 1048608 | tf_op jit(solution)/shard_map/gather | solution.py:172
  44.0 0.0 copy-done.1
  44.0 0.8 fusion.1
  44.8 28.0 %shard_map.64 = bf16[128,1024]{1,0:T(8,128)(2,1)} custom-call(s32[10]{0:T(128)} %pad_add_fusion.info_ref, bf16[1024,128]{1,0:T(8,128)(2,1)} %bitcast.32, bf16[4,2304,128]{2,1,0:T(8,128)(2,1)} %copy-done.1, bf16[4,2304,128]{2,1,0:T(8,128)(2,1)} %copy-done.1, bf16[4,2304,128]{2,1,0:T(8,128)(2,1)} %collective-permute-done.4.ok_ref.ov_ref, ...), custom_call_target="tpu_custom_call" | custom-call | tf_op jit(solution)/shard_map/pallas_call | solution.py:123
  72.8 15.7 %all_to_all.19 = bf16[8,16,1024]{2,1,0:T(8,128)(2,1)S(1)} all-to-all(bf16[8,16,1024]{2,1,0:T(8,128)(2,1)} %bitcast.33), channel_id=1, replica_groups=mesh['req'=64,'tp'=8] {'tp'}, dimensions={0} | all-to-all | bytes 524288 | tf_op jit(solution)/shard_map/all_to_all | solution.py:178
  88.5 0.7 copy.13
  (7 shorter events, 0.1 us)
Async XLA Ops:
  0.0 37.8 %copy-start = (bf16[128,1024]{1,0:T(8,128)(2,1)S(1)}, bf16[128,1024]{1,0:T(8,128)(2,1)}, u32[]{:S(2)}) copy-start(bf16[128,1024]{1,0:T(8,128)(2,1)} %param.6) | copy-start | bytes 786436
  3.5 16.9 %collective-permute-start.1 = (bf16[2304,128]{1,0:T(8,128)(2,1)S(1)}, bf16[2304,128]{1,0:T(8,128)(2,1)S(1)}, u32[]{:S(2)}, u32[]{:S(2)}) collective-permute-start(bf16[2304,128]{1,0:T(8,128)(2,1)S(1)} %constant_dynamic-update-slice_fusion), channel_id=1, source_target_pairs={{0,32},{8,40},{16,48},{24,56},{32,0},{40,8},{48,16},{56,24},{64,96... | collective-permute-start | bytes 1769480 | tf_op jit(solution)/shard_map/ppermute | solution.py:18
  6.5 17.5 %collective-permute-start = (bf16[2304,128]{1,0:T(8,128)(2,1)S(1)}, bf16[2304,128]{1,0:T(8,128)(2,1)S(1)}, u32[]{:S(2)}, u32[]{:S(2)}) collective-permute-start(bf16[2304,128]{1,0:T(8,128)(2,1)S(1)} %constant_dynamic-update-slice_fusion), channel_id=1, source_target_pairs={{0,16},{8,24},{16,0},{24,8},{32,48},{40,56},{48,32},{56,40},{64,80... | collective-permute-start | bytes 1769480 | tf_op jit(solution)/shard_map/ppermute | solution.py:18
  20.5 9.8 %collective-permute-start.2 = (bf16[1152,128]{1,0:T(8,128)(2,1)S(1)}, bf16[1152,128]{1,0:T(8,128)(2,1)S(1)}, u32[]{:S(2)}, u32[]{:S(2)}) collective-permute-start(bf16[1152,128]{1,0:T(8,128)(2,1)S(1)} %slice.26), channel_id=1, source_target_pairs={{0,16},{8,24},{16,0},{24,8},{32,48},{40,56},{48,32},{56,40},{64,80... | collective-permute-start | bytes 884744 | tf_op jit(solution)/shard_map/ppermute | solution.py:18
  24.0 9.5 %collective-permute-start.3 = (bf16[1152,128]{1,0:T(8,128)(2,1)S(1)}, bf16[1152,128]{1,0:T(8,128)(2,1)S(1)}, u32[]{:S(2)}, u32[]{:S(2)}) collective-permute-start(bf16[1152,128]{1,0:T(8,128)(2,1)S(1)} %slice.27), channel_id=1, source_target_pairs={{0,32},{8,40},{16,48},{24,56},{32,0},{40,8},{48,16},{56,24},{64,96... | collective-permute-start | bytes 884744 | tf_op jit(solution)/shard_map/ppermute | solution.py:18
  33.5 2.3 %copy-start.2 = (s32[8]{0:T(128)S(1)}, s32[8]{0:T(128)}, u32[]{:S(2)}) copy-start(s32[8]{0:T(128)} %param.11) | copy-start | bytes 100
  33.8 10.1 %copy-start.1 = (bf16[4,2304,128]{2,1,0:T(8,128)(2,1)}, bf16[4,2304,128]{2,1,0:T(8,128)(2,1)S(1)}, u32[]{:S(2)}) copy-start(bf16[4,2304,128]{2,1,0:T(8,128)(2,1)S(1)} %pad_maximum_fusion.lk_ref.lv_ref) | copy-start | bytes 7077892
  33.8 6.6 %collective-permute-start.4 = (bf16[4,2304,128]{2,1,0:T(8,128)(2,1)S(1)}, bf16[4,2304,128]{2,1,0:T(8,128)(2,1)}, u32[]{:S(2)}, u32[]{:S(2)}) collective-permute-start(bf16[4,2304,128]{2,1,0:T(8,128)(2,1)S(1)} %pad_maximum_fusion.lk_ref.lv_ref), channel_id=1, source_target_pairs={{0,8},{8,0},{16,24},{24,16},{32,40},{40,32},{48,56},{56,48},{64,72... | collective-permute-start | bytes 7077896 | tf_op jit(solution)/shard_map/ppermute | solution.py:18

commit v4 on v3

v4 whole, which is shorter than its diff:
```python
import math

import jax
import jax.numpy as jnp
from jax import lax
from jax.experimental import pallas as pl
from jax.experimental.pallas import tpu as pltpu
from jax.sharding import Mesh, PartitionSpec as P

HEAD_SIZE = 128
GROUP_DEVS = 8
GROUP_COUNT = 8
NEG_FILL = -1e30
SCALE = 1.0 / math.sqrt(HEAD_SIZE)


def attn_kernel(info_ref, q_ref, k_ref, v_ref, sk_ref, sv_ref, o_ref, m_sc, l_sc, acc_sc):
    step = pl.program_id(0)
    last = pl.num_programs(0) - 1
    rows = q_ref.shape[0]
    tokens = o_ref.shape[0]
    heads = rows // tokens
    block = k_ref.shape[0]
    span = sk_ref.shape[0]
    length = info_ref[0]
    first_token = info_ref[1]
    start = step * block

    @pl.when(step == 0)
    def _init():
        m_sc[...] = jnp.full(m_sc.shape, NEG_FILL, jnp.float32)
        l_sc[...] = jnp.zeros(l_sc.shape, jnp.float32)
        acc_sc[...] = jnp.zeros(acc_sc.shape, jnp.float32)

    def process(keys, values, allowed):
        s = lax.dot_general(
            q_ref[...], keys, (((1,), (1,)), ((), ())), preferred_element_type=jnp.float32
        )
        if allowed is not None:
            s = jnp.where(allowed, s, NEG_FILL)
        m_prev = m_sc[...]
        m_new = jnp.maximum(m_prev, jnp.max(s, axis=1, keepdims=True))
        alpha = jnp.exp((m_prev - m_new) * SCALE)
        p = jnp.exp((s - m_new) * SCALE)
        l_sc[...] = alpha * l_sc[...] + jnp.sum(p, axis=1, keepdims=True)
        pv = jnp.dot(p.astype(jnp.bfloat16), values, preferred_element_type=jnp.float32)
        acc_sc[...] = alpha * acc_sc[...] + pv
        m_sc[...] = m_new

    def slot(k_ref, v_ref):
        full = start + block <= length
        partial = jnp.logical_and(start < length, jnp.logical_not(full))

        @pl.when(full)
        def _():
            process(k_ref[...], v_ref[...], None)

        @pl.when(partial)
        def _():
            key_rows = start + lax.broadcasted_iota(jnp.int32, (rows, block), 1)
            process(k_ref[...], v_ref[...], key_rows < length)

    @pl.when(step < last)
    def _cache():
        slot(k_ref, v_ref)

    @pl.when(step == last)
    def _span():
        key_pos = lax.broadcasted_iota(jnp.int32, (rows, span), 1)
        query_pos = first_token + lax.rem(lax.broadcasted_iota(jnp.int32, (rows, span), 0), tokens)
        process(sk_ref[...], sv_ref[...], key_pos <= query_pos)

    @pl.when(step == last)
    def _finish():
        for h in range(heads):
            rows_h = slice(h * tokens, (h + 1) * tokens)
            o_ref[:, h * HEAD_SIZE:(h + 1) * HEAD_SIZE] = (
                acc_sc[rows_h, :] / l_sc[rows_h, :]
            ).astype(o_ref.dtype)


def attention(info, q_rows, packs, span_k, span_v, block, tokens):
    rows = q_rows.shape[0]
    heads = rows // tokens
    width = heads * HEAD_SIZE
    slots = packs.shape[0]
    span = span_k.shape[0]
    fixed = lambda k, info: (0, 0)
    in_specs = [
        pl.BlockSpec((rows, HEAD_SIZE), fixed),
        pl.BlockSpec((None, block, HEAD_SIZE), lambda k, info: (jnp.minimum(k, slots - 1), 0, 0)),
        pl.BlockSpec((None, block, HEAD_SIZE), lambda k, info: (jnp.minimum(k, slots - 1), 1, 0)),
        pl.BlockSpec((span, HEAD_SIZE), fixed),
        pl.BlockSpec((span, HEAD_SIZE), fixed),
    ]
    return pl.pallas_call(
        attn_kernel,
        out_shape=jax.ShapeDtypeStruct((tokens, width), jnp.bfloat16),
        grid_spec=pltpu.PrefetchScalarGridSpec(
            num_scalar_prefetch=1,
            grid=(slots + 1,),
            in_specs=in_specs,
            out_specs=pl.BlockSpec((tokens, width), fixed),
            scratch_shapes=[
                pltpu.VMEM((rows, 1), jnp.float32),
                pltpu.VMEM((rows, 1), jnp.float32),
                pltpu.VMEM((rows, HEAD_SIZE), jnp.float32),
            ],
        ),
        compiler_params=pltpu.CompilerParams(
            dimension_semantics=("arbitrary",), vmem_limit_bytes=56 * 1024 * 1024
        ),
    )(info, q_rows, packs, packs, span_k, span_v)


def heads_as_rows(queries):
    tokens, width = queries.shape
    heads = width // HEAD_SIZE
    return queries.reshape(tokens, heads, HEAD_SIZE).transpose(1, 0, 2).reshape(heads * tokens, HEAD_SIZE)


def body(queries, span_rotated_keys, span_token_values, cache_keys, prompt_cache_values, lengths):
    tok_rows = queries.shape[0]
    cache_rows = cache_keys.shape[0]
    span_rows = span_rotated_keys.shape[0]
    position = lax.axis_index("pos")
    group_length = lax.dynamic_index_in_dim(lengths, lax.axis_index("grp"), 0, keepdims=False)

    pack = jnp.concatenate(
        [cache_keys, prompt_cache_values, span_rotated_keys, span_token_values], 0
    )
    packs = lax.all_gather(pack, "pos")
    info = jnp.stack([group_length, position * tok_rows]).astype(jnp.int32)
    span_cut = 2 * cache_rows
    span_k = packs[:, span_cut:span_cut + span_rows].reshape(-1, HEAD_SIZE)
    span_v = packs[:, span_cut + span_rows:].reshape(-1, HEAD_SIZE)
    attended = attention(info, heads_as_rows(queries), packs, span_k, span_v, cache_rows, tok_rows)
    return lax.all_to_all(attended, "tp", split_axis=0, concat_axis=1, tiled=True)


def solution(mesh):
    groups = GROUP_COUNT
    req = mesh.shape["req"]
    devices = mesh.devices.reshape(groups, req // groups, mesh.shape["tp"])
    group_mesh = Mesh(devices, ("grp", "pos", "tp"))
    rows = P(("grp", "pos"), "tp")
    in_specs = (rows, rows, rows, rows, rows, P())
    out_specs = P(("grp", "pos", "tp"), None)
    return jax.shard_map(
        body, mesh=group_mesh, in_specs=in_specs, out_specs=out_specs, check_vma=False
    )
```

time: 89.9 us -> 108 us (1.20)
  the two profiles are of different devices: /device:TPU:320 before, /device:TPU:1 now
where the time goes in v4:
time: 108 us; the launch traced here: 107 us
  waiting for transfers between devices  45.6 us (42%)
  Pallas kernels  27.3 us (25%)
  blocking collectives  13.9 us (13%)
  between operations  13.4 us (12%)
  local copies, waits for them, and re-layouts  3.96 us (4%)
  other arithmetic  3.2 us (3%)
    all_gather x1, waiting for transfers between devices, body(): packs = lax.all_gather(pack, 'pos')  45.6 us
    pallas_call x1, Pallas kernels, attention(): pl.pallas_call(attn_kernel, out_shape=jax.ShapeDtypeStruct((tokens, width...  27.3 us
    all_to_all x1, blocking collectives, body(): lax.all_to_all(attended, 'tp', split_axis=0, concat_axis=1, tiled=True)  13.9 us
  transfers between devices with their start and end apart: 1, of which 1 were waited for; matrix products, arithmetic and copies ran while one was open for 2% of the time, Pallas kernels for 0%

profile of v4, /device:TPU:1, one launch (start us, length us, event | category | flops | bytes accessed | tf_op | source)
XLA Modules:
  0.0 107.4 jit_solution(4933513508974205160)
XLA Ops:
  6.5 0.0 copy-start
  6.5 0.0 copy-start.1
  6.5 0.0 all-gather.3.cloned.1.call-start
  6.5 2.0 %pad_maximum_fusion = bf16[2304,128]{1,0:T(8,128)(2,1)} fusion(bf16[128,128]{1,0:T(8,128)(2,1)} %param.8, bf16[128,128]{1,0:T(8,128)(2,1)} %param.7, bf16[1024,128]{1,0:T(8,128)(2,1)} %param.10, bf16[1024,128]{1,0:T(8,128)(2,1)} %param.9), kind=kLoop, calls=%fused_computation | loop fusion | flops 2359296 | bytes 1179648 | tf_op jit(solution)/shard_map/concatenate | solution.py:129
  8.5 0.0 all-gather.3.cloned.1.call-update
  8.6 0.0 copy-done.1
  8.6 0.6 dynamic_slice.4
  9.2 1.2 %pad_add_fusion.info_ref = s32[2]{0:T(128)} fusion(s32[1]{0:T(128)} %bitcast, s32[1]{0:T(128)} %dynamic_slice.4), kind=kLoop, calls=%fused_computation.2 | loop fusion | flops 2 | bytes 16 | tf_op jit(solution)/shard_map/stack | solution.py:133
  10.4 0.0 copy-done
  10.4 0.8 copy_bitcast_fusion
  11.1 45.6 %all-gather.3.cloned.1.call-done = bf16[18432,128]{1,0:T(8,128)(2,1)} async-done(((bf16[2304,128]{1,0:T(8,128)(2,1)}), bf16[18432,128]{1,0:T(8,128)(2,1)}) %all-gather.3.cloned.1.call-update) | async-done | bytes 4718608 | tf_op jit(solution)/shard_map/all_gather | solution.py:132
  56.7 1.9 %fusion = (bf16[8,128,128]{2,1,0:T(8,128)(2,1)}, bf16[8,128,128]{2,1,0:T(8,128)(2,1)}) fusion(bf16[8,2304,128]{2,1,0:T(8,128)(2,1)} %bitcast.16), kind=kLoop, calls=%fused_computation.3 | loop fusion | bytes 1048576 | tf_op jit(solution)/shard_map/slice | solution.py:136
  58.6 27.3 %shard_map.64 = bf16[128,1024]{1,0:T(8,128)(2,1)} custom-call(s32[2]{0:T(128)} %pad_add_fusion.info_ref, bf16[1024,128]{1,0:T(8,128)(2,1)} %bitcast.20, bf16[8,2304,128]{2,1,0:T(8,128)(2,1)} %bitcast.17, bf16[8,2304,128]{2,1,0:T(8,128)(2,1)} %bitcast.18, bf16[1024,128]{1,0:T(8,128)(2,1)} %bitcast.23, bf16[1024,128]{1,0:T(8,128)(2,1)} %bitcast.22), custom_call_target="tpu_custom_call" | custom-call | tf_op jit(solution)/shard_map/pallas_call | solution.py:96
  86.0 13.9 %all_to_all.19 = bf16[8,16,1024]{2,1,0:T(8,128)(2,1)S(1)} all-to-all(bf16[8,16,1024]{2,1,0:T(8,128)(2,1)} %bitcast.21), channel_id=1, replica_groups=mesh['grp'=8,'pos'=8,'tp'=8] {'tp'}, dimensions={0} | all-to-all | bytes 524288 | tf_op jit(solution)/shard_map/all_to_all | solution.py:138
  99.8 0.7 copy.10
Async XLA Ops:
  6.5 3.8 %copy-start = (bf16[128,1024]{1,0:T(8,128)(2,1)S(1)}, bf16[128,1024]{1,0:T(8,128)(2,1)}, u32[]{:S(2)}) copy-start(bf16[128,1024]{1,0:T(8,128)(2,1)} %param.6) | copy-start | bytes 786436
  6.5 2.0 %copy-start.1 = (s32[8]{0:T(128)S(1)}, s32[8]{0:T(128)}, u32[]{:S(2)}) copy-start(s32[8]{0:T(128)} %param.11) | copy-start | bytes 100
  6.5 50.2 %all-gather.3.cloned.1.call-start = ((), (), s32[]{:S(2)}) async-start(), calls=%async_computation.1 | async-start | bytes 5308416 | tf_op jit(solution)/shard_map/all_gather | solution.py:132
Sparse Core Ops, SparseCore 0:
  9.5 47.1 all-gather.2

commit v5 on v3

--- a/solution.py
+++ b/solution.py
@@ -30,21 +30,40 @@
     return local, other
 
 
-def attn_kernel(info_ref, q_ref, lk_ref, lv_ref, ok_ref, ov_ref, sk_ref, sv_ref, o_ref,
-                m_sc, l_sc, acc_sc):
+def span_copies(info_ref, local_any, other_any, sk_sc, sv_sc, sems, block, span):
+    copies = []
+    for j in range(local_any.shape[0]):
+        for parity, source in ((0, local_any), (1, other_any)):
+            slot = 2 * j + parity
+            offset = pl.multiple_of(info_ref[2 + GROUP_DEVS + slot], span)
+            for part, target in ((0, sk_sc), (1, sv_sc)):
+                copies.append(
+                    pltpu.make_async_copy(
+                        source.at[j, pl.ds(2 * block + part * span, span), :],
+                        target.at[pl.ds(offset, span), :],
+                        sems.at[2 * slot + part],
+                    )
+                )
+    return copies
+
+
+def attn_kernel(info_ref, q_ref, lk_ref, lv_ref, ok_ref, ov_ref, la_ref, oa_ref, o_ref,
+                m_sc, l_sc, acc_sc, sk_sc, sv_sc, sems):
     step = pl.program_id(0)
     last = pl.num_programs(0) - 1
     rows = q_ref.shape[0]
     tokens = o_ref.shape[0]
     heads = rows // tokens
     block = lk_ref.shape[0]
-    span = sk_ref.shape[0]
+    span = sk_sc.shape[0] // GROUP_DEVS
     length = info_ref[0]
     first_token = info_ref[1]
     start = info_ref[2 + jnp.minimum(step, last - 1)]
 
     @pl.when(step == 0)
     def _init():
+        for copy in span_copies(info_ref, la_ref, oa_ref, sk_sc, sv_sc, sems, block, span):
+            copy.start()
         m_sc[...] = jnp.full(m_sc.shape, NEG_FILL, jnp.float32)
         l_sc[...] = jnp.zeros(l_sc.shape, jnp.float32)
         acc_sc[...] = jnp.zeros(acc_sc.shape, jnp.float32)
@@ -87,9 +106,12 @@
 
     @pl.when(step == last)
     def _span():
-        key_pos = lax.broadcasted_iota(jnp.int32, (rows, span), 1)
-        query_pos = first_token + lax.rem(lax.broadcasted_iota(jnp.int32, (rows, span), 0), tokens)
-        process(sk_ref[...], sv_ref[...], key_pos <= query_pos)
+        for copy in span_copies(info_ref, la_ref, oa_ref, sk_sc, sv_sc, sems, block, span):
+            copy.wait()
+        span_rows = sk_sc.shape[0]
+        key_pos = lax.broadcasted_iota(jnp.int32, (rows, span_rows), 1)
+        query_pos = first_token + lax.rem(lax.broadcasted_iota(jnp.int32, (rows, span_rows), 0), tokens)
+        process(sk_sc[...], sv_sc[...], key_pos <= query_pos)
 
     @pl.when(step == last)
     def _finish():
@@ -100,12 +122,11 @@
             ).astype(o_ref.dtype)
 
 
-def attention(info, q_rows, local, other, span_k, span_v, block, tokens):
+def attention(info, q_rows, local, other, block, span, tokens):
     rows = q_rows.shape[0]
     heads = rows // tokens
     width = heads * HEAD_SIZE
     slots = 2 * local.shape[0]
-    span = span_k.shape[0]
 
     def views(pick):
         return [
@@ -118,7 +139,7 @@
         [pl.BlockSpec((rows, HEAD_SIZE), fixed)]
         + views(lambda k: k // 2)
         + views(lambda k: jnp.maximum(k - 1, 0) // 2)
-        + [pl.BlockSpec((span, HEAD_SIZE), fixed), pl.BlockSpec((span, HEAD_SIZE), fixed)]
+        + [pl.BlockSpec(memory_space=pl.ANY), pl.BlockSpec(memory_space=pl.ANY)]
     )
     return pl.pallas_call(
         attn_kernel,
@@ -132,12 +153,32 @@
                 pltpu.VMEM((rows, 1), jnp.float32),
                 pltpu.VMEM((rows, 1), jnp.float32),
                 pltpu.VMEM((rows, HEAD_SIZE), jnp.float32),
+                pltpu.VMEM((slots * span, HEAD_SIZE), jnp.bfloat16),
+                pltpu.VMEM((slots * span, HEAD_SIZE), jnp.bfloat16),
+                pltpu.SemaphoreType.DMA((4 * slots,)),
             ],
         ),
         compiler_params=pltpu.CompilerParams(
             dimension_semantics=("arbitrary",), vmem_limit_bytes=56 * 1024 * 1024
         ),
-    )(info, q_rows, local, local, other, other, span_k, span_v)
+    )(info, q_rows, local, local, other, other, local, other)
+
+
+def pack_kernel(k_ref, v_ref, sk_ref, sv_ref, o_ref):
+    rows = k_ref.shape[0]
+    span = sk_ref.shape[0]
+    o_ref[0:rows, :] = k_ref[...]
+    o_ref[rows:2 * rows, :] = v_ref[...]
+    o_ref[2 * rows:2 * rows + span, :] = sk_ref[...]
+    o_ref[2 * rows + span:2 * rows + 2 * span, :] = sv_ref[...]
+
+
+def make_pack(cache_k, cache_v, span_k, span_v):
+    rows = 2 * cache_k.shape[0] + 2 * span_k.shape[0]
+    return pl.pallas_call(
+        pack_kernel,
+        out_shape=jax.ShapeDtypeStruct((rows, HEAD_SIZE), cache_k.dtype),
+    )(cache_k, cache_v, span_k, span_v)
 
 
 def heads_as_rows(queries):
@@ -155,26 +196,18 @@
     position = device % GROUP_DEVS
     group_length = lax.dynamic_index_in_dim(lengths, device // GROUP_DEVS, 0, keepdims=False)
 
-    pack = jnp.concatenate(
-        [cache_keys, prompt_cache_values, span_rotated_keys, span_token_values], 0
-    )
+    pack = make_pack(cache_keys, prompt_cache_values, span_rotated_keys, span_token_values)
     local, other = gather_group(pack)
     slot_pos = jnp.arange(GROUP_DEVS, dtype=jnp.int32) ^ position
+    span_rows = span_rotated_keys.shape[0]
     info = jnp.concatenate(
         [
             jnp.stack([group_length, position * tok_rows]).astype(jnp.int32),
             (slot_pos * cache_rows).astype(jnp.int32),
+            (slot_pos * span_rows).astype(jnp.int32),
         ]
     )
-    span_rows = span_rotated_keys.shape[0]
-    span_cut = 2 * cache_rows
-    by_slot = jnp.stack([local[:, span_cut:], other[:, span_cut:]], 1)
-    by_position = by_slot.reshape(GROUP_DEVS, 2 * span_rows, HEAD_SIZE)[slot_pos]
-    span_k = by_position[:, :span_rows].reshape(-1, HEAD_SIZE)
-    span_v = by_position[:, span_rows:].reshape(-1, HEAD_SIZE)
-    attended = attention(
-        info, heads_as_rows(queries), local, other, span_k, span_v, cache_rows, tok_rows
-    )
+    attended = attention(info, heads_as_rows(queries), local, other, cache_rows, span_rows, tok_rows)
     return lax.all_to_all(attended, "tp", split_axis=0, concat_axis=1, tiled=True)
 
 

time: 89.9 us -> 84.4 us (0.939)
  the two profiles are of different devices: /device:TPU:320 before, /device:TPU:64 now
where the time goes in v5:
time: 84.4 us; the launch traced here: 83.9 us
  Pallas kernels  29.9 us (35%)
  waiting for transfers between devices  18.2 us (22%)
  starting transfers between devices  16.3 us (19%)
  blocking collectives  15.7 us (19%)
  local copies, waits for them, and re-layouts  2.09 us (2%)
  other arithmetic  1.54 us (2%)
    pallas_call x1, Pallas kernels, attention(): pl.pallas_call(attn_kernel, out_shape=jax.ShapeDtypeStruct((tokens, width...  28 us
    ppermute x5, waiting for transfers between devices, exchange(): return lax.ppermute(value, axis, pairs)  18.2 us
    ppermute x5, starting transfers between devices, exchange(): return lax.ppermute(value, axis, pairs)  16.3 us
    all_to_all x1, blocking collectives, body(): lax.all_to_all(attended, 'tp', split_axis=0, concat_axis=1, tiled=True)  15.7 us
    pallas_call x1, Pallas kernels, make_pack(): pl.pallas_call(pack_kernel, out_shape=jax.ShapeDtypeStruct((rows, HEAD_SI...  1.93 us
  transfers between devices with their start and end apart: 5, of which 4 were waited for; matrix products, arithmetic and copies ran while one was open for 3% of the time, Pallas kernels for 0%

profile of v5, /device:TPU:64, one launch (start us, length us, event | category | flops | bytes accessed | tf_op | source)
XLA Modules:
  0.0 83.9 jit_solution(13769521945446733758)
XLA Ops:
  0.0 0.0 copy-start
  0.0 1.9 %shard_map.64 = bf16[2304,128]{1,0:T(8,128)(2,1)} custom-call(bf16[1024,128]{1,0:T(8,128)(2,1)} %k_ref.1, bf16[1024,128]{1,0:T(8,128)(2,1)} %v_ref.1, bf16[128,128]{1,0:T(8,128)(2,1)} %sk_ref.1, bf16[128,128]{1,0:T(8,128)(2,1)} %sv_ref.1), custom_call_target="tpu_custom_call" | custom-call | tf_op jit(solution)/shard_map/pallas_call | solution.py:178
  1.9 0.0 copy-start.2
  1.9 3.9 %collective-permute-start.1 = (bf16[2304,128]{1,0:T(8,128)(2,1)}, bf16[2304,128]{1,0:T(8,128)(2,1)S(1)}, u32[]{:S(2)}, u32[]{:S(2)}) collective-permute-start(bf16[2304,128]{1,0:T(8,128)(2,1)} %shard_map.64), channel_id=1, source_target_pairs={{0,32},{8,40},{16,48},{24,56},{32,0},{40,8},{48,16},{56,24},{64,96... | collective-permute-start | bytes 1769480 | tf_op jit(solution)/shard_map/ppermute | solution.py:18
  5.9 3.4 %collective-permute-start = (bf16[2304,128]{1,0:T(8,128)(2,1)}, bf16[2304,128]{1,0:T(8,128)(2,1)S(1)}, u32[]{:S(2)}, u32[]{:S(2)}) collective-permute-start(bf16[2304,128]{1,0:T(8,128)(2,1)} %shard_map.64), channel_id=1, source_target_pairs={{0,16},{8,24},{16,0},{24,8},{32,48},{40,56},{48,32},{56,40},{64,80... | collective-permute-start | bytes 1769480 | tf_op jit(solution)/shard_map/ppermute | solution.py:18
  9.3 10.1 %collective-permute-done.1 = bf16[2304,128]{1,0:T(8,128)(2,1)S(1)} collective-permute-done((bf16[2304,128]{1,0:T(8,128)(2,1)}, bf16[2304,128]{1,0:T(8,128)(2,1)S(1)}, u32[]{:S(2)}, u32[]{:S(2)}) %collective-permute-start.1) | collective-permute-done | bytes 589856 | tf_op jit(solution)/shard_map/ppermute | solution.py:18
  19.4 3.4 %collective-permute-start.2 = (bf16[1152,128]{1,0:T(8,128)(2,1)S(1)}, bf16[1152,128]{1,0:T(8,128)(2,1)S(1)}, u32[]{:S(2)}, u32[]{:S(2)}) collective-permute-start(bf16[1152,128]{1,0:T(8,128)(2,1)S(1)} %slice.8), channel_id=1, source_target_pairs={{0,16},{8,24},{16,0},{24,8},{32,48},{40,56},{48,32},{56,40},{64,80... | collective-permute-start | bytes 884744 | tf_op jit(solution)/shard_map/ppermute | solution.py:18
  22.8 0.0 collective-permute-done
  22.9 3.6 %collective-permute-start.3 = (bf16[1152,128]{1,0:T(8,128)(2,1)S(1)}, bf16[1152,128]{1,0:T(8,128)(2,1)S(1)}, u32[]{:S(2)}, u32[]{:S(2)}) collective-permute-start(bf16[1152,128]{1,0:T(8,128)(2,1)S(1)} %slice.9), channel_id=1, source_target_pairs={{0,32},{8,40},{16,48},{24,56},{32,0},{40,8},{48,16},{56,24},{64,96... | collective-permute-start | bytes 884744 | tf_op jit(solution)/shard_map/ppermute | solution.py:18
  26.5 2.9 %collective-permute-done.2 = bf16[1152,128]{1,0:T(8,128)(2,1)S(1)} collective-permute-done((bf16[1152,128]{1,0:T(8,128)(2,1)S(1)}, bf16[1152,128]{1,0:T(8,128)(2,1)S(1)}, u32[]{:S(2)}, u32[]{:S(2)}) %collective-permute-start.2) | collective-permute-done | bytes 294944 | tf_op jit(solution)/shard_map/ppermute | solution.py:18
  29.4 3.2 %collective-permute-done.3 = bf16[1152,128]{1,0:T(8,128)(2,1)S(1)} collective-permute-done((bf16[1152,128]{1,0:T(8,128)(2,1)S(1)}, bf16[1152,128]{1,0:T(8,128)(2,1)S(1)}, u32[]{:S(2)}, u32[]{:S(2)}) %collective-permute-start.3) | collective-permute-done | bytes 294944 | tf_op jit(solution)/shard_map/ppermute | solution.py:18
  32.6 0.0 copy-done.2
  32.6 0.0 copy-start.3
  32.6 0.3 pad_maximum_fusion.lk_ref.lv_ref.la_ref
  32.9 0.0 copy-start.1
  32.9 1.9 %collective-permute-start.4 = (bf16[4,2304,128]{2,1,0:T(8,128)(2,1)S(1)}, bf16[4,2304,128]{2,1,0:T(8,128)(2,1)}, u32[]{:S(2)}, u32[]{:S(2)}) collective-permute-start(bf16[4,2304,128]{2,1,0:T(8,128)(2,1)S(1)} %pad_maximum_fusion.lk_ref.lv_ref.la_ref), channel_id=1, source_target_pairs={{0,8},{8,0},{16,24},{24,16},{32,40},{40,32},{48,56},{56,48},{64,72... | collective-permute-start | bytes 7077896 | tf_op jit(solution)/shard_map/ppermute | solution.py:18
  34.9 0.0 copy-done.3
  34.9 0.6 dynamic_slice.4
  35.5 1.2 %pad_add_fusion.info_ref = s32[18]{0:T(128)} fusion(s32[8]{0:T(128)S(1)} %get-tuple-element.5, s32[8]{0:T(128)S(1)} %get-tuple-element.6, s32[1]{0:T(128)} %bitcast, s32[1]{0:T(128)} %dynamic_slice.4), kind=kLoop, calls=%fused_computation.3 | loop fusion | flops 54 | bytes 144 | tf_op jit(solution)/shard_map/concatenate | solution.py:203
  36.7 0.0 copy-done
  36.7 0.8 copy_bitcast_fusion
  37.4 2.1 %collective-permute-done.4.ok_ref.ov_ref.oa_ref = bf16[4,2304,128]{2,1,0:T(8,128)(2,1)} collective-permute-done((bf16[4,2304,128]{2,1,0:T(8,128)(2,1)S(1)}, bf16[4,2304,128]{2,1,0:T(8,128)(2,1)}, u32[]{:S(2)}, u32[]{:S(2)}) %collective-permute-start.4) | collective-permute-done | bytes 2359328 | tf_op jit(solution)/shard_map/ppermute | solution.py:18
  39.5 0.0 copy-done.1
  39.5 28.0 %shard_map.65 = bf16[128,1024]{1,0:T(8,128)(2,1)} custom-call(s32[18]{0:T(128)} %pad_add_fusion.info_ref, bf16[1024,128]{1,0:T(8,128)(2,1)} %bitcast.21, bf16[4,2304,128]{2,1,0:T(8,128)(2,1)} %copy-done.1, bf16[4,2304,128]{2,1,0:T(8,128)(2,1)} %copy-done.1, bf16[4,2304,128]{2,1,0:T(8,128)(2,1)} %collective-permute-done.4.ok_ref.ov_ref.oa_ref, ...), custom_call_target="tpu_custom_call" | custom-call | tf_op jit(solution)/shard_map/pallas_call | solution.py:144
  67.5 15.7 %all_to_all.19 = bf16[8,16,1024]{2,1,0:T(8,128)(2,1)S(1)} all-to-all(bf16[8,16,1024]{2,1,0:T(8,128)(2,1)} %bitcast.22), channel_id=1, replica_groups=mesh['req'=64,'tp'=8] {'tp'}, dimensions={0} | all-to-all | bytes 524288 | tf_op jit(solution)/shard_map/all_to_all | solution.py:211
  83.2 0.7 copy.10
  (4 shorter events, 0.1 us)
Async XLA Ops:
  0.0 36.7 %copy-start = (bf16[128,1024]{1,0:T(8,128)(2,1)S(1)}, bf16[128,1024]{1,0:T(8,128)(2,1)}, u32[]{:S(2)}) copy-start(bf16[128,1024]{1,0:T(8,128)(2,1)} %param.6) | copy-start | bytes 786436
  1.9 30.7 %copy-start.2 = (bf16[2304,128]{1,0:T(8,128)(2,1)S(1)}, bf16[2304,128]{1,0:T(8,128)(2,1)}, u32[]{:S(2)}) copy-start(bf16[2304,128]{1,0:T(8,128)(2,1)} %shard_map.64) | copy-start | bytes 1769476
  1.9 17.5 %collective-permute-start.1 = (bf16[2304,128]{1,0:T(8,128)(2,1)}, bf16[2304,128]{1,0:T(8,128)(2,1)S(1)}, u32[]{:S(2)}, u32[]{:S(2)}) collective-permute-start(bf16[2304,128]{1,0:T(8,128)(2,1)} %shard_map.64), channel_id=1, source_target_pairs={{0,32},{8,40},{16,48},{24,56},{32,0},{40,8},{48,16},{56,24},{64,96... | collective-permute-start | bytes 1769480 | tf_op jit(solution)/shard_map/ppermute | solution.py:18
  5.9 17.0 %collective-permute-start = (bf16[2304,128]{1,0:T(8,128)(2,1)}, bf16[2304,128]{1,0:T(8,128)(2,1)S(1)}, u32[]{:S(2)}, u32[]{:S(2)}) collective-permute-start(bf16[2304,128]{1,0:T(8,128)(2,1)} %shard_map.64), channel_id=1, source_target_pairs={{0,16},{8,24},{16,0},{24,8},{32,48},{40,56},{48,32},{56,40},{64,80... | collective-permute-start | bytes 1769480 | tf_op jit(solution)/shard_map/ppermute | solution.py:18
  19.4 10.0 %collective-permute-start.2 = (bf16[1152,128]{1,0:T(8,128)(2,1)S(1)}, bf16[1152,128]{1,0:T(8,128)(2,1)S(1)}, u32[]{:S(2)}, u32[]{:S(2)}) collective-permute-start(bf16[1152,128]{1,0:T(8,128)(2,1)S(1)} %slice.8), channel_id=1, source_target_pairs={{0,16},{8,24},{16,0},{24,8},{32,48},{40,56},{48,32},{56,40},{64,80... | collective-permute-start | bytes 884744 | tf_op jit(solution)/shard_map/ppermute | solution.py:18
  22.9 9.7 %collective-permute-start.3 = (bf16[1152,128]{1,0:T(8,128)(2,1)S(1)}, bf16[1152,128]{1,0:T(8,128)(2,1)S(1)}, u32[]{:S(2)}, u32[]{:S(2)}) collective-permute-start(bf16[1152,128]{1,0:T(8,128)(2,1)S(1)} %slice.9), channel_id=1, source_target_pairs={{0,32},{8,40},{16,48},{24,56},{32,0},{40,8},{48,16},{56,24},{64,96... | collective-permute-start | bytes 884744 | tf_op jit(solution)/shard_map/ppermute | solution.py:18
  32.6 2.3 %copy-start.3 = (s32[8]{0:T(128)S(1)}, s32[8]{0:T(128)}, u32[]{:S(2)}) copy-start(s32[8]{0:T(128)} %param.11) | copy-start | bytes 100
  32.9 6.6 %copy-start.1 = (bf16[4,2304,128]{2,1,0:T(8,128)(2,1)}, bf16[4,2304,128]{2,1,0:T(8,128)(2,1)S(1)}, u32[]{:S(2)}) copy-start(bf16[4,2304,128]{2,1,0:T(8,128)(2,1)S(1)} %pad_maximum_fusion.lk_ref.lv_ref.la_ref) | copy-start | bytes 7077892
  32.9 6.6 %collective-permute-start.4 = (bf16[4,2304,128]{2,1,0:T(8,128)(2,1)S(1)}, bf16[4,2304,128]{2,1,0:T(8,128)(2,1)}, u32[]{:S(2)}, u32[]{:S(2)}) collective-permute-start(bf16[4,2304,128]{2,1,0:T(8,128)(2,1)S(1)} %pad_maximum_fusion.lk_ref.lv_ref.la_ref), channel_id=1, source_target_pairs={{0,8},{8,0},{16,24},{24,16},{32,40},{40,32},{48,56},{56,48},{64,72... | collective-permute-start | bytes 7077896 | tf_op jit(solution)/shard_map/ppermute | solution.py:18

commit v6 on v5

--- a/solution.py
+++ b/solution.py
@@ -11,6 +11,7 @@
 GROUP_DEVS = 8
 NEG_FILL = -1e30
 SCALE = 1.0 / math.sqrt(HEAD_SIZE)
+EXP2_SCALE = SCALE * math.log2(math.e)
 
 
 def exchange(value, axis, mask):
@@ -76,8 +77,8 @@
             s = jnp.where(allowed, s, NEG_FILL)
         m_prev = m_sc[...]
         m_new = jnp.maximum(m_prev, jnp.max(s, axis=1, keepdims=True))
-        alpha = jnp.exp((m_prev - m_new) * SCALE)
-        p = jnp.exp((s - m_new) * SCALE)
+        alpha = jnp.exp2((m_prev - m_new) * EXP2_SCALE)
+        p = jnp.exp2((s - m_new) * EXP2_SCALE)
         l_sc[...] = alpha * l_sc[...] + jnp.sum(p, axis=1, keepdims=True)
         pv = jnp.dot(p.astype(jnp.bfloat16), values, preferred_element_type=jnp.float32)
         acc_sc[...] = alpha * acc_sc[...] + pv

time: 84.4 us -> 83.6 us (level)
  no operation moved by 1% of the time
where the time goes in v6:
time: 83.6 us; the launch traced here: 83.1 us
  Pallas kernels  29.1 us (35%)
  waiting for transfers between devices  18.2 us (22%)
  starting transfers between devices  16.3 us (19%)
  blocking collectives  15.7 us (19%)
  local copies, waits for them, and re-layouts  2.09 us (2%)
  other arithmetic  1.54 us (2%)
    pallas_call x1, Pallas kernels, attention(): pl.pallas_call(attn_kernel, out_shape=jax.ShapeDtypeStruct((tokens, width...  27.2 us
    ppermute x5, waiting for transfers between devices, exchange(): return lax.ppermute(value, axis, pairs)  18.2 us
    ppermute x5, starting transfers between devices, exchange(): return lax.ppermute(value, axis, pairs)  16.3 us
    all_to_all x1, blocking collectives, body(): lax.all_to_all(attended, 'tp', split_axis=0, concat_axis=1, tiled=True)  15.7 us
    pallas_call x1, Pallas kernels, make_pack(): pl.pallas_call(pack_kernel, out_shape=jax.ShapeDtypeStruct((rows, HEAD_SI...  1.93 us
  transfers between devices with their start and end apart: 5, of which 4 were waited for; matrix products, arithmetic and copies ran while one was open for 3% of the time, Pallas kernels for 0%

profile of v6, /device:TPU:64, one launch (start us, length us, event | category | flops | bytes accessed | tf_op | source)
XLA Modules:
  0.0 83.1 jit_solution(11044049881590524870)
XLA Ops:
  0.0 0.0 copy-start
  0.0 1.9 %shard_map.64 = bf16[2304,128]{1,0:T(8,128)(2,1)} custom-call(bf16[1024,128]{1,0:T(8,128)(2,1)} %k_ref.1, bf16[1024,128]{1,0:T(8,128)(2,1)} %v_ref.1, bf16[128,128]{1,0:T(8,128)(2,1)} %sk_ref.1, bf16[128,128]{1,0:T(8,128)(2,1)} %sv_ref.1), custom_call_target="tpu_custom_call" | custom-call | tf_op jit(solution)/shard_map/pallas_call | solution.py:179
  1.9 0.0 copy-start.2
  1.9 3.9 %collective-permute-start.1 = (bf16[2304,128]{1,0:T(8,128)(2,1)}, bf16[2304,128]{1,0:T(8,128)(2,1)S(1)}, u32[]{:S(2)}, u32[]{:S(2)}) collective-permute-start(bf16[2304,128]{1,0:T(8,128)(2,1)} %shard_map.64), channel_id=1, source_target_pairs={{0,32},{8,40},{16,48},{24,56},{32,0},{40,8},{48,16},{56,24},{64,96... | collective-permute-start | bytes 1769480 | tf_op jit(solution)/shard_map/ppermute | solution.py:19
  5.9 3.4 %collective-permute-start = (bf16[2304,128]{1,0:T(8,128)(2,1)}, bf16[2304,128]{1,0:T(8,128)(2,1)S(1)}, u32[]{:S(2)}, u32[]{:S(2)}) collective-permute-start(bf16[2304,128]{1,0:T(8,128)(2,1)} %shard_map.64), channel_id=1, source_target_pairs={{0,16},{8,24},{16,0},{24,8},{32,48},{40,56},{48,32},{56,40},{64,80... | collective-permute-start | bytes 1769480 | tf_op jit(solution)/shard_map/ppermute | solution.py:19
  9.3 10.1 %collective-permute-done.1 = bf16[2304,128]{1,0:T(8,128)(2,1)S(1)} collective-permute-done((bf16[2304,128]{1,0:T(8,128)(2,1)}, bf16[2304,128]{1,0:T(8,128)(2,1)S(1)}, u32[]{:S(2)}, u32[]{:S(2)}) %collective-permute-start.1) | collective-permute-done | bytes 589856 | tf_op jit(solution)/shard_map/ppermute | solution.py:19
  19.4 3.4 %collective-permute-start.2 = (bf16[1152,128]{1,0:T(8,128)(2,1)S(1)}, bf16[1152,128]{1,0:T(8,128)(2,1)S(1)}, u32[]{:S(2)}, u32[]{:S(2)}) collective-permute-start(bf16[1152,128]{1,0:T(8,128)(2,1)S(1)} %slice.8), channel_id=1, source_target_pairs={{0,16},{8,24},{16,0},{24,8},{32,48},{40,56},{48,32},{56,40},{64,80... | collective-permute-start | bytes 884744 | tf_op jit(solution)/shard_map/ppermute | solution.py:19
  22.8 0.0 collective-permute-done
  22.9 3.6 %collective-permute-start.3 = (bf16[1152,128]{1,0:T(8,128)(2,1)S(1)}, bf16[1152,128]{1,0:T(8,128)(2,1)S(1)}, u32[]{:S(2)}, u32[]{:S(2)}) collective-permute-start(bf16[1152,128]{1,0:T(8,128)(2,1)S(1)} %slice.9), channel_id=1, source_target_pairs={{0,32},{8,40},{16,48},{24,56},{32,0},{40,8},{48,16},{56,24},{64,96... | collective-permute-start | bytes 884744 | tf_op jit(solution)/shard_map/ppermute | solution.py:19
  26.5 2.9 %collective-permute-done.2 = bf16[1152,128]{1,0:T(8,128)(2,1)S(1)} collective-permute-done((bf16[1152,128]{1,0:T(8,128)(2,1)S(1)}, bf16[1152,128]{1,0:T(8,128)(2,1)S(1)}, u32[]{:S(2)}, u32[]{:S(2)}) %collective-permute-start.2) | collective-permute-done | bytes 294944 | tf_op jit(solution)/shard_map/ppermute | solution.py:19
  29.4 3.2 %collective-permute-done.3 = bf16[1152,128]{1,0:T(8,128)(2,1)S(1)} collective-permute-done((bf16[1152,128]{1,0:T(8,128)(2,1)S(1)}, bf16[1152,128]{1,0:T(8,128)(2,1)S(1)}, u32[]{:S(2)}, u32[]{:S(2)}) %collective-permute-start.3) | collective-permute-done | bytes 294944 | tf_op jit(solution)/shard_map/ppermute | solution.py:19
  32.6 0.0 copy-done.2
  32.6 0.0 copy-start.3
  32.6 0.3 pad_maximum_fusion.lk_ref.lv_ref.la_ref
  32.9 0.0 copy-start.1
  32.9 1.9 %collective-permute-start.4 = (bf16[4,2304,128]{2,1,0:T(8,128)(2,1)S(1)}, bf16[4,2304,128]{2,1,0:T(8,128)(2,1)}, u32[]{:S(2)}, u32[]{:S(2)}) collective-permute-start(bf16[4,2304,128]{2,1,0:T(8,128)(2,1)S(1)} %pad_maximum_fusion.lk_ref.lv_ref.la_ref), channel_id=1, source_target_pairs={{0,8},{8,0},{16,24},{24,16},{32,40},{40,32},{48,56},{56,48},{64,72... | collective-permute-start | bytes 7077896 | tf_op jit(solution)/shard_map/ppermute | solution.py:19
  34.9 0.0 copy-done.3
  34.9 0.6 dynamic_slice.4
  35.5 1.2 %pad_add_fusion.info_ref = s32[18]{0:T(128)} fusion(s32[8]{0:T(128)S(1)} %get-tuple-element.5, s32[8]{0:T(128)S(1)} %get-tuple-element.6, s32[1]{0:T(128)} %bitcast, s32[1]{0:T(128)} %dynamic_slice.4), kind=kLoop, calls=%fused_computation.3 | loop fusion | flops 54 | bytes 144 | tf_op jit(solution)/shard_map/concatenate | solution.py:204
  36.7 0.0 copy-done
  36.7 0.8 copy_bitcast_fusion
  37.4 2.1 %collective-permute-done.4.ok_ref.ov_ref.oa_ref = bf16[4,2304,128]{2,1,0:T(8,128)(2,1)} collective-permute-done((bf16[4,2304,128]{2,1,0:T(8,128)(2,1)S(1)}, bf16[4,2304,128]{2,1,0:T(8,128)(2,1)}, u32[]{:S(2)}, u32[]{:S(2)}) %collective-permute-start.4) | collective-permute-done | bytes 2359328 | tf_op jit(solution)/shard_map/ppermute | solution.py:19
  39.5 0.0 copy-done.1
  39.5 27.2 %shard_map.65 = bf16[128,1024]{1,0:T(8,128)(2,1)} custom-call(s32[18]{0:T(128)} %pad_add_fusion.info_ref, bf16[1024,128]{1,0:T(8,128)(2,1)} %bitcast.21, bf16[4,2304,128]{2,1,0:T(8,128)(2,1)} %copy-done.1, bf16[4,2304,128]{2,1,0:T(8,128)(2,1)} %copy-done.1, bf16[4,2304,128]{2,1,0:T(8,128)(2,1)} %collective-permute-done.4.ok_ref.ov_ref.oa_ref, ...), custom_call_target="tpu_custom_call" | custom-call | tf_op jit(solution)/shard_map/pallas_call | solution.py:145
  66.7 15.7 %all_to_all.19 = bf16[8,16,1024]{2,1,0:T(8,128)(2,1)S(1)} all-to-all(bf16[8,16,1024]{2,1,0:T(8,128)(2,1)} %bitcast.22), channel_id=1, replica_groups=mesh['req'=64,'tp'=8] {'tp'}, dimensions={0} | all-to-all | bytes 524288 | tf_op jit(solution)/shard_map/all_to_all | solution.py:212
  82.4 0.7 copy.10
  (4 shorter events, 0.1 us)
Async XLA Ops:
  0.0 36.7 %copy-start = (bf16[128,1024]{1,0:T(8,128)(2,1)S(1)}, bf16[128,1024]{1,0:T(8,128)(2,1)}, u32[]{:S(2)}) copy-start(bf16[128,1024]{1,0:T(8,128)(2,1)} %param.6) | copy-start | bytes 786436
  1.9 30.7 %copy-start.2 = (bf16[2304,128]{1,0:T(8,128)(2,1)S(1)}, bf16[2304,128]{1,0:T(8,128)(2,1)}, u32[]{:S(2)}) copy-start(bf16[2304,128]{1,0:T(8,128)(2,1)} %shard_map.64) | copy-start | bytes 1769476
  1.9 17.5 %collective-permute-start.1 = (bf16[2304,128]{1,0:T(8,128)(2,1)}, bf16[2304,128]{1,0:T(8,128)(2,1)S(1)}, u32[]{:S(2)}, u32[]{:S(2)}) collective-permute-start(bf16[2304,128]{1,0:T(8,128)(2,1)} %shard_map.64), channel_id=1, source_target_pairs={{0,32},{8,40},{16,48},{24,56},{32,0},{40,8},{48,16},{56,24},{64,96... | collective-permute-start | bytes 1769480 | tf_op jit(solution)/shard_map/ppermute | solution.py:19
  5.9 17.0 %collective-permute-start = (bf16[2304,128]{1,0:T(8,128)(2,1)}, bf16[2304,128]{1,0:T(8,128)(2,1)S(1)}, u32[]{:S(2)}, u32[]{:S(2)}) collective-permute-start(bf16[2304,128]{1,0:T(8,128)(2,1)} %shard_map.64), channel_id=1, source_target_pairs={{0,16},{8,24},{16,0},{24,8},{32,48},{40,56},{48,32},{56,40},{64,80... | collective-permute-start | bytes 1769480 | tf_op jit(solution)/shard_map/ppermute | solution.py:19
  19.4 10.0 %collective-permute-start.2 = (bf16[1152,128]{1,0:T(8,128)(2,1)S(1)}, bf16[1152,128]{1,0:T(8,128)(2,1)S(1)}, u32[]{:S(2)}, u32[]{:S(2)}) collective-permute-start(bf16[1152,128]{1,0:T(8,128)(2,1)S(1)} %slice.8), channel_id=1, source_target_pairs={{0,16},{8,24},{16,0},{24,8},{32,48},{40,56},{48,32},{56,40},{64,80... | collective-permute-start | bytes 884744 | tf_op jit(solution)/shard_map/ppermute | solution.py:19
  22.9 9.7 %collective-permute-start.3 = (bf16[1152,128]{1,0:T(8,128)(2,1)S(1)}, bf16[1152,128]{1,0:T(8,128)(2,1)S(1)}, u32[]{:S(2)}, u32[]{:S(2)}) collective-permute-start(bf16[1152,128]{1,0:T(8,128)(2,1)S(1)} %slice.9), channel_id=1, source_target_pairs={{0,32},{8,40},{16,48},{24,56},{32,0},{40,8},{48,16},{56,24},{64,96... | collective-permute-start | bytes 884744 | tf_op jit(solution)/shard_map/ppermute | solution.py:19
  32.6 2.3 %copy-start.3 = (s32[8]{0:T(128)S(1)}, s32[8]{0:T(128)}, u32[]{:S(2)}) copy-start(s32[8]{0:T(128)} %param.11) | copy-start | bytes 100
  32.9 6.6 %copy-start.1 = (bf16[4,2304,128]{2,1,0:T(8,128)(2,1)}, bf16[4,2304,128]{2,1,0:T(8,128)(2,1)S(1)}, u32[]{:S(2)}) copy-start(bf16[4,2304,128]{2,1,0:T(8,128)(2,1)S(1)} %pad_maximum_fusion.lk_ref.lv_ref.la_ref) | copy-start | bytes 7077892
  32.9 6.6 %collective-permute-start.4 = (bf16[4,2304,128]{2,1,0:T(8,128)(2,1)S(1)}, bf16[4,2304,128]{2,1,0:T(8,128)(2,1)}, u32[]{:S(2)}, u32[]{:S(2)}) collective-permute-start(bf16[4,2304,128]{2,1,0:T(8,128)(2,1)S(1)} %pad_maximum_fusion.lk_ref.lv_ref.la_ref), channel_id=1, source_target_pairs={{0,8},{8,0},{16,24},{24,16},{32,40},{40,32},{48,56},{56,48},{64,72... | collective-permute-start | bytes 7077896 | tf_op jit(solution)/shard_map/ppermute | solution.py:19

commit v7 on v6

--- a/solution.py
+++ b/solution.py
@@ -77,11 +77,14 @@
             s = jnp.where(allowed, s, NEG_FILL)
         m_prev = m_sc[...]
         m_new = jnp.maximum(m_prev, jnp.max(s, axis=1, keepdims=True))
-        alpha = jnp.exp2((m_prev - m_new) * EXP2_SCALE)
-        p = jnp.exp2((s - m_new) * EXP2_SCALE)
-        l_sc[...] = alpha * l_sc[...] + jnp.sum(p, axis=1, keepdims=True)
-        pv = jnp.dot(p.astype(jnp.bfloat16), values, preferred_element_type=jnp.float32)
-        acc_sc[...] = alpha * acc_sc[...] + pv
+        m_scaled = m_new * EXP2_SCALE
+        alpha = jnp.exp2(m_prev * EXP2_SCALE - m_scaled)
+        p = jnp.exp2(s * EXP2_SCALE - m_scaled)
+        ones = (lax.broadcasted_iota(jnp.int32, values.shape, 1) == 0).astype(values.dtype)
+        wide = jnp.concatenate([values, ones], 1)
+        pv = jnp.dot(p.astype(jnp.bfloat16), wide, preferred_element_type=jnp.float32)
+        l_sc[...] = alpha * l_sc[...] + pv[:, HEAD_SIZE:HEAD_SIZE + 1]
+        acc_sc[...] = alpha * acc_sc[...] + pv[:, :HEAD_SIZE]
         m_sc[...] = m_new
 
     def slot(k_ref, v_ref):

time: 83.6 us -> 86.7 us (1.037)
  the two profiles are of different devices: /device:TPU:64 before, /device:TPU:1 now
where the time goes in v7:
time: 86.7 us; the launch traced here: 86 us
  Pallas kernels  32.6 us (38%)
  starting transfers between devices  22.6 us (26%)
  blocking collectives  14 us (16%)
  waiting for transfers between devices  13.1 us (15%)
  local copies, waits for them, and re-layouts  2.09 us (2%)
  other arithmetic  1.54 us (2%)
    pallas_call x1, Pallas kernels, attention(): pl.pallas_call(attn_kernel, out_shape=jax.ShapeDtypeStruct((tokens, width...  30.7 us
    ppermute x5, starting transfers between devices, exchange(): return lax.ppermute(value, axis, pairs)  22.6 us
    all_to_all x1, blocking collectives, body(): lax.all_to_all(attended, 'tp', split_axis=0, concat_axis=1, tiled=True)  14 us
    ppermute x5, waiting for transfers between devices, exchange(): return lax.ppermute(value, axis, pairs)  13.1 us
    pallas_call x1, Pallas kernels, make_pack(): pl.pallas_call(pack_kernel, out_shape=jax.ShapeDtypeStruct((rows, HEAD_SI...  1.93 us
  transfers between devices with their start and end apart: 5, of which 4 were waited for; matrix products, arithmetic and copies ran while one was open for 3% of the time, Pallas kernels for 0%

profile of v7, /device:TPU:1, one launch (start us, length us, event | category | flops | bytes accessed | tf_op | source)
XLA Modules:
  0.0 86.0 jit_solution(6387458556149782202)
XLA Ops:
  0.0 0.0 copy-start
  0.0 1.9 %shard_map.64 = bf16[2304,128]{1,0:T(8,128)(2,1)} custom-call(bf16[1024,128]{1,0:T(8,128)(2,1)} %k_ref.1, bf16[1024,128]{1,0:T(8,128)(2,1)} %v_ref.1, bf16[128,128]{1,0:T(8,128)(2,1)} %sk_ref.1, bf16[128,128]{1,0:T(8,128)(2,1)} %sv_ref.1), custom_call_target="tpu_custom_call" | custom-call | tf_op jit(solution)/shard_map/pallas_call | solution.py:182
  1.9 0.0 copy-start.2
  1.9 4.5 %collective-permute-start.1 = (bf16[2304,128]{1,0:T(8,128)(2,1)}, bf16[2304,128]{1,0:T(8,128)(2,1)S(1)}, u32[]{:S(2)}, u32[]{:S(2)}) collective-permute-start(bf16[2304,128]{1,0:T(8,128)(2,1)} %shard_map.64), channel_id=1, source_target_pairs={{0,32},{8,40},{16,48},{24,56},{32,0},{40,8},{48,16},{56,24},{64,96... | collective-permute-start | bytes 1769480 | tf_op jit(solution)/shard_map/ppermute | solution.py:19
  6.4 3.1 %collective-permute-start = (bf16[2304,128]{1,0:T(8,128)(2,1)}, bf16[2304,128]{1,0:T(8,128)(2,1)S(1)}, u32[]{:S(2)}, u32[]{:S(2)}) collective-permute-start(bf16[2304,128]{1,0:T(8,128)(2,1)} %shard_map.64), channel_id=1, source_target_pairs={{0,16},{8,24},{16,0},{24,8},{32,48},{40,56},{48,32},{56,40},{64,80... | collective-permute-start | bytes 1769480 | tf_op jit(solution)/shard_map/ppermute | solution.py:19
  9.6 5.7 %collective-permute-done.1 = bf16[2304,128]{1,0:T(8,128)(2,1)S(1)} collective-permute-done((bf16[2304,128]{1,0:T(8,128)(2,1)}, bf16[2304,128]{1,0:T(8,128)(2,1)S(1)}, u32[]{:S(2)}, u32[]{:S(2)}) %collective-permute-start.1) | collective-permute-done | bytes 589856 | tf_op jit(solution)/shard_map/ppermute | solution.py:19
  15.3 7.4 %collective-permute-start.2 = (bf16[1152,128]{1,0:T(8,128)(2,1)S(1)}, bf16[1152,128]{1,0:T(8,128)(2,1)S(1)}, u32[]{:S(2)}, u32[]{:S(2)}) collective-permute-start(bf16[1152,128]{1,0:T(8,128)(2,1)S(1)} %slice.8), channel_id=1, source_target_pairs={{0,16},{8,24},{16,0},{24,8},{32,48},{40,56},{48,32},{56,40},{64,80... | collective-permute-start | bytes 884744 | tf_op jit(solution)/shard_map/ppermute | solution.py:19
  22.7 0.0 collective-permute-done
  22.7 3.2 %collective-permute-start.3 = (bf16[1152,128]{1,0:T(8,128)(2,1)S(1)}, bf16[1152,128]{1,0:T(8,128)(2,1)S(1)}, u32[]{:S(2)}, u32[]{:S(2)}) collective-permute-start(bf16[1152,128]{1,0:T(8,128)(2,1)S(1)} %slice.9), channel_id=1, source_target_pairs={{0,32},{8,40},{16,48},{24,56},{32,0},{40,8},{48,16},{56,24},{64,96... | collective-permute-start | bytes 884744 | tf_op jit(solution)/shard_map/ppermute | solution.py:19
  25.9 2.3 %collective-permute-done.2 = bf16[1152,128]{1,0:T(8,128)(2,1)S(1)} collective-permute-done((bf16[1152,128]{1,0:T(8,128)(2,1)S(1)}, bf16[1152,128]{1,0:T(8,128)(2,1)S(1)}, u32[]{:S(2)}, u32[]{:S(2)}) %collective-permute-start.2) | collective-permute-done | bytes 294944 | tf_op jit(solution)/shard_map/ppermute | solution.py:19
  28.2 3.4 %collective-permute-done.3 = bf16[1152,128]{1,0:T(8,128)(2,1)S(1)} collective-permute-done((bf16[1152,128]{1,0:T(8,128)(2,1)S(1)}, bf16[1152,128]{1,0:T(8,128)(2,1)S(1)}, u32[]{:S(2)}, u32[]{:S(2)}) %collective-permute-start.3) | collective-permute-done | bytes 294944 | tf_op jit(solution)/shard_map/ppermute | solution.py:19
  31.6 0.0 copy-done.2
  31.6 0.0 copy-start.3
  31.6 0.3 pad_maximum_fusion.lk_ref.lv_ref.la_ref
  31.9 0.0 copy-start.1
  32.0 4.4 %collective-permute-start.4 = (bf16[4,2304,128]{2,1,0:T(8,128)(2,1)S(1)}, bf16[4,2304,128]{2,1,0:T(8,128)(2,1)}, u32[]{:S(2)}, u32[]{:S(2)}) collective-permute-start(bf16[4,2304,128]{2,1,0:T(8,128)(2,1)S(1)} %pad_maximum_fusion.lk_ref.lv_ref.la_ref), channel_id=1, source_target_pairs={{0,8},{8,0},{16,24},{24,16},{32,40},{40,32},{48,56},{56,48},{64,72... | collective-permute-start | bytes 7077896 | tf_op jit(solution)/shard_map/ppermute | solution.py:19
  36.4 0.0 copy-done.3
  36.4 0.6 dynamic_slice.4
  37.0 1.2 %pad_add_fusion.info_ref = s32[18]{0:T(128)} fusion(s32[8]{0:T(128)S(1)} %get-tuple-element.5, s32[8]{0:T(128)S(1)} %get-tuple-element.6, s32[1]{0:T(128)} %bitcast, s32[1]{0:T(128)} %dynamic_slice.4), kind=kLoop, calls=%fused_computation.3 | loop fusion | flops 54 | bytes 144 | tf_op jit(solution)/shard_map/concatenate | solution.py:207
  38.2 0.0 copy-done
  38.2 0.8 copy_bitcast_fusion
  38.9 1.7 %collective-permute-done.4.ok_ref.ov_ref.oa_ref = bf16[4,2304,128]{2,1,0:T(8,128)(2,1)} collective-permute-done((bf16[4,2304,128]{2,1,0:T(8,128)(2,1)S(1)}, bf16[4,2304,128]{2,1,0:T(8,128)(2,1)}, u32[]{:S(2)}, u32[]{:S(2)}) %collective-permute-start.4) | collective-permute-done | bytes 2359328 | tf_op jit(solution)/shard_map/ppermute | solution.py:19
  40.6 0.0 copy-done.1
  40.6 30.7 %shard_map.65 = bf16[128,1024]{1,0:T(8,128)(2,1)} custom-call(s32[18]{0:T(128)} %pad_add_fusion.info_ref, bf16[1024,128]{1,0:T(8,128)(2,1)} %bitcast.21, bf16[4,2304,128]{2,1,0:T(8,128)(2,1)} %copy-done.1, bf16[4,2304,128]{2,1,0:T(8,128)(2,1)} %copy-done.1, bf16[4,2304,128]{2,1,0:T(8,128)(2,1)} %collective-permute-done.4.ok_ref.ov_ref.oa_ref, ...), custom_call_target="tpu_custom_call" | custom-call | tf_op jit(solution)/shard_map/pallas_call | solution.py:148
  71.3 14.0 %all_to_all.19 = bf16[8,16,1024]{2,1,0:T(8,128)(2,1)S(1)} all-to-all(bf16[8,16,1024]{2,1,0:T(8,128)(2,1)} %bitcast.22), channel_id=1, replica_groups=mesh['req'=64,'tp'=8] {'tp'}, dimensions={0} | all-to-all | bytes 524288 | tf_op jit(solution)/shard_map/all_to_all | solution.py:215
  85.3 0.7 copy.10
  (4 shorter events, 0.1 us)
Async XLA Ops:
  0.0 38.2 %copy-start = (bf16[128,1024]{1,0:T(8,128)(2,1)S(1)}, bf16[128,1024]{1,0:T(8,128)(2,1)}, u32[]{:S(2)}) copy-start(bf16[128,1024]{1,0:T(8,128)(2,1)} %param.6) | copy-start | bytes 786436
  1.9 29.7 %copy-start.2 = (bf16[2304,128]{1,0:T(8,128)(2,1)S(1)}, bf16[2304,128]{1,0:T(8,128)(2,1)}, u32[]{:S(2)}) copy-start(bf16[2304,128]{1,0:T(8,128)(2,1)} %shard_map.64) | copy-start | bytes 1769476
  1.9 13.4 %collective-permute-start.1 = (bf16[2304,128]{1,0:T(8,128)(2,1)}, bf16[2304,128]{1,0:T(8,128)(2,1)S(1)}, u32[]{:S(2)}, u32[]{:S(2)}) collective-permute-start(bf16[2304,128]{1,0:T(8,128)(2,1)} %shard_map.64), channel_id=1, source_target_pairs={{0,32},{8,40},{16,48},{24,56},{32,0},{40,8},{48,16},{56,24},{64,96... | collective-permute-start | bytes 1769480 | tf_op jit(solution)/shard_map/ppermute | solution.py:19
  6.4 16.3 %collective-permute-start = (bf16[2304,128]{1,0:T(8,128)(2,1)}, bf16[2304,128]{1,0:T(8,128)(2,1)S(1)}, u32[]{:S(2)}, u32[]{:S(2)}) collective-permute-start(bf16[2304,128]{1,0:T(8,128)(2,1)} %shard_map.64), channel_id=1, source_target_pairs={{0,16},{8,24},{16,0},{24,8},{32,48},{40,56},{48,32},{56,40},{64,80... | collective-permute-start | bytes 1769480 | tf_op jit(solution)/shard_map/ppermute | solution.py:19
  15.3 12.9 %collective-permute-start.2 = (bf16[1152,128]{1,0:T(8,128)(2,1)S(1)}, bf16[1152,128]{1,0:T(8,128)(2,1)S(1)}, u32[]{:S(2)}, u32[]{:S(2)}) collective-permute-start(bf16[1152,128]{1,0:T(8,128)(2,1)S(1)} %slice.8), channel_id=1, source_target_pairs={{0,16},{8,24},{16,0},{24,8},{32,48},{40,56},{48,32},{56,40},{64,80... | collective-permute-start | bytes 884744 | tf_op jit(solution)/shard_map/ppermute | solution.py:19
  22.7 8.8 %collective-permute-start.3 = (bf16[1152,128]{1,0:T(8,128)(2,1)S(1)}, bf16[1152,128]{1,0:T(8,128)(2,1)S(1)}, u32[]{:S(2)}, u32[]{:S(2)}) collective-permute-start(bf16[1152,128]{1,0:T(8,128)(2,1)S(1)} %slice.9), channel_id=1, source_target_pairs={{0,32},{8,40},{16,48},{24,56},{32,0},{40,8},{48,16},{56,24},{64,96... | collective-permute-start | bytes 884744 | tf_op jit(solution)/shard_map/ppermute | solution.py:19
  31.6 4.8 %copy-start.3 = (s32[8]{0:T(128)S(1)}, s32[8]{0:T(128)}, u32[]{:S(2)}) copy-start(s32[8]{0:T(128)} %param.11) | copy-start | bytes 100
  31.9 8.7 %copy-start.1 = (bf16[4,2304,128]{2,1,0:T(8,128)(2,1)}, bf16[4,2304,128]{2,1,0:T(8,128)(2,1)S(1)}, u32[]{:S(2)}) copy-start(bf16[4,2304,128]{2,1,0:T(8,128)(2,1)S(1)} %pad_maximum_fusion.lk_ref.lv_ref.la_ref) | copy-start | bytes 7077892
  32.0 8.7 %collective-permute-start.4 = (bf16[4,2304,128]{2,1,0:T(8,128)(2,1)S(1)}, bf16[4,2304,128]{2,1,0:T(8,128)(2,1)}, u32[]{:S(2)}, u32[]{:S(2)}) collective-permute-start(bf16[4,2304,128]{2,1,0:T(8,128)(2,1)S(1)} %pad_maximum_fusion.lk_ref.lv_ref.la_ref), channel_id=1, source_target_pairs={{0,8},{8,0},{16,24},{24,16},{32,40},{40,32},{48,56},{56,48},{64,72... | collective-permute-start | bytes 7077896 | tf_op jit(solution)/shard_map/ppermute | solution.py:19

commit v8 on v6

v8 whole, which is shorter than its diff:
```python
import functools
import math

import jax
import jax.numpy as jnp
from jax import lax
from jax.experimental import pallas as pl
from jax.experimental.pallas import tpu as pltpu
from jax.sharding import PartitionSpec as P


HEAD_SIZE = 128
GROUP_DEVS = 8
NEG_FILL = -1e30
SCALE = 1.0 / math.sqrt(HEAD_SIZE)
EXP2_SCALE = SCALE * math.log2(math.e)


def exchange(value, axis, mask):
    pairs = [(source, source ^ mask) for source in range(lax.axis_size(axis))]
    return lax.ppermute(value, axis, pairs)


def span_copies(info_ref, local_any, other_any, sk_sc, sv_sc, sems, block, span):
    copies = []
    for j in range(local_any.shape[0]):
        for parity, source in ((0, local_any), (1, other_any)):
            slot = 2 * j + parity
            offset = pl.multiple_of(info_ref[2 + GROUP_DEVS + slot], span)
            for part, target in ((0, sk_sc), (1, sv_sc)):
                copies.append(
                    pltpu.make_async_copy(
                        source.at[j, pl.ds(2 * block + part * span, span), :],
                        target.at[pl.ds(offset, span), :],
                        sems.at[2 * slot + part],
                    )
                )
    return copies


def attn_kernel(plan, first, final, info_ref, q_ref, *refs):
    refs = list(refs)
    n_arrays = max(array for array, _ in plan) + 1
    state_in = [] if first else [refs.pop(0) for _ in range(3)]
    kv_refs = [(refs.pop(0), refs.pop(0)) for _ in range(n_arrays)]
    if final:
        la_ref, oa_ref, o_ref = refs.pop(0), refs.pop(0), refs.pop(0)
        m_sc, l_sc, acc_sc, sk_sc, sv_sc, sems = refs
    else:
        m_out, l_out, acc_out, m_sc, l_sc, acc_sc = refs
    step = pl.program_id(0)
    last = pl.num_programs(0) - 1
    rows = q_ref.shape[0]
    block = kv_refs[0][0].shape[0]
    length = info_ref[0]
    first_token = info_ref[1]

    @pl.when(step == 0)
    def _init():
        if final:
            span = sk_sc.shape[0] // GROUP_DEVS
            for copy in span_copies(info_ref, la_ref, oa_ref, sk_sc, sv_sc, sems, block, span):
                copy.start()
        if first:
            m_sc[...] = jnp.full(m_sc.shape, NEG_FILL, jnp.float32)
            l_sc[...] = jnp.zeros(l_sc.shape, jnp.float32)
            acc_sc[...] = jnp.zeros(acc_sc.shape, jnp.float32)
        else:
            m_sc[...] = state_in[0][...]
            l_sc[...] = state_in[1][...]
            acc_sc[...] = state_in[2][...]

    def process(keys, values, allowed):
        s = lax.dot_general(
            q_ref[...], keys, (((1,), (1,)), ((), ())), preferred_element_type=jnp.float32
        )
        if allowed is not None:
            s = jnp.where(allowed, s, NEG_FILL)
        m_prev = m_sc[...]
        m_new = jnp.maximum(m_prev, jnp.max(s, axis=1, keepdims=True))
        alpha = jnp.exp2((m_prev - m_new) * EXP2_SCALE)
        p = jnp.exp2((s - m_new) * EXP2_SCALE)
        l_sc[...] = alpha * l_sc[...] + jnp.sum(p, axis=1, keepdims=True)
        pv = jnp.dot(p.astype(jnp.bfloat16), values, preferred_element_type=jnp.float32)
        acc_sc[...] = alpha * acc_sc[...] + pv
        m_sc[...] = m_new

    def slot(k_ref, v_ref, start):
        full = start + block <= length
        partial = jnp.logical_and(start < length, jnp.logical_not(full))

        @pl.when(full)
        def _():
            process(k_ref[...], v_ref[...], None)

        @pl.when(partial)
        def _():
            key_rows = start + lax.broadcasted_iota(jnp.int32, (rows, block), 1)
            process(k_ref[...], v_ref[...], key_rows < length)

    for array in range(n_arrays):
        steps = [i for i, (a, _) in enumerate(plan) if a == array]
        uses = functools.reduce(jnp.logical_or, [step == i for i in steps])

        @pl.when(uses)
        def _():
            slot(kv_refs[array][0], kv_refs[array][1], info_ref[2 + 2 * GROUP_DEVS + step])

    if final:
        tokens = o_ref.shape[0]
        heads = rows // tokens

        @pl.when(step == last)
        def _span():
            span = sk_sc.shape[0] // GROUP_DEVS
            for copy in span_copies(info_ref, la_ref, oa_ref, sk_sc, sv_sc, sems, block, span):
                copy.wait()
            span_rows = sk_sc.shape[0]
            key_pos = lax.broadcasted_iota(jnp.int32, (rows, span_rows), 1)
            query_pos = first_token + lax.rem(
                lax.broadcasted_iota(jnp.int32, (rows, span_rows), 0), tokens
            )
            process(sk_sc[...], sv_sc[...], key_pos <= query_pos)
            for h in range(heads):
                rows_h = slice(h * tokens, (h + 1) * tokens)
                o_ref[:, h * HEAD_SIZE:(h + 1) * HEAD_SIZE] = (
                    acc_sc[rows_h, :] / l_sc[rows_h, :]
                ).astype(o_ref.dtype)
    else:
        @pl.when(step == last)
        def _save():
            m_out[...] = m_sc[...]
            l_out[...] = l_sc[...]
            acc_out[...] = acc_sc[...]


def index_map(plan, array):
    used = [(i, index) for i, (a, index) in enumerate(plan) if a == array]
    table = []
    for i in range(len(plan) + 1):
        before = [index for j, index in used if j <= i]
        table.append(before[-1] if before else used[0][1])

    def pick(k):
        result = table[-1]
        for i in reversed(range(len(table) - 1)):
            result = jnp.where(k == i, table[i], result)
        return result

    return pick


def attention(info, q_rows, arrays, plan, state, span_sources, tokens, block, span):
    rows = q_rows.shape[0]
    first = state is None
    final = span_sources is not None
    n_steps = len(plan) + (1 if final else 0)
    fixed = lambda k, info: (0, 0)
    in_specs = [pl.BlockSpec((rows, HEAD_SIZE), fixed)]
    operands = [info, q_rows]
    if not first:
        in_specs += [pl.BlockSpec((rows, 1), fixed), pl.BlockSpec((rows, 1), fixed),
                     pl.BlockSpec((rows, HEAD_SIZE), fixed)]
        operands += list(state)
    for array_id, array in enumerate(arrays):
        pick = index_map(plan, array_id)
        in_specs += [
            pl.BlockSpec((None, block, HEAD_SIZE), lambda k, info, pick=pick: (pick(k), 0, 0)),
            pl.BlockSpec((None, block, HEAD_SIZE), lambda k, info, pick=pick: (pick(k), 1, 0)),
        ]
        operands += [array, array]
    scratch = [
        pltpu.VMEM((rows, 1), jnp.float32),
        pltpu.VMEM((rows, 1), jnp.float32),
        pltpu.VMEM((rows, HEAD_SIZE), jnp.float32),
    ]
    if final:
        in_specs += [pl.BlockSpec(memory_space=pl.ANY), pl.BlockSpec(memory_space=pl.ANY)]
        operands += list(span_sources)
        heads = rows // tokens
        out_shape = jax.ShapeDtypeStruct((tokens, heads * HEAD_SIZE), jnp.bfloat16)
        out_specs = pl.BlockSpec((tokens, heads * HEAD_SIZE), fixed)
        scratch += [
            pltpu.VMEM((GROUP_DEVS * span, HEAD_SIZE), jnp.bfloat16),
            pltpu.VMEM((GROUP_DEVS * span, HEAD_SIZE), jnp.bfloat16),
            pltpu.SemaphoreType.DMA((4 * GROUP_DEVS,)),
        ]
    else:
        out_shape = (
            jax.ShapeDtypeStruct((rows, 1), jnp.float32),
            jax.ShapeDtypeStruct((rows, 1), jnp.float32),
            jax.ShapeDtypeStruct((rows, HEAD_SIZE), jnp.float32),
        )
        out_specs = (pl.BlockSpec((rows, 1), fixed), pl.BlockSpec((rows, 1), fixed),
                     pl.BlockSpec((rows, HEAD_SIZE), fixed))
    flops = 4 * rows * block * HEAD_SIZE * n_steps
    return pl.pallas_call(
        functools.partial(attn_kernel, plan, first, final),
        out_shape=out_shape,
        grid_spec=pltpu.PrefetchScalarGridSpec(
            num_scalar_prefetch=1,
            grid=(n_steps,),
            in_specs=in_specs,
            out_specs=out_specs,
            scratch_shapes=scratch,
        ),
        compiler_params=pltpu.CompilerParams(
            dimension_semantics=("arbitrary",), vmem_limit_bytes=56 * 1024 * 1024
        ),
        cost_estimate=pl.CostEstimate(
            flops=flops, transcendentals=rows * block * n_steps,
            bytes_accessed=n_steps * 2 * block * HEAD_SIZE * 2,
        ),
    )(*operands)


def pack_kernel(k_ref, v_ref, sk_ref, sv_ref, o_ref):
    rows = k_ref.shape[0]
    span = sk_ref.shape[0]
    o_ref[0:rows, :] = k_ref[...]
    o_ref[rows:2 * rows, :] = v_ref[...]
    o_ref[2 * rows:2 * rows + span, :] = sk_ref[...]
    o_ref[2 * rows + span:2 * rows + 2 * span, :] = sv_ref[...]


def make_pack(cache_k, cache_v, span_k, span_v):
    rows = 2 * cache_k.shape[0] + 2 * span_k.shape[0]
    return pl.pallas_call(
        pack_kernel,
        out_shape=jax.ShapeDtypeStruct((rows, HEAD_SIZE), cache_k.dtype),
    )(cache_k, cache_v, span_k, span_v)


def heads_as_rows(queries):
    tokens, width = queries.shape
    heads = width // HEAD_SIZE
    return queries.reshape(tokens, heads, HEAD_SIZE).transpose(1, 0, 2).reshape(heads * tokens, HEAD_SIZE)


def body(queries, span_rotated_keys, span_token_values, cache_keys, prompt_cache_values, lengths):
    tok_rows = queries.shape[0]
    cache_rows = cache_keys.shape[0]
    group_devs = lax.axis_size("req") // lengths.shape[0]
    assert group_devs == GROUP_DEVS
    device = lax.axis_index("req")
    position = device % GROUP_DEVS
    group_length = lax.dynamic_index_in_dim(lengths, device // GROUP_DEVS, 0, keepdims=False)

    pack = make_pack(cache_keys, prompt_cache_values, span_rotated_keys, span_token_values)
    span_rows = span_rotated_keys.shape[0]
    slot_pos = jnp.arange(GROUP_DEVS, dtype=jnp.int32) ^ position
    starts = slot_pos * cache_rows
    step_slots = jnp.asarray([0, 2, 4, 6, 1, 3, 5, 7], jnp.int32)
    info = jnp.concatenate(
        [
            jnp.stack([group_length, position * tok_rows]).astype(jnp.int32),
            starts.astype(jnp.int32),
            (slot_pos * span_rows).astype(jnp.int32),
            starts[step_slots].astype(jnp.int32),
        ]
    )
    info_b = jnp.concatenate([info[:2 + 2 * GROUP_DEVS], info[2 + 2 * GROUP_DEVS + 1:]])
    info_c = jnp.concatenate([info[:2 + 2 * GROUP_DEVS], info[2 + 2 * GROUP_DEVS + 3:]])
    q_rows = heads_as_rows(queries)
    size = (tok_rows, cache_rows, span_rows)

    half = pack.shape[0] // 2
    from_x = exchange(pack, "req", 2)
    from_z = exchange(pack, "req", 4)
    state = attention(info, q_rows, [pack[None]], [(0, 0)], None, None, *size)
    diag_lo = exchange(from_z[:half], "req", 2)
    diag_hi = exchange(from_x[half:], "req", 4)
    state = attention(
        info_b, q_rows, [from_x[None], from_z[None]], [(0, 0), (1, 0)], state, None, *size
    )
    diag = jnp.concatenate([diag_lo, diag_hi], 0)
    local = jnp.stack([pack, from_x, from_z, diag])
    other = exchange(local, "req", 1)
    plan = [(0, 3), (1, 0), (1, 1), (1, 2), (1, 3)]
    attended = attention(info_c, q_rows, [local, other], plan, state, (local, other), *size)
    return lax.all_to_all(attended, "tp", split_axis=0, concat_axis=1, tiled=True)


def solution(mesh):
    in_specs = (P("req", "tp"), P("req", "tp"), P("req", "tp"), P("req", "tp"), P("req", "tp"), P())
    out_specs = P(("req", "tp"), None)
    return jax.shard_map(body, mesh=mesh, in_specs=in_specs, out_specs=out_specs, check_vma=False)
```

time: 83.6 us -> 93.1 us (1.11)
  the two profiles are of different devices: /device:TPU:64 before, /device:TPU:128 now
where the time goes in v8:
time: 93.1 us; the launch traced here: 92.5 us
  Pallas kernels  36.7 us (39%)
  starting transfers between devices  16.3 us (18%)
  waiting for transfers between devices  16.2 us (17%)
  blocking collectives  15.9 us (17%)
  local copies, waits for them, and re-layouts  6.83 us (7%)
    pallas_call x3, Pallas kernels, attention(): pl.pallas_call(functools.partial(attn_kernel, plan, first, final), out_sh...  34.8 us
    ppermute x5, starting transfers between devices, exchange(): return lax.ppermute(value, axis, pairs)  16.3 us
    ppermute x5, waiting for transfers between devices, exchange(): return lax.ppermute(value, axis, pairs)  16.2 us
    all_to_all x1, blocking collectives, body(): lax.all_to_all(attended, 'tp', split_axis=0, concat_axis=1, tiled=True)  15.9 us
    pallas_call x1, Pallas kernels, make_pack(): pl.pallas_call(pack_kernel, out_shape=jax.ShapeDtypeStruct((rows, HEAD_SI...  1.94 us
  transfers between devices with their start and end apart: 5, of which 3 were waited for; matrix products, arithmetic and copies ran while one was open for 7% of the time, Pallas kernels for 16%

profile of v8, /device:TPU:128, one launch (start us, length us, event | category | flops | bytes accessed | tf_op | source)
XLA Modules:
  0.0 92.5 jit_solution(6106597945474169061)
XLA Ops:
  0.0 0.0 copy-start
  0.0 1.9 %shard_map.73 = bf16[2304,128]{1,0:T(8,128)(2,1)} custom-call(bf16[1024,128]{1,0:T(8,128)(2,1)} %k_ref.1, bf16[1024,128]{1,0:T(8,128)(2,1)} %v_ref.1, bf16[128,128]{1,0:T(8,128)(2,1)} %sk_ref.1, bf16[128,128]{1,0:T(8,128)(2,1)} %sv_ref.1), custom_call_target="tpu_custom_call" | custom-call | tf_op jit(solution)/shard_map/pallas_call | solution.py:228
  1.9 3.9 %collective-permute-start.1 = (bf16[2304,128]{1,0:T(8,128)(2,1)}, bf16[2304,128]{1,0:T(8,128)(2,1)S(1)}, u32[]{:S(2)}, u32[]{:S(2)}) collective-permute-start(bf16[2304,128]{1,0:T(8,128)(2,1)} %shard_map.73), channel_id=1, source_target_pairs={{0,32},{8,40},{16,48},{24,56},{32,0},{40,8},{48,16},{56,24},{64,96... | collective-permute-start | bytes 1769480 | tf_op jit(solution)/shard_map/ppermute | solution.py:21
  5.9 3.4 %collective-permute-start = (bf16[2304,128]{1,0:T(8,128)(2,1)}, bf16[2304,128]{1,0:T(8,128)(2,1)S(1)}, u32[]{:S(2)}, u32[]{:S(2)}) collective-permute-start(bf16[2304,128]{1,0:T(8,128)(2,1)} %shard_map.73), channel_id=1, source_target_pairs={{0,16},{8,24},{16,0},{24,8},{32,48},{40,56},{48,32},{56,40},{64,80... | collective-permute-start | bytes 1769480 | tf_op jit(solution)/shard_map/ppermute | solution.py:21
  9.3 10.1 %collective-permute-done.1 = bf16[2304,128]{1,0:T(8,128)(2,1)S(1)} collective-permute-done((bf16[2304,128]{1,0:T(8,128)(2,1)}, bf16[2304,128]{1,0:T(8,128)(2,1)S(1)}, u32[]{:S(2)}, u32[]{:S(2)}) %collective-permute-start.1) | collective-permute-done | bytes 589856 | tf_op jit(solution)/shard_map/ppermute | solution.py:21
  19.4 3.4 %collective-permute-start.2 = (bf16[1152,128]{1,0:T(8,128)(2,1)S(1)}, bf16[1152,128]{1,0:T(8,128)(2,1)S(1)}, u32[]{:S(2)}, u32[]{:S(2)}) collective-permute-start(bf16[1152,128]{1,0:T(8,128)(2,1)S(1)} %slice.21), channel_id=1, source_target_pairs={{0,16},{8,24},{16,0},{24,8},{32,48},{40,56},{48,32},{56,40},{64,80... | collective-permute-start | bytes 884744 | tf_op jit(solution)/shard_map/ppermute | solution.py:21
  22.9 0.0 collective-permute-done
  22.9 3.6 %collective-permute-start.3 = (bf16[1152,128]{1,0:T(8,128)(2,1)S(1)}, bf16[1152,128]{1,0:T(8,128)(2,1)S(1)}, u32[]{:S(2)}, u32[]{:S(2)}) collective-permute-start(bf16[1152,128]{1,0:T(8,128)(2,1)S(1)} %slice.22), channel_id=1, source_target_pairs={{0,32},{8,40},{16,48},{24,56},{32,0},{40,8},{48,16},{56,24},{64,96... | collective-permute-start | bytes 884744 | tf_op jit(solution)/shard_map/ppermute | solution.py:21
  26.6 2.9 %collective-permute-done.2 = bf16[1152,128]{1,0:T(8,128)(2,1)S(1)} collective-permute-done((bf16[1152,128]{1,0:T(8,128)(2,1)S(1)}, bf16[1152,128]{1,0:T(8,128)(2,1)S(1)}, u32[]{:S(2)}, u32[]{:S(2)}) %collective-permute-start.2) | collective-permute-done | bytes 294944 | tf_op jit(solution)/shard_map/ppermute | solution.py:21
  29.4 3.2 %collective-permute-done.3 = bf16[1152,128]{1,0:T(8,128)(2,1)S(1)} collective-permute-done((bf16[1152,128]{1,0:T(8,128)(2,1)S(1)}, bf16[1152,128]{1,0:T(8,128)(2,1)S(1)}, u32[]{:S(2)}, u32[]{:S(2)}) %collective-permute-start.3) | collective-permute-done | bytes 294944 | tf_op jit(solution)/shard_map/ppermute | solution.py:21
  32.6 0.0 copy-start.5
  32.7 0.0 copy-start.6
  32.7 0.3 pad_maximum_fusion.refs_3_.refs_4_.refs_7_
  33.0 0.0 copy-done.2
  33.0 0.0 copy-done.3
  33.0 0.0 copy-start.1
  33.0 1.9 %collective-permute-start.4 = (bf16[4,2304,128]{2,1,0:T(8,128)(2,1)S(1)}, bf16[4,2304,128]{2,1,0:T(8,128)(2,1)}, u32[]{:S(2)}, u32[]{:S(2)}) collective-permute-start(bf16[4,2304,128]{2,1,0:T(8,128)(2,1)S(1)} %pad_maximum_fusion.refs_3_.refs_4_.refs_7_), channel_id=1, source_target_pairs={{0,8},{8,0},{16,24},{24,16},{32,40},{40,32},{48,56},{56,48},{64,72... | collective-permute-start | bytes 7077896 | tf_op jit(solution)/shard_map/ppermute | solution.py:21
  35.0 0.6 gather_fusion
  35.6 0.1 slice.16
  35.7 0.1 slice.15
  35.8 0.0 copy-done.6
  35.8 0.6 dynamic_slice.4
  36.4 1.3 %concatenate.17.info_ref = s32[26]{0:T(128)} concatenate(s32[1]{0:T(128)} %dynamic_slice.4, s32[1]{0:T(128)} %bitcast, s32[8]{0:T(128)S(1)} %get-tuple-element.18, s32[8]{0:T(128)S(1)} %get-tuple-element.17, s32[8]{0:T(128)S(1)} %gather_fusion), dimensions={0} | concatenate | bytes 208 | tf_op jit(solution)/shard_map/concatenate | solution.py:254
  37.7 1.3 %concatenate.16.info_ref = s32[25]{0:T(128)} concatenate(s32[1]{0:T(128)} %dynamic_slice.4, s32[1]{0:T(128)} %bitcast, s32[8]{0:T(128)S(1)} %get-tuple-element.18, s32[8]{0:T(128)S(1)} %get-tuple-element.17, s32[7]{0:T(128)S(1)} %slice.16), dimensions={0} | concatenate | bytes 200 | tf_op jit(solution)/shard_map/concatenate | solution.py:262
  39.0 1.3 %concatenate.15.info_ref = s32[23]{0:T(128)} concatenate(s32[1]{0:T(128)} %dynamic_slice.4, s32[1]{0:T(128)} %bitcast, s32[8]{0:T(128)S(1)} %get-tuple-element.18, s32[8]{0:T(128)S(1)} %get-tuple-element.17, s32[5]{0:T(128)S(1)} %slice.15), dimensions={0} | concatenate | bytes 184 | tf_op jit(solution)/shard_map/concatenate | solution.py:263
  40.3 0.8 copy_bitcast_fusion
  41.0 5.8 %shard_map.74 = (f32[1024,1]{1,0:T(8,128)}, f32[1024,1]{1,0:T(8,128)}, f32[1024,128]{1,0:T(8,128)}) custom-call(s32[26]{0:T(128)} %concatenate.17.info_ref, bf16[1024,128]{1,0:T(8,128)(2,1)} %bitcast.24, bf16[1,2304,128]{2,1,0:T(8,128)(2,1)} %bitcast.27, bf16[1,2304,128]{2,1,0:T(8,128)(2,1)} %bitcast.28), custom_call_target="tpu_custom_call" | custom-call | flops 536870912 | bytes 524288 | tf_op jit(solution)/shard_map/pallas_call | solution.py:197
  46.8 8.9 %shard_map.75 = (f32[1024,1]{1,0:T(8,128)}, f32[1024,1]{1,0:T(8,128)}, f32[1024,128]{1,0:T(8,128)}) custom-call(s32[25]{0:T(128)} %concatenate.16.info_ref, bf16[1024,128]{1,0:T(8,128)(2,1)} %bitcast.25, f32[1024,1]{1,0:T(8,128)} %get-tuple-element.11.refs_0_, f32[1024,1]{1,0:T(8,128)} %get-tuple-element.12.refs_1_, f32[1024,128]{1,0:T(8,128)} %get-tuple-element.13.refs_2_, ...), custom_call_target="tpu_custom_call" | custom-call | flops 1073741824 | bytes 1048576 | tf_op jit(solution)/shard_map/pallas_call | solution.py:197
  55.7 0.0 collective-permute-done.4.refs_5_.refs_6_.refs_8_
  55.7 20.1 %shard_map.76 = bf16[128,1024]{1,0:T(8,128)(2,1)} custom-call(s32[23]{0:T(128)} %concatenate.15.info_ref, bf16[1024,128]{1,0:T(8,128)(2,1)} %bitcast.26, f32[1024,1]{1,0:T(8,128)} %get-tuple-element.14.refs_0_, f32[1024,1]{1,0:T(8,128)} %get-tuple-element.15.refs_1_, f32[1024,128]{1,0:T(8,128)} %get-tuple-element.16.refs_2_, ...), custom_call_target="tpu_custom_call" | custom-call | flops 3221225472 | bytes 3145728 | tf_op jit(solution)/shard_map/pallas_call | solution.py:197
  75.8 15.9 %all_to_all.19 = bf16[8,16,1024]{2,1,0:T(8,128)(2,1)S(1)} all-to-all(bf16[8,16,1024]{2,1,0:T(8,128)(2,1)} %bitcast.30), channel_id=1, replica_groups=mesh['req'=64,'tp'=8] {'tp'}, dimensions={0} | all-to-all | bytes 524288 | tf_op jit(solution)/shard_map/all_to_all | solution.py:281
  91.8 0.7 copy.13
  (12 shorter events, 0.1 us)
Async XLA Ops:
  0.0 40.3 %copy-start = (bf16[128,1024]{1,0:T(8,128)(2,1)S(1)}, bf16[128,1024]{1,0:T(8,128)(2,1)}, u32[]{:S(2)}) copy-start(bf16[128,1024]{1,0:T(8,128)(2,1)} %param.7) | copy-start | bytes 786436
  1.9 30.7 %copy-start.4 = (bf16[2304,128]{1,0:T(8,128)(2,1)S(1)}, bf16[2304,128]{1,0:T(8,128)(2,1)}, u32[]{:S(2)}) copy-start(bf16[2304,128]{1,0:T(8,128)(2,1)} %shard_map.73) | copy-start | bytes 1769476
  1.9 17.5 %collective-permute-start.1 = (bf16[2304,128]{1,0:T(8,128)(2,1)}, bf16[2304,128]{1,0:T(8,128)(2,1)S(1)}, u32[]{:S(2)}, u32[]{:S(2)}) collective-permute-start(bf16[2304,128]{1,0:T(8,128)(2,1)} %shard_map.73), channel_id=1, source_target_pairs={{0,32},{8,40},{16,48},{24,56},{32,0},{40,8},{48,16},{56,24},{64,96... | collective-permute-start | bytes 1769480 | tf_op jit(solution)/shard_map/ppermute | solution.py:21
  5.9 17.0 %collective-permute-start = (bf16[2304,128]{1,0:T(8,128)(2,1)}, bf16[2304,128]{1,0:T(8,128)(2,1)S(1)}, u32[]{:S(2)}, u32[]{:S(2)}) collective-permute-start(bf16[2304,128]{1,0:T(8,128)(2,1)} %shard_map.73), channel_id=1, source_target_pairs={{0,16},{8,24},{16,0},{24,8},{32,48},{40,56},{48,32},{56,40},{64,80... | collective-permute-start | bytes 1769480 | tf_op jit(solution)/shard_map/ppermute | solution.py:21
  19.4 13.6 %copy-start.2 = (bf16[2304,128]{1,0:T(8,128)(2,1)}, bf16[2304,128]{1,0:T(8,128)(2,1)S(1)}, u32[]{:S(2)}) copy-start(bf16[2304,128]{1,0:T(8,128)(2,1)S(1)} %collective-permute-done.1) | copy-start | bytes 1769476
  19.4 10.0 %collective-permute-start.2 = (bf16[1152,128]{1,0:T(8,128)(2,1)S(1)}, bf16[1152,128]{1,0:T(8,128)(2,1)S(1)}, u32[]{:S(2)}, u32[]{:S(2)}) collective-permute-start(bf16[1152,128]{1,0:T(8,128)(2,1)S(1)} %slice.21), channel_id=1, source_target_pairs={{0,16},{8,24},{16,0},{24,8},{32,48},{40,56},{48,32},{56,40},{64,80... | collective-permute-start | bytes 884744 | tf_op jit(solution)/shard_map/ppermute | solution.py:21
  22.9 10.1 %copy-start.3 = (bf16[2304,128]{1,0:T(8,128)(2,1)}, bf16[2304,128]{1,0:T(8,128)(2,1)S(1)}, u32[]{:S(2)}) copy-start(bf16[2304,128]{1,0:T(8,128)(2,1)S(1)} %collective-permute-done) | copy-start | bytes 1769476
  22.9 9.7 %collective-permute-start.3 = (bf16[1152,128]{1,0:T(8,128)(2,1)S(1)}, bf16[1152,128]{1,0:T(8,128)(2,1)S(1)}, u32[]{:S(2)}, u32[]{:S(2)}) collective-permute-start(bf16[1152,128]{1,0:T(8,128)(2,1)S(1)} %slice.22), channel_id=1, source_target_pairs={{0,32},{8,40},{16,48},{24,56},{32,0},{40,8},{48,16},{56,24},{64,96... | collective-permute-start | bytes 884744 | tf_op jit(solution)/shard_map/ppermute | solution.py:21
  32.6 2.3 %copy-start.5 = (s32[8]{0:T(128)S(1)}, s32[8]{0:T(128)}, u32[]{:S(2)}) copy-start(s32[8]{0:T(128)} %constant.50) | copy-start | bytes 100
  32.7 3.1 %copy-start.6 = (s32[8]{0:T(128)S(1)}, s32[8]{0:T(128)}, u32[]{:S(2)}) copy-start(s32[8]{0:T(128)} %param.12) | copy-start | bytes 100
  33.0 22.7 %copy-start.1 = (bf16[4,2304,128]{2,1,0:T(8,128)(2,1)}, bf16[4,2304,128]{2,1,0:T(8,128)(2,1)S(1)}, u32[]{:S(2)}) copy-start(bf16[4,2304,128]{2,1,0:T(8,128)(2,1)S(1)} %pad_maximum_fusion.refs_3_.refs_4_.refs_7_) | copy-start | bytes 7077892
  33.0 22.7 %collective-permute-start.4 = (bf16[4,2304,128]{2,1,0:T(8,128)(2,1)S(1)}, bf16[4,2304,128]{2,1,0:T(8,128)(2,1)}, u32[]{:S(2)}, u32[]{:S(2)}) collective-permute-start(bf16[4,2304,128]{2,1,0:T(8,128)(2,1)S(1)} %pad_maximum_fusion.refs_3_.refs_4_.refs_7_), channel_id=1, source_target_pairs={{0,8},{8,0},{16,24},{24,16},{32,40},{40,32},{48,56},{56,48},{64,72... | collective-permute-start | bytes 7077896 | tf_op jit(solution)/shard_map/ppermute | solution.py:21

commit v9 on v8

--- a/solution.py
+++ b/solution.py
@@ -11,6 +11,7 @@
 
 HEAD_SIZE = 128
 GROUP_DEVS = 8
+STEP_SLOTS = (0, 2, 4, 6, 1, 3, 5, 7)
 NEG_FILL = -1e30
 SCALE = 1.0 / math.sqrt(HEAD_SIZE)
 EXP2_SCALE = SCALE * math.log2(math.e)
@@ -38,7 +39,7 @@
     return copies
 
 
-def attn_kernel(plan, first, final, info_ref, q_ref, *refs):
+def attn_kernel(plan, offset, first, final, info_ref, q_ref, *refs):
     refs = list(refs)
     n_arrays = max(array for array, _ in plan) + 1
     state_in = [] if first else [refs.pop(0) for _ in range(3)]
@@ -104,7 +105,7 @@
 
         @pl.when(uses)
         def _():
-            slot(kv_refs[array][0], kv_refs[array][1], info_ref[2 + 2 * GROUP_DEVS + step])
+            slot(kv_refs[array][0], kv_refs[array][1], info_ref[2 + 2 * GROUP_DEVS + offset + step])
 
     if final:
         tokens = o_ref.shape[0]
@@ -150,7 +151,7 @@
     return pick
 
 
-def attention(info, q_rows, arrays, plan, state, span_sources, tokens, block, span):
+def attention(info, offset, q_rows, arrays, plan, state, span_sources, tokens, block, span):
     rows = q_rows.shape[0]
     first = state is None
     final = span_sources is not None
@@ -195,7 +196,7 @@
                      pl.BlockSpec((rows, HEAD_SIZE), fixed))
     flops = 4 * rows * block * HEAD_SIZE * n_steps
     return pl.pallas_call(
-        functools.partial(attn_kernel, plan, first, final),
+        functools.partial(attn_kernel, plan, offset, first, final),
         out_shape=out_shape,
         grid_spec=pltpu.PrefetchScalarGridSpec(
             num_scalar_prefetch=1,
@@ -249,35 +250,32 @@
     pack = make_pack(cache_keys, prompt_cache_values, span_rotated_keys, span_token_values)
     span_rows = span_rotated_keys.shape[0]
     slot_pos = jnp.arange(GROUP_DEVS, dtype=jnp.int32) ^ position
-    starts = slot_pos * cache_rows
-    step_slots = jnp.asarray([0, 2, 4, 6, 1, 3, 5, 7], jnp.int32)
+    step_pos = jnp.asarray(STEP_SLOTS, jnp.int32) ^ position
     info = jnp.concatenate(
         [
             jnp.stack([group_length, position * tok_rows]).astype(jnp.int32),
-            starts.astype(jnp.int32),
+            (slot_pos * cache_rows).astype(jnp.int32),
             (slot_pos * span_rows).astype(jnp.int32),
-            starts[step_slots].astype(jnp.int32),
+            (step_pos * cache_rows).astype(jnp.int32),
         ]
     )
-    info_b = jnp.concatenate([info[:2 + 2 * GROUP_DEVS], info[2 + 2 * GROUP_DEVS + 1:]])
-    info_c = jnp.concatenate([info[:2 + 2 * GROUP_DEVS], info[2 + 2 * GROUP_DEVS + 3:]])
     q_rows = heads_as_rows(queries)
     size = (tok_rows, cache_rows, span_rows)
 
     half = pack.shape[0] // 2
     from_x = exchange(pack, "req", 2)
     from_z = exchange(pack, "req", 4)
-    state = attention(info, q_rows, [pack[None]], [(0, 0)], None, None, *size)
+    state = attention(info, 0, q_rows, [pack[None]], [(0, 0)], None, None, *size)
     diag_lo = exchange(from_z[:half], "req", 2)
     diag_hi = exchange(from_x[half:], "req", 4)
     state = attention(
-        info_b, q_rows, [from_x[None], from_z[None]], [(0, 0), (1, 0)], state, None, *size
+        info, 1, q_rows, [from_x[None], from_z[None]], [(0, 0), (1, 0)], state, None, *size
     )
     diag = jnp.concatenate([diag_lo, diag_hi], 0)
     local = jnp.stack([pack, from_x, from_z, diag])
     other = exchange(local, "req", 1)
     plan = [(0, 3), (1, 0), (1, 1), (1, 2), (1, 3)]
-    attended = attention(info_c, q_rows, [local, other], plan, state, (local, other), *size)
+    attended = attention(info, 3, q_rows, [local, other], plan, state, (local, other), *size)
     return lax.all_to_all(attended, "tp", split_axis=0, concat_axis=1, tiled=True)
 
 

time: 93.1 us -> 89.6 us (0.962)
  local copies, waits for them, and re-layouts: 6.83 us -> 3.41 us
    concatenate x2 -> x0, local copies, waits for them, and re-layouts: 2.59 us -> none  [the longest x1 1.31 us: body(): jnp.concatenate([info[:2 + 2 * GROUP_DEVS], info[2 + 2 * GROUP_DEVS + 1:]])]
  transfers between devices with their start and end apart: 5 -> 5, of which waited for: 3 -> 3; matrix products, arithmetic and copies ran while one was open for 7% -> 3% of each run, Pallas kernels for 16% -> 16%
where the time goes in v9:
time: 89.6 us; the launch traced here: 89.1 us
  Pallas kernels  36.7 us (41%)
  starting transfers between devices  16.3 us (18%)
  waiting for transfers between devices  16.2 us (18%)
  blocking collectives  15.9 us (18%)
  local copies, waits for them, and re-layouts  3.41 us (4%)
    pallas_call x3, Pallas kernels, attention(): pl.pallas_call(functools.partial(attn_kernel, plan, offset, first, final)...  34.8 us
    ppermute x5, starting transfers between devices, exchange(): return lax.ppermute(value, axis, pairs)  16.3 us
    ppermute x5, waiting for transfers between devices, exchange(): return lax.ppermute(value, axis, pairs)  16.2 us
    all_to_all x1, blocking collectives, body(): lax.all_to_all(attended, 'tp', split_axis=0, concat_axis=1, tiled=True)  15.9 us
    pallas_call x1, Pallas kernels, make_pack(): pl.pallas_call(pack_kernel, out_shape=jax.ShapeDtypeStruct((rows, HEAD_SI...  1.94 us
  transfers between devices with their start and end apart: 5, of which 3 were waited for; matrix products, arithmetic and copies ran while one was open for 3% of the time, Pallas kernels for 16%

profile of v9, /device:TPU:128, one launch (start us, length us, event | category | flops | bytes accessed | tf_op | source)
XLA Modules:
  0.0 89.1 jit_solution(12535455232550277579)
XLA Ops:
  0.0 0.0 copy-start
  0.0 1.9 %shard_map.73 = bf16[2304,128]{1,0:T(8,128)(2,1)} custom-call(bf16[1024,128]{1,0:T(8,128)(2,1)} %k_ref.1, bf16[1024,128]{1,0:T(8,128)(2,1)} %v_ref.1, bf16[128,128]{1,0:T(8,128)(2,1)} %sk_ref.1, bf16[128,128]{1,0:T(8,128)(2,1)} %sv_ref.1), custom_call_target="tpu_custom_call" | custom-call | tf_op jit(solution)/shard_map/pallas_call | solution.py:229
  1.9 3.9 %collective-permute-start.1 = (bf16[2304,128]{1,0:T(8,128)(2,1)}, bf16[2304,128]{1,0:T(8,128)(2,1)S(1)}, u32[]{:S(2)}, u32[]{:S(2)}) collective-permute-start(bf16[2304,128]{1,0:T(8,128)(2,1)} %shard_map.73), channel_id=1, source_target_pairs={{0,32},{8,40},{16,48},{24,56},{32,0},{40,8},{48,16},{56,24},{64,96... | collective-permute-start | bytes 1769480 | tf_op jit(solution)/shard_map/ppermute | solution.py:22
  5.9 3.4 %collective-permute-start = (bf16[2304,128]{1,0:T(8,128)(2,1)}, bf16[2304,128]{1,0:T(8,128)(2,1)S(1)}, u32[]{:S(2)}, u32[]{:S(2)}) collective-permute-start(bf16[2304,128]{1,0:T(8,128)(2,1)} %shard_map.73), channel_id=1, source_target_pairs={{0,16},{8,24},{16,0},{24,8},{32,48},{40,56},{48,32},{56,40},{64,80... | collective-permute-start | bytes 1769480 | tf_op jit(solution)/shard_map/ppermute | solution.py:22
  9.3 10.1 %collective-permute-done.1 = bf16[2304,128]{1,0:T(8,128)(2,1)S(1)} collective-permute-done((bf16[2304,128]{1,0:T(8,128)(2,1)}, bf16[2304,128]{1,0:T(8,128)(2,1)S(1)}, u32[]{:S(2)}, u32[]{:S(2)}) %collective-permute-start.1) | collective-permute-done | bytes 589856 | tf_op jit(solution)/shard_map/ppermute | solution.py:22
  19.4 3.4 %collective-permute-start.2 = (bf16[1152,128]{1,0:T(8,128)(2,1)S(1)}, bf16[1152,128]{1,0:T(8,128)(2,1)S(1)}, u32[]{:S(2)}, u32[]{:S(2)}) collective-permute-start(bf16[1152,128]{1,0:T(8,128)(2,1)S(1)} %slice.8), channel_id=1, source_target_pairs={{0,16},{8,24},{16,0},{24,8},{32,48},{40,56},{48,32},{56,40},{64,80... | collective-permute-start | bytes 884744 | tf_op jit(solution)/shard_map/ppermute | solution.py:22
  22.9 0.0 collective-permute-done
  22.9 0.0 copy-start.3
  22.9 3.6 %collective-permute-start.3 = (bf16[1152,128]{1,0:T(8,128)(2,1)S(1)}, bf16[1152,128]{1,0:T(8,128)(2,1)S(1)}, u32[]{:S(2)}, u32[]{:S(2)}) collective-permute-start(bf16[1152,128]{1,0:T(8,128)(2,1)S(1)} %slice.9), channel_id=1, source_target_pairs={{0,32},{8,40},{16,48},{24,56},{32,0},{40,8},{48,16},{56,24},{64,96... | collective-permute-start | bytes 884744 | tf_op jit(solution)/shard_map/ppermute | solution.py:22
  26.6 2.9 %collective-permute-done.2 = bf16[1152,128]{1,0:T(8,128)(2,1)S(1)} collective-permute-done((bf16[1152,128]{1,0:T(8,128)(2,1)S(1)}, bf16[1152,128]{1,0:T(8,128)(2,1)S(1)}, u32[]{:S(2)}, u32[]{:S(2)}) %collective-permute-start.2) | collective-permute-done | bytes 294944 | tf_op jit(solution)/shard_map/ppermute | solution.py:22
  29.4 3.2 %collective-permute-done.3 = bf16[1152,128]{1,0:T(8,128)(2,1)S(1)} collective-permute-done((bf16[1152,128]{1,0:T(8,128)(2,1)S(1)}, bf16[1152,128]{1,0:T(8,128)(2,1)S(1)}, u32[]{:S(2)}, u32[]{:S(2)}) %collective-permute-start.3) | collective-permute-done | bytes 294944 | tf_op jit(solution)/shard_map/ppermute | solution.py:22
  32.6 0.0 copy-done.4
  32.6 0.0 copy-start.6
  32.7 0.0 copy-start.5
  32.7 0.3 pad_maximum_fusion.refs_3_.refs_4_.refs_7_
  33.0 0.0 copy-done.2
  33.0 0.0 copy-done.3
  33.0 0.0 copy-start.1
  33.0 1.9 %collective-permute-start.4 = (bf16[4,2304,128]{2,1,0:T(8,128)(2,1)S(1)}, bf16[4,2304,128]{2,1,0:T(8,128)(2,1)}, u32[]{:S(2)}, u32[]{:S(2)}) collective-permute-start(bf16[4,2304,128]{2,1,0:T(8,128)(2,1)S(1)} %pad_maximum_fusion.refs_3_.refs_4_.refs_7_), channel_id=1, source_target_pairs={{0,8},{8,0},{16,24},{24,16},{32,40},{40,32},{48,56},{56,48},{64,72... | collective-permute-start | bytes 7077896 | tf_op jit(solution)/shard_map/ppermute | solution.py:22
  35.0 0.0 copy-done.6
  35.0 0.6 dynamic_slice.4
  35.6 0.0 copy-done.5
  35.6 1.3 %concatenate.6.info_ref = s32[26]{0:T(128)} concatenate(s32[1]{0:T(128)} %dynamic_slice.4, s32[1]{0:T(128)} %bitcast, s32[8]{0:T(128)S(1)} %fusion.1, s32[8]{0:T(128)S(1)} %get-tuple-element.18, s32[8]{0:T(128)S(1)} %get-tuple-element.17), dimensions={0} | concatenate | bytes 208 | tf_op jit(solution)/shard_map/concatenate | solution.py:254
  36.8 0.0 copy-done
  36.8 0.8 copy_bitcast_fusion
  37.6 5.8 %shard_map.74 = (f32[1024,1]{1,0:T(8,128)}, f32[1024,1]{1,0:T(8,128)}, f32[1024,128]{1,0:T(8,128)}) custom-call(s32[26]{0:T(128)} %concatenate.6.info_ref, bf16[1024,128]{1,0:T(8,128)(2,1)} %bitcast.24, bf16[1,2304,128]{2,1,0:T(8,128)(2,1)} %bitcast.27, bf16[1,2304,128]{2,1,0:T(8,128)(2,1)} %bitcast.28), custom_call_target="tpu_custom_call" | custom-call | flops 536870912 | bytes 524288 | tf_op jit(solution)/shard_map/pallas_call | solution.py:198
  43.4 8.9 %shard_map.75 = (f32[1024,1]{1,0:T(8,128)}, f32[1024,1]{1,0:T(8,128)}, f32[1024,128]{1,0:T(8,128)}) custom-call(s32[26]{0:T(128)} %concatenate.6.info_ref, bf16[1024,128]{1,0:T(8,128)(2,1)} %bitcast.25, f32[1024,1]{1,0:T(8,128)} %get-tuple-element.11.refs_0_, f32[1024,1]{1,0:T(8,128)} %get-tuple-element.12.refs_1_, f32[1024,128]{1,0:T(8,128)} %get-tuple-element.13.refs_2_, ...), custom_call_target="tpu_custom_call" | custom-call | flops 1073741824 | bytes 1048576 | tf_op jit(solution)/shard_map/pallas_call | solution.py:198
  52.3 0.0 copy-done.1
  52.3 0.0 collective-permute-done.4.refs_5_.refs_6_.refs_8_
  52.3 20.1 %shard_map.76 = bf16[128,1024]{1,0:T(8,128)(2,1)} custom-call(s32[26]{0:T(128)} %concatenate.6.info_ref, bf16[1024,128]{1,0:T(8,128)(2,1)} %bitcast.26, f32[1024,1]{1,0:T(8,128)} %get-tuple-element.14.refs_0_, f32[1024,1]{1,0:T(8,128)} %get-tuple-element.15.refs_1_, f32[1024,128]{1,0:T(8,128)} %get-tuple-element.16.refs_2_, bf16[4,2304,128]{2,1,0:T(8,128)(2,1)} %copy-done.1, ...), custom_call_target="tpu_custom_call" | custom-call | flops 3221225472 | bytes 3145728 | tf_op jit(solution)/shard_map/pallas_call | solution.py:198
  72.4 15.9 %all_to_all.19 = bf16[8,16,1024]{2,1,0:T(8,128)(2,1)S(1)} all-to-all(bf16[8,16,1024]{2,1,0:T(8,128)(2,1)} %bitcast.30), channel_id=1, replica_groups=mesh['req'=64,'tp'=8] {'tp'}, dimensions={0} | all-to-all | bytes 524288 | tf_op jit(solution)/shard_map/all_to_all | solution.py:279
  88.3 0.7 copy.11
  (7 shorter events, 0.1 us)
Async XLA Ops:
  0.0 36.8 %copy-start = (bf16[128,1024]{1,0:T(8,128)(2,1)S(1)}, bf16[128,1024]{1,0:T(8,128)(2,1)}, u32[]{:S(2)}) copy-start(bf16[128,1024]{1,0:T(8,128)(2,1)} %param.7) | copy-start | bytes 786436
  1.9 30.7 %copy-start.4 = (bf16[2304,128]{1,0:T(8,128)(2,1)S(1)}, bf16[2304,128]{1,0:T(8,128)(2,1)}, u32[]{:S(2)}) copy-start(bf16[2304,128]{1,0:T(8,128)(2,1)} %shard_map.73) | copy-start | bytes 1769476
  1.9 17.5 %collective-permute-start.1 = (bf16[2304,128]{1,0:T(8,128)(2,1)}, bf16[2304,128]{1,0:T(8,128)(2,1)S(1)}, u32[]{:S(2)}, u32[]{:S(2)}) collective-permute-start(bf16[2304,128]{1,0:T(8,128)(2,1)} %shard_map.73), channel_id=1, source_target_pairs={{0,32},{8,40},{16,48},{24,56},{32,0},{40,8},{48,16},{56,24},{64,96... | collective-permute-start | bytes 1769480 | tf_op jit(solution)/shard_map/ppermute | solution.py:22
  5.9 17.0 %collective-permute-start = (bf16[2304,128]{1,0:T(8,128)(2,1)}, bf16[2304,128]{1,0:T(8,128)(2,1)S(1)}, u32[]{:S(2)}, u32[]{:S(2)}) collective-permute-start(bf16[2304,128]{1,0:T(8,128)(2,1)} %shard_map.73), channel_id=1, source_target_pairs={{0,16},{8,24},{16,0},{24,8},{32,48},{40,56},{48,32},{56,40},{64,80... | collective-permute-start | bytes 1769480 | tf_op jit(solution)/shard_map/ppermute | solution.py:22
  19.4 13.6 %copy-start.2 = (bf16[2304,128]{1,0:T(8,128)(2,1)}, bf16[2304,128]{1,0:T(8,128)(2,1)S(1)}, u32[]{:S(2)}) copy-start(bf16[2304,128]{1,0:T(8,128)(2,1)S(1)} %collective-permute-done.1) | copy-start | bytes 1769476
  19.4 10.0 %collective-permute-start.2 = (bf16[1152,128]{1,0:T(8,128)(2,1)S(1)}, bf16[1152,128]{1,0:T(8,128)(2,1)S(1)}, u32[]{:S(2)}, u32[]{:S(2)}) collective-permute-start(bf16[1152,128]{1,0:T(8,128)(2,1)S(1)} %slice.8), channel_id=1, source_target_pairs={{0,16},{8,24},{16,0},{24,8},{32,48},{40,56},{48,32},{56,40},{64,80... | collective-permute-start | bytes 884744 | tf_op jit(solution)/shard_map/ppermute | solution.py:22
  22.9 10.1 %copy-start.3 = (bf16[2304,128]{1,0:T(8,128)(2,1)}, bf16[2304,128]{1,0:T(8,128)(2,1)S(1)}, u32[]{:S(2)}) copy-start(bf16[2304,128]{1,0:T(8,128)(2,1)S(1)} %collective-permute-done) | copy-start | bytes 1769476
  22.9 9.7 %collective-permute-start.3 = (bf16[1152,128]{1,0:T(8,128)(2,1)S(1)}, bf16[1152,128]{1,0:T(8,128)(2,1)S(1)}, u32[]{:S(2)}, u32[]{:S(2)}) collective-permute-start(bf16[1152,128]{1,0:T(8,128)(2,1)S(1)} %slice.9), channel_id=1, source_target_pairs={{0,32},{8,40},{16,48},{24,56},{32,0},{40,8},{48,16},{56,24},{64,96... | collective-permute-start | bytes 884744 | tf_op jit(solution)/shard_map/ppermute | solution.py:22
  32.6 2.3 %copy-start.6 = (s32[8]{0:T(128)S(1)}, s32[8]{0:T(128)}, u32[]{:S(2)}) copy-start(s32[8]{0:T(128)} %param.12) | copy-start | bytes 100
  32.7 2.9 %copy-start.5 = (s32[8]{0:T(128)S(1)}, s32[8]{0:T(128)}, u32[]{:S(2)}) copy-start(s32[8]{0:T(128)} %constant.43.clone) | copy-start | bytes 100
  33.0 19.3 %copy-start.1 = (bf16[4,2304,128]{2,1,0:T(8,128)(2,1)}, bf16[4,2304,128]{2,1,0:T(8,128)(2,1)S(1)}, u32[]{:S(2)}) copy-start(bf16[4,2304,128]{2,1,0:T(8,128)(2,1)S(1)} %pad_maximum_fusion.refs_3_.refs_4_.refs_7_) | copy-start | bytes 7077892
  33.0 19.3 %collective-permute-start.4 = (bf16[4,2304,128]{2,1,0:T(8,128)(2,1)S(1)}, bf16[4,2304,128]{2,1,0:T(8,128)(2,1)}, u32[]{:S(2)}, u32[]{:S(2)}) collective-permute-start(bf16[4,2304,128]{2,1,0:T(8,128)(2,1)S(1)} %pad_maximum_fusion.refs_3_.refs_4_.refs_7_), channel_id=1, source_target_pairs={{0,8},{8,0},{16,24},{24,16},{32,40},{40,32},{48,56},{56,48},{64,72... | collective-permute-start | bytes 7077896 | tf_op jit(solution)/shard_map/ppermute | solution.py:22

commit v10 on v9

--- a/solution.py
+++ b/solution.py
@@ -22,30 +22,30 @@
     return lax.ppermute(value, axis, pairs)
 
 
-def span_copies(info_ref, local_any, other_any, sk_sc, sv_sc, sems, block, span):
+def span_copies(info_ref, sources, plan, sk_sc, sv_sc, sems, block, span):
     copies = []
-    for j in range(local_any.shape[0]):
-        for parity, source in ((0, local_any), (1, other_any)):
-            slot = 2 * j + parity
-            offset = pl.multiple_of(info_ref[2 + GROUP_DEVS + slot], span)
-            for part, target in ((0, sk_sc), (1, sv_sc)):
-                copies.append(
-                    pltpu.make_async_copy(
-                        source.at[j, pl.ds(2 * block + part * span, span), :],
-                        target.at[pl.ds(offset, span), :],
-                        sems.at[2 * slot + part],
-                    )
+    for source_id, j, slot in plan:
+        offset = pl.multiple_of(info_ref[2 + GROUP_DEVS + slot], span)
+        for part, target in ((0, sk_sc), (1, sv_sc)):
+            copies.append(
+                pltpu.make_async_copy(
+                    sources[source_id].at[j, pl.ds(2 * block + part * span, span), :],
+                    target.at[pl.ds(offset, span), :],
+                    sems.at[2 * slot + part],
                 )
+            )
     return copies
 
 
-def attn_kernel(plan, offset, first, final, info_ref, q_ref, *refs):
+def attn_kernel(plan, offset, first, final, span_plan, info_ref, q_ref, *refs):
     refs = list(refs)
     n_arrays = max(array for array, _ in plan) + 1
     state_in = [] if first else [refs.pop(0) for _ in range(3)]
     kv_refs = [(refs.pop(0), refs.pop(0)) for _ in range(n_arrays)]
     if final:
-        la_ref, oa_ref, o_ref = refs.pop(0), refs.pop(0), refs.pop(0)
+        n_sources = max(source for source, _, _ in span_plan) + 1
+        span_refs = [refs.pop(0) for _ in range(n_sources)]
+        o_ref = refs.pop(0)
         m_sc, l_sc, acc_sc, sk_sc, sv_sc, sems = refs
     else:
         m_out, l_out, acc_out, m_sc, l_sc, acc_sc = refs
@@ -60,7 +60,7 @@
     def _init():
         if final:
             span = sk_sc.shape[0] // GROUP_DEVS
-            for copy in span_copies(info_ref, la_ref, oa_ref, sk_sc, sv_sc, sems, block, span):
+            for copy in span_copies(info_ref, span_refs, span_plan, sk_sc, sv_sc, sems, block, span):
                 copy.start()
         if first:
             m_sc[...] = jnp.full(m_sc.shape, NEG_FILL, jnp.float32)
@@ -114,7 +114,7 @@
         @pl.when(step == last)
         def _span():
             span = sk_sc.shape[0] // GROUP_DEVS
-            for copy in span_copies(info_ref, la_ref, oa_ref, sk_sc, sv_sc, sems, block, span):
+            for copy in span_copies(info_ref, span_refs, span_plan, sk_sc, sv_sc, sems, block, span):
                 copy.wait()
             span_rows = sk_sc.shape[0]
             key_pos = lax.broadcasted_iota(jnp.int32, (rows, span_rows), 1)
@@ -151,7 +151,8 @@
     return pick
 
 
-def attention(info, offset, q_rows, arrays, plan, state, span_sources, tokens, block, span):
+def attention(info, offset, q_rows, arrays, plan, state, span_sources, tokens, block, span,
+              span_plan=None):
     rows = q_rows.shape[0]
     first = state is None
     final = span_sources is not None
@@ -176,7 +177,7 @@
         pltpu.VMEM((rows, HEAD_SIZE), jnp.float32),
     ]
     if final:
-        in_specs += [pl.BlockSpec(memory_space=pl.ANY), pl.BlockSpec(memory_space=pl.ANY)]
+        in_specs += [pl.BlockSpec(memory_space=pl.ANY) for _ in span_sources]
         operands += list(span_sources)
         heads = rows // tokens
         out_shape = jax.ShapeDtypeStruct((tokens, heads * HEAD_SIZE), jnp.bfloat16)
@@ -196,7 +197,7 @@
                      pl.BlockSpec((rows, HEAD_SIZE), fixed))
     flops = 4 * rows * block * HEAD_SIZE * n_steps
     return pl.pallas_call(
-        functools.partial(attn_kernel, plan, offset, first, final),
+        functools.partial(attn_kernel, plan, offset, first, final, span_plan),
         out_shape=out_shape,
         grid_spec=pltpu.PrefetchScalarGridSpec(
             num_scalar_prefetch=1,
@@ -266,16 +267,22 @@
     from_x = exchange(pack, "req", 2)
     from_z = exchange(pack, "req", 4)
     state = attention(info, 0, q_rows, [pack[None]], [(0, 0)], None, None, *size)
+    early = jnp.stack([pack, from_x, from_z])
     diag_lo = exchange(from_z[:half], "req", 2)
     diag_hi = exchange(from_x[half:], "req", 4)
+    other_early = exchange(early, "req", 1)
     state = attention(
         info, 1, q_rows, [from_x[None], from_z[None]], [(0, 0), (1, 0)], state, None, *size
     )
-    diag = jnp.concatenate([diag_lo, diag_hi], 0)
-    local = jnp.stack([pack, from_x, from_z, diag])
-    other = exchange(local, "req", 1)
-    plan = [(0, 3), (1, 0), (1, 1), (1, 2), (1, 3)]
-    attended = attention(info, 3, q_rows, [local, other], plan, state, (local, other), *size)
+    diag = jnp.concatenate([diag_lo, diag_hi], 0)[None]
+    other_diag = exchange(diag, "req", 1)
+    plan = [(0, 0), (1, 0), (1, 1), (1, 2), (2, 0)]
+    span_plan = [(0, 0, 0), (0, 1, 2), (0, 2, 4), (1, 0, 6), (2, 0, 1), (2, 1, 3), (2, 2, 5),
+                 (3, 0, 7)]
+    attended = attention(
+        info, 3, q_rows, [diag, other_early, other_diag], plan, state,
+        (early, diag, other_early, other_diag), *size, span_plan=span_plan,
+    )
     return lax.all_to_all(attended, "tp", split_axis=0, concat_axis=1, tiled=True)
 
 

time: 89.6 us -> 101 us (1.13)
  waiting for transfers between devices: 16.2 us -> 21.8 us
  other arithmetic: 0.34 us -> 3.72 us
  local copies, waits for them, and re-layouts: 3.41 us -> 4.88 us
    ppermute x5 -> x6, waiting for transfers between devices: 16.2 us -> 21.8 us  [exchange(): return lax.ppermute(value, axis, pairs)]
    another operation x2 -> x1, other arithmetic: 0.34 us -> 2.71 us  [body(): early = jnp.stack([pack, from_x, from_z])]
    unnamed x14 -> x16, local copies, waits for them, and re-layouts: 0.03 us -> 1.47 us
    ppermute x5 -> x6, starting transfers between devices: 16.3 us -> 16.8 us  [exchange(): return lax.ppermute(value, axis, pairs)]
  transfers between devices with their start and end apart: 5 -> 6, of which waited for: 3 -> 4; matrix products, arithmetic and copies ran while one was open for 3% -> 4% of each run, Pallas kernels for 16% -> 15%
where the time goes in v10:
time: 101 us; the launch traced here: 100 us
  Pallas kernels  36.8 us (36%)
  waiting for transfers between devices  21.8 us (22%)
  starting transfers between devices  16.8 us (17%)
  blocking collectives  15.9 us (16%)
  local copies, waits for them, and re-layouts  4.88 us (5%)
  other arithmetic  3.72 us (4%)
    pallas_call x3, Pallas kernels, attention(): pl.pallas_call(functools.partial(attn_kernel, plan, offset, first, final,...  34.9 us
    ppermute x6, waiting for transfers between devices, exchange(): return lax.ppermute(value, axis, pairs)  21.8 us
    ppermute x6, starting transfers between devices, exchange(): return lax.ppermute(value, axis, pairs)  16.8 us
    all_to_all x1, blocking collectives, body(): lax.all_to_all(attended, 'tp', split_axis=0, concat_axis=1, tiled=True)  15.9 us
    another operation x1, other arithmetic, body(): early = jnp.stack([pack, from_x, from_z])  2.71 us
  transfers between devices with their start and end apart: 6, of which 4 were waited for; matrix products, arithmetic and copies ran while one was open for 4% of the time, Pallas kernels for 15%

profile of v10, /device:TPU:128, one launch (start us, length us, event | category | flops | bytes accessed | tf_op | source)
XLA Modules:
  0.0 100.1 jit_solution(13633845759690573786)
XLA Ops:
  0.0 0.0 copy-start
  0.0 1.9 %shard_map.73 = bf16[2304,128]{1,0:T(8,128)(2,1)} custom-call(bf16[1024,128]{1,0:T(8,128)(2,1)} %k_ref.1, bf16[1024,128]{1,0:T(8,128)(2,1)} %v_ref.1, bf16[128,128]{1,0:T(8,128)(2,1)} %sk_ref.1, bf16[128,128]{1,0:T(8,128)(2,1)} %sv_ref.1), custom_call_target="tpu_custom_call" | custom-call | tf_op jit(solution)/shard_map/pallas_call | solution.py:230
  1.9 3.8 %collective-permute-start.1 = (bf16[2304,128]{1,0:T(8,128)(2,1)}, bf16[2304,128]{1,0:T(8,128)(2,1)S(1)}, u32[]{:S(2)}, u32[]{:S(2)}) collective-permute-start(bf16[2304,128]{1,0:T(8,128)(2,1)} %shard_map.73), channel_id=1, source_target_pairs={{0,32},{8,40},{16,48},{24,56},{32,0},{40,8},{48,16},{56,24},{64,96... | collective-permute-start | bytes 1769480 | tf_op jit(solution)/shard_map/ppermute | solution.py:22
  5.7 3.4 %collective-permute-start = (bf16[2304,128]{1,0:T(8,128)(2,1)}, bf16[2304,128]{1,0:T(8,128)(2,1)S(1)}, u32[]{:S(2)}, u32[]{:S(2)}) collective-permute-start(bf16[2304,128]{1,0:T(8,128)(2,1)} %shard_map.73), channel_id=1, source_target_pairs={{0,16},{8,24},{16,0},{24,8},{32,48},{40,56},{48,32},{56,40},{64,80... | collective-permute-start | bytes 1769480 | tf_op jit(solution)/shard_map/ppermute | solution.py:22
  9.2 10.1 %collective-permute-done.1 = bf16[2304,128]{1,0:T(8,128)(2,1)S(1)} collective-permute-done((bf16[2304,128]{1,0:T(8,128)(2,1)}, bf16[2304,128]{1,0:T(8,128)(2,1)S(1)}, u32[]{:S(2)}, u32[]{:S(2)}) %collective-permute-start.1) | collective-permute-done | bytes 589856 | tf_op jit(solution)/shard_map/ppermute | solution.py:22
  19.3 3.4 %collective-permute-done = bf16[2304,128]{1,0:T(8,128)(2,1)S(1)} collective-permute-done((bf16[2304,128]{1,0:T(8,128)(2,1)}, bf16[2304,128]{1,0:T(8,128)(2,1)S(1)}, u32[]{:S(2)}, u32[]{:S(2)}) %collective-permute-start) | collective-permute-done | bytes 589856 | tf_op jit(solution)/shard_map/ppermute | solution.py:22
  22.6 2.7 %pad_maximum_fusion.refs_9_ = bf16[3,2304,128]{2,1,0:T(8,128)(2,1)} fusion(bf16[1,2304,128]{2,1,0:T(8,128)(2,1)S(1)} %bitcast.18, bf16[1,2304,128]{2,1,0:T(8,128)(2,1)S(1)} %bitcast.21, bf16[1,2304,128]{2,1,0:T(8,128)(2,1)} %bitcast.24), kind=kLoop, calls=%fused_computation | loop fusion | flops 1769472 | bytes 3538944 | tf_op jit(solution)/shard_map/stack | solution.py:270
  25.4 2.0 %collective-permute-start.4 = (bf16[3,2304,128]{2,1,0:T(8,128)(2,1)}, bf16[3,2304,128]{2,1,0:T(8,128)(2,1)S(1)}, u32[]{:S(2)}, u32[]{:S(2)}) collective-permute-start(bf16[3,2304,128]{2,1,0:T(8,128)(2,1)} %pad_maximum_fusion.refs_9_), channel_id=1, source_target_pairs={{0,8},{8,0},{16,24},{24,16},{32,40},{40,32},{48,56},{56,48},{64,72... | collective-permute-start | bytes 5308424 | tf_op jit(solution)/shard_map/ppermute | solution.py:22
  27.4 0.0 copy-done.3
  27.4 3.4 %collective-permute-start.2 = (bf16[1152,128]{1,0:T(8,128)(2,1)S(1)}, bf16[1152,128]{1,0:T(8,128)(2,1)S(1)}, u32[]{:S(2)}, u32[]{:S(2)}) collective-permute-start(bf16[1152,128]{1,0:T(8,128)(2,1)S(1)} %slice.8), channel_id=1, source_target_pairs={{0,16},{8,24},{16,0},{24,8},{32,48},{40,56},{48,32},{56,40},{64,80... | collective-permute-start | bytes 884744 | tf_op jit(solution)/shard_map/ppermute | solution.py:22
  30.9 0.0 copy-done.4
  30.9 2.2 %collective-permute-start.3 = (bf16[1152,128]{1,0:T(8,128)(2,1)S(1)}, bf16[1152,128]{1,0:T(8,128)(2,1)}, u32[]{:S(2)}, u32[]{:S(2)}) collective-permute-start(bf16[1152,128]{1,0:T(8,128)(2,1)S(1)} %slice.9), channel_id=1, source_target_pairs={{0,32},{8,40},{16,48},{24,56},{32,0},{40,8},{48,16},{56,24},{64,96... | collective-permute-start | bytes 884744 | tf_op jit(solution)/shard_map/ppermute | solution.py:22
  33.1 0.0 copy-done.7
  33.1 0.6 dynamic_slice.4
  33.7 5.0 %collective-permute-done.2 = bf16[1152,128]{1,0:T(8,128)(2,1)S(1)} collective-permute-done((bf16[1152,128]{1,0:T(8,128)(2,1)S(1)}, bf16[1152,128]{1,0:T(8,128)(2,1)S(1)}, u32[]{:S(2)}, u32[]{:S(2)}) %collective-permute-start.2) | collective-permute-done | bytes 294944 | tf_op jit(solution)/shard_map/ppermute | solution.py:22
  38.7 3.3 %collective-permute-done.3 = bf16[1152,128]{1,0:T(8,128)(2,1)} collective-permute-done((bf16[1152,128]{1,0:T(8,128)(2,1)S(1)}, bf16[1152,128]{1,0:T(8,128)(2,1)}, u32[]{:S(2)}, u32[]{:S(2)}) %collective-permute-start.3) | collective-permute-done | bytes 294944 | tf_op jit(solution)/shard_map/ppermute | solution.py:22
  42.0 1.0 maximum_bitcast_fusion.refs_3_.refs_4_.refs_10_
  43.0 1.9 %collective-permute-start.5 = (bf16[1,2304,128]{2,1,0:T(8,128)(2,1)S(1)}, bf16[1,2304,128]{2,1,0:T(8,128)(2,1)S(1)}, u32[]{:S(2)}, u32[]{:S(2)}) collective-permute-start(bf16[1,2304,128]{2,1,0:T(8,128)(2,1)S(1)} %maximum_bitcast_fusion.refs_3_.refs_4_.refs_10_), channel_id=1, source_target_pairs={{0,8},{8,0},{16,24},{24,16},{32,40},{40,32},{48,56},{56,48},{64,72... | collective-permute-start | bytes 1769480 | tf_op jit(solution)/shard_map/ppermute | solution.py:22
  45.0 1.3 %concatenate.6.info_ref = s32[26]{0:T(128)} concatenate(s32[1]{0:T(128)} %dynamic_slice.4, s32[1]{0:T(128)} %bitcast, s32[8]{0:T(128)S(1)} %fusion.1, s32[8]{0:T(128)S(1)} %get-tuple-element.18, s32[8]{0:T(128)S(1)} %get-tuple-element.17), dimensions={0} | concatenate | bytes 208 | tf_op jit(solution)/shard_map/concatenate | solution.py:255
  46.3 0.0 copy-done
  46.3 0.8 copy_bitcast_fusion
  47.1 5.8 %shard_map.74 = (f32[1024,1]{1,0:T(8,128)}, f32[1024,1]{1,0:T(8,128)}, f32[1024,128]{1,0:T(8,128)}) custom-call(s32[26]{0:T(128)} %concatenate.6.info_ref, bf16[1024,128]{1,0:T(8,128)(2,1)} %bitcast.27, bf16[1,2304,128]{2,1,0:T(8,128)(2,1)} %bitcast.25, bf16[1,2304,128]{2,1,0:T(8,128)(2,1)} %bitcast.26), custom_call_target="tpu_custom_call" | custom-call | flops 536870912 | bytes 524288 | tf_op jit(solution)/shard_map/pallas_call | solution.py:199
  52.8 8.8 %shard_map.75 = (f32[1024,1]{1,0:T(8,128)}, f32[1024,1]{1,0:T(8,128)}, f32[1024,128]{1,0:T(8,128)}) custom-call(s32[26]{0:T(128)} %concatenate.6.info_ref, bf16[1024,128]{1,0:T(8,128)(2,1)} %bitcast.28, f32[1024,1]{1,0:T(8,128)} %get-tuple-element.11.refs_0_, f32[1024,1]{1,0:T(8,128)} %get-tuple-element.12.refs_1_, f32[1024,128]{1,0:T(8,128)} %get-tuple-element.13.refs_2_, ...), custom_call_target="tpu_custom_call" | custom-call | flops 1073741824 | bytes 1048576 | tf_op jit(solution)/shard_map/pallas_call | solution.py:199
  61.6 0.0 copy-done.2
  61.6 0.0 collective-permute-done.5.refs_7_.refs_8_.refs_12_
  61.6 0.0 copy-start.5
  61.6 0.0 collective-permute-done.4.refs_5_.refs_6_.refs_11_
  61.7 0.8 copy-done.5
  62.4 0.7 copy-done.1
  63.1 20.3 %shard_map.76 = bf16[128,1024]{1,0:T(8,128)(2,1)} custom-call(s32[26]{0:T(128)} %concatenate.6.info_ref, bf16[1024,128]{1,0:T(8,128)(2,1)} %bitcast.29, f32[1024,1]{1,0:T(8,128)} %get-tuple-element.14.refs_0_, f32[1024,1]{1,0:T(8,128)} %get-tuple-element.15.refs_1_, f32[1024,128]{1,0:T(8,128)} %get-tuple-element.16.refs_2_, bf16[1,2304,128]{2,1,0:T(8,128)(2,1)} %copy-done.2, ...), custom_call_target="tpu_custom_call" | custom-call | flops 3221225472 | bytes 3145728 | tf_op jit(solution)/shard_map/pallas_call | solution.py:199
  83.4 15.9 %all_to_all.19 = bf16[8,16,1024]{2,1,0:T(8,128)(2,1)S(1)} all-to-all(bf16[8,16,1024]{2,1,0:T(8,128)(2,1)} %bitcast.30), channel_id=1, replica_groups=mesh['req'=64,'tp'=8] {'tp'}, dimensions={0} | all-to-all | bytes 524288 | tf_op jit(solution)/shard_map/all_to_all | solution.py:286
  99.3 0.7 copy.11
  (11 shorter events, 0.1 us)
Async XLA Ops:
  0.0 46.3 %copy-start = (bf16[128,1024]{1,0:T(8,128)(2,1)S(1)}, bf16[128,1024]{1,0:T(8,128)(2,1)}, u32[]{:S(2)}) copy-start(bf16[128,1024]{1,0:T(8,128)(2,1)} %param.7) | copy-start | bytes 786436
  1.9 17.3 %collective-permute-start.1 = (bf16[2304,128]{1,0:T(8,128)(2,1)}, bf16[2304,128]{1,0:T(8,128)(2,1)S(1)}, u32[]{:S(2)}, u32[]{:S(2)}) collective-permute-start(bf16[2304,128]{1,0:T(8,128)(2,1)} %shard_map.73), channel_id=1, source_target_pairs={{0,32},{8,40},{16,48},{24,56},{32,0},{40,8},{48,16},{56,24},{64,96... | collective-permute-start | bytes 1769480 | tf_op jit(solution)/shard_map/ppermute | solution.py:22
  5.7 16.9 %collective-permute-start = (bf16[2304,128]{1,0:T(8,128)(2,1)}, bf16[2304,128]{1,0:T(8,128)(2,1)S(1)}, u32[]{:S(2)}, u32[]{:S(2)}) collective-permute-start(bf16[2304,128]{1,0:T(8,128)(2,1)} %shard_map.73), channel_id=1, source_target_pairs={{0,16},{8,24},{16,0},{24,8},{32,48},{40,56},{48,32},{56,40},{64,80... | collective-permute-start | bytes 1769480 | tf_op jit(solution)/shard_map/ppermute | solution.py:22
  19.3 8.1 %copy-start.3 = (bf16[2304,128]{1,0:T(8,128)(2,1)}, bf16[2304,128]{1,0:T(8,128)(2,1)S(1)}, u32[]{:S(2)}) copy-start(bf16[2304,128]{1,0:T(8,128)(2,1)S(1)} %collective-permute-done.1) | copy-start | bytes 1769476
  22.6 8.2 %copy-start.4 = (bf16[2304,128]{1,0:T(8,128)(2,1)}, bf16[2304,128]{1,0:T(8,128)(2,1)S(1)}, u32[]{:S(2)}) copy-start(bf16[2304,128]{1,0:T(8,128)(2,1)S(1)} %collective-permute-done) | copy-start | bytes 1769476
  22.6 10.5 %copy-start.7 = (s32[8]{0:T(128)S(1)}, s32[8]{0:T(128)}, u32[]{:S(2)}) copy-start(s32[8]{0:T(128)} %param.12) | copy-start | bytes 100
  25.4 19.6 %copy-start.6 = (s32[8]{0:T(128)S(1)}, s32[8]{0:T(128)}, u32[]{:S(2)}) copy-start(s32[8]{0:T(128)} %constant.43.clone) | copy-start | bytes 100
  25.4 36.3 %collective-permute-start.4 = (bf16[3,2304,128]{2,1,0:T(8,128)(2,1)}, bf16[3,2304,128]{2,1,0:T(8,128)(2,1)S(1)}, u32[]{:S(2)}, u32[]{:S(2)}) collective-permute-start(bf16[3,2304,128]{2,1,0:T(8,128)(2,1)} %pad_maximum_fusion.refs_9_), channel_id=1, source_target_pairs={{0,8},{8,0},{16,24},{24,16},{32,40},{40,32},{48,56},{56,48},{64,72... | collective-permute-start | bytes 5308424 | tf_op jit(solution)/shard_map/ppermute | solution.py:22
  27.4 11.3 %collective-permute-start.2 = (bf16[1152,128]{1,0:T(8,128)(2,1)S(1)}, bf16[1152,128]{1,0:T(8,128)(2,1)S(1)}, u32[]{:S(2)}, u32[]{:S(2)}) collective-permute-start(bf16[1152,128]{1,0:T(8,128)(2,1)S(1)} %slice.8), channel_id=1, source_target_pairs={{0,16},{8,24},{16,0},{24,8},{32,48},{40,56},{48,32},{56,40},{64,80... | collective-permute-start | bytes 884744 | tf_op jit(solution)/shard_map/ppermute | solution.py:22
  30.9 11.1 %collective-permute-start.3 = (bf16[1152,128]{1,0:T(8,128)(2,1)S(1)}, bf16[1152,128]{1,0:T(8,128)(2,1)}, u32[]{:S(2)}, u32[]{:S(2)}) collective-permute-start(bf16[1152,128]{1,0:T(8,128)(2,1)S(1)} %slice.9), channel_id=1, source_target_pairs={{0,32},{8,40},{16,48},{24,56},{32,0},{40,8},{48,16},{56,24},{64,96... | collective-permute-start | bytes 884744 | tf_op jit(solution)/shard_map/ppermute | solution.py:22
  43.0 18.6 %copy-start.2 = (bf16[1,2304,128]{2,1,0:T(8,128)(2,1)}, bf16[1,2304,128]{2,1,0:T(8,128)(2,1)S(1)}, u32[]{:S(2)}) copy-start(bf16[1,2304,128]{2,1,0:T(8,128)(2,1)S(1)} %maximum_bitcast_fusion.refs_3_.refs_4_.refs_10_) | copy-start | bytes 1769476
  43.0 18.6 %collective-permute-start.5 = (bf16[1,2304,128]{2,1,0:T(8,128)(2,1)S(1)}, bf16[1,2304,128]{2,1,0:T(8,128)(2,1)S(1)}, u32[]{:S(2)}, u32[]{:S(2)}) collective-permute-start(bf16[1,2304,128]{2,1,0:T(8,128)(2,1)S(1)} %maximum_bitcast_fusion.refs_3_.refs_4_.refs_10_), channel_id=1, source_target_pairs={{0,8},{8,0},{16,24},{24,16},{32,40},{40,32},{48,56},{56,48},{64,72... | collective-permute-start | bytes 1769480 | tf_op jit(solution)/shard_map/ppermute | solution.py:22
  61.6 0.8 copy-start.5
  61.6 1.5 %copy-start.1 = (bf16[3,2304,128]{2,1,0:T(8,128)(2,1)}, bf16[3,2304,128]{2,1,0:T(8,128)(2,1)S(1)}, u32[]{:S(2)}) copy-start(bf16[3,2304,128]{2,1,0:T(8,128)(2,1)S(1)} %collective-permute-done.4.refs_5_.refs_6_.refs_11_) | copy-start | bytes 5308420

commit v11 on v9

--- a/solution.py
+++ b/solution.py
@@ -6,11 +6,12 @@
 from jax import lax
 from jax.experimental import pallas as pl
 from jax.experimental.pallas import tpu as pltpu
-from jax.sharding import PartitionSpec as P
+from jax.sharding import Mesh, PartitionSpec as P
 
 
 HEAD_SIZE = 128
 GROUP_DEVS = 8
+TP_HI = 2
 STEP_SLOTS = (0, 2, 4, 6, 1, 3, 5, 7)
 NEG_FILL = -1e30
 SCALE = 1.0 / math.sqrt(HEAD_SIZE)
@@ -276,10 +277,18 @@
     other = exchange(local, "req", 1)
     plan = [(0, 3), (1, 0), (1, 1), (1, 2), (1, 3)]
     attended = attention(info, 3, q_rows, [local, other], plan, state, (local, other), *size)
-    return lax.all_to_all(attended, "tp", split_axis=0, concat_axis=1, tiled=True)
+    hi, lo = lax.axis_size("tph"), lax.axis_size("tpl")
+    pieces = attended.reshape(hi, lo, tok_rows // (hi * lo), attended.shape[1])
+    pieces = lax.all_to_all(pieces.transpose(1, 0, 2, 3), "tpl", 0, 0)
+    pieces = lax.all_to_all(pieces.transpose(1, 0, 2, 3), "tph", 0, 0)
+    return pieces.transpose(2, 0, 1, 3).reshape(pieces.shape[2], -1)
 
 
 def solution(mesh):
-    in_specs = (P("req", "tp"), P("req", "tp"), P("req", "tp"), P("req", "tp"), P("req", "tp"), P())
-    out_specs = P(("req", "tp"), None)
+    tp_hi = TP_HI
+    devices = mesh.devices.reshape(mesh.shape["req"], tp_hi, mesh.shape["tp"] // tp_hi)
+    mesh = Mesh(devices, ("req", "tph", "tpl"))
+    rows = P("req", ("tph", "tpl"))
+    in_specs = (rows, rows, rows, rows, rows, P())
+    out_specs = P(("req", "tph", "tpl"), None)
     return jax.shard_map(body, mesh=mesh, in_specs=in_specs, out_specs=out_specs, check_vma=False)

time: 89.6 us -> 97.1 us (1.084)
  blocking collectives: 15.9 us -> 22.1 us
  local copies, waits for them, and re-layouts: 3.41 us -> 4.77 us
    all_to_all x1 -> x2, blocking collectives: 15.9 us -> 22.1 us  [the longest x1 11.6 us: body(): pieces = lax.all_to_all(pieces.transpose(1, 0, 2, 3), 'tpl', 0, 0)]
    reshape x0 -> x2, local copies, waits for them, and re-layouts: none -> 1.85 us  [the longest x1 0.97 us: body(): pieces = attended.reshape(hi, lo, tok_rows // (hi * lo), attended.shape[1])]
  transfers between devices with their start and end apart: 5 -> 5, of which waited for: 3 -> 3; matrix products, arithmetic and copies ran while one was open for 3% -> 3% of each run, Pallas kernels for 16% -> 15%
where the time goes in v11:
time: 97.1 us; the launch traced here: 96.6 us
  Pallas kernels  36.7 us (38%)
  blocking collectives  22.1 us (23%)
  starting transfers between devices  16.3 us (17%)
  waiting for transfers between devices  16.2 us (17%)
  local copies, waits for them, and re-layouts  4.77 us (5%)
    pallas_call x3, Pallas kernels, attention(): pl.pallas_call(functools.partial(attn_kernel, plan, offset, first, final)...  34.8 us
    ppermute x5, starting transfers between devices, exchange(): return lax.ppermute(value, axis, pairs)  16.3 us
    ppermute x5, waiting for transfers between devices, exchange(): return lax.ppermute(value, axis, pairs)  16.2 us
    all_to_all x1, blocking collectives, body(): pieces = lax.all_to_all(pieces.transpose(1, 0, 2, 3), 'tpl', 0, 0)  11.6 us
    all_to_all x1, blocking collectives, body(): pieces = lax.all_to_all(pieces.transpose(1, 0, 2, 3), 'tph', 0, 0)  10.5 us
  transfers between devices with their start and end apart: 5, of which 3 were waited for; matrix products, arithmetic and copies ran while one was open for 3% of the time, Pallas kernels for 15%

profile of v11, /device:TPU:128, one launch (start us, length us, event | category | flops | bytes accessed | tf_op | source)
XLA Modules:
  0.0 96.6 jit_solution(4494133606205141251)
XLA Ops:
  0.0 0.0 copy-start
  0.0 1.9 %shard_map.73 = bf16[2304,128]{1,0:T(8,128)(2,1)} custom-call(bf16[1024,128]{1,0:T(8,128)(2,1)} %k_ref.1, bf16[1024,128]{1,0:T(8,128)(2,1)} %v_ref.1, bf16[128,128]{1,0:T(8,128)(2,1)} %sk_ref.1, bf16[128,128]{1,0:T(8,128)(2,1)} %sv_ref.1), custom_call_target="tpu_custom_call" | custom-call | tf_op jit(solution)/shard_map/pallas_call | solution.py:230
  1.9 3.9 %collective-permute-start.1 = (bf16[2304,128]{1,0:T(8,128)(2,1)}, bf16[2304,128]{1,0:T(8,128)(2,1)S(1)}, u32[]{:S(2)}, u32[]{:S(2)}) collective-permute-start(bf16[2304,128]{1,0:T(8,128)(2,1)} %shard_map.73), channel_id=1, source_target_pairs={{0,32},{8,40},{16,48},{24,56},{32,0},{40,8},{48,16},{56,24},{64,96... | collective-permute-start | bytes 1769480 | tf_op jit(solution)/shard_map/ppermute | solution.py:23
  5.9 3.4 %collective-permute-start = (bf16[2304,128]{1,0:T(8,128)(2,1)}, bf16[2304,128]{1,0:T(8,128)(2,1)S(1)}, u32[]{:S(2)}, u32[]{:S(2)}) collective-permute-start(bf16[2304,128]{1,0:T(8,128)(2,1)} %shard_map.73), channel_id=1, source_target_pairs={{0,16},{8,24},{16,0},{24,8},{32,48},{40,56},{48,32},{56,40},{64,80... | collective-permute-start | bytes 1769480 | tf_op jit(solution)/shard_map/ppermute | solution.py:23
  9.3 10.1 %collective-permute-done.1 = bf16[2304,128]{1,0:T(8,128)(2,1)S(1)} collective-permute-done((bf16[2304,128]{1,0:T(8,128)(2,1)}, bf16[2304,128]{1,0:T(8,128)(2,1)S(1)}, u32[]{:S(2)}, u32[]{:S(2)}) %collective-permute-start.1) | collective-permute-done | bytes 589856 | tf_op jit(solution)/shard_map/ppermute | solution.py:23
  19.4 3.4 %collective-permute-start.2 = (bf16[1152,128]{1,0:T(8,128)(2,1)S(1)}, bf16[1152,128]{1,0:T(8,128)(2,1)S(1)}, u32[]{:S(2)}, u32[]{:S(2)}) collective-permute-start(bf16[1152,128]{1,0:T(8,128)(2,1)S(1)} %slice.8), channel_id=1, source_target_pairs={{0,16},{8,24},{16,0},{24,8},{32,48},{40,56},{48,32},{56,40},{64,80... | collective-permute-start | bytes 884744 | tf_op jit(solution)/shard_map/ppermute | solution.py:23
  22.9 0.0 collective-permute-done
  22.9 0.0 copy-start.3
  22.9 3.6 %collective-permute-start.3 = (bf16[1152,128]{1,0:T(8,128)(2,1)S(1)}, bf16[1152,128]{1,0:T(8,128)(2,1)S(1)}, u32[]{:S(2)}, u32[]{:S(2)}) collective-permute-start(bf16[1152,128]{1,0:T(8,128)(2,1)S(1)} %slice.9), channel_id=1, source_target_pairs={{0,32},{8,40},{16,48},{24,56},{32,0},{40,8},{48,16},{56,24},{64,96... | collective-permute-start | bytes 884744 | tf_op jit(solution)/shard_map/ppermute | solution.py:23
  26.6 2.9 %collective-permute-done.2 = bf16[1152,128]{1,0:T(8,128)(2,1)S(1)} collective-permute-done((bf16[1152,128]{1,0:T(8,128)(2,1)S(1)}, bf16[1152,128]{1,0:T(8,128)(2,1)S(1)}, u32[]{:S(2)}, u32[]{:S(2)}) %collective-permute-start.2) | collective-permute-done | bytes 294944 | tf_op jit(solution)/shard_map/ppermute | solution.py:23
  29.4 3.2 %collective-permute-done.3 = bf16[1152,128]{1,0:T(8,128)(2,1)S(1)} collective-permute-done((bf16[1152,128]{1,0:T(8,128)(2,1)S(1)}, bf16[1152,128]{1,0:T(8,128)(2,1)S(1)}, u32[]{:S(2)}, u32[]{:S(2)}) %collective-permute-start.3) | collective-permute-done | bytes 294944 | tf_op jit(solution)/shard_map/ppermute | solution.py:23
  32.6 0.0 copy-start.6
  32.7 0.0 copy-start.5
  32.7 0.3 pad_maximum_fusion.refs_3_.refs_4_.refs_7_
  33.0 0.0 copy-done.2
  33.0 0.0 copy-done.3
  33.0 0.0 copy-start.1
  33.0 1.9 %collective-permute-start.4 = (bf16[4,2304,128]{2,1,0:T(8,128)(2,1)S(1)}, bf16[4,2304,128]{2,1,0:T(8,128)(2,1)}, u32[]{:S(2)}, u32[]{:S(2)}) collective-permute-start(bf16[4,2304,128]{2,1,0:T(8,128)(2,1)S(1)} %pad_maximum_fusion.refs_3_.refs_4_.refs_7_), channel_id=1, source_target_pairs={{0,8},{8,0},{16,24},{24,16},{32,40},{40,32},{48,56},{56,48},{64,72... | collective-permute-start | bytes 7077896 | tf_op jit(solution)/shard_map/ppermute | solution.py:23
  35.0 0.6 dynamic_slice.4
  35.6 0.0 copy-done.5
  35.6 1.3 %concatenate.6.info_ref = s32[26]{0:T(128)} concatenate(s32[1]{0:T(128)} %dynamic_slice.4, s32[1]{0:T(128)} %bitcast, s32[8]{0:T(128)S(1)} %fusion.1, s32[8]{0:T(128)S(1)} %get-tuple-element.18, s32[8]{0:T(128)S(1)} %get-tuple-element.17), dimensions={0} | concatenate | bytes 208 | tf_op jit(solution)/shard_map/concatenate | solution.py:255
  36.8 0.8 copy_bitcast_fusion
  37.6 5.8 %shard_map.74 = (f32[1024,1]{1,0:T(8,128)}, f32[1024,1]{1,0:T(8,128)}, f32[1024,128]{1,0:T(8,128)}) custom-call(s32[26]{0:T(128)} %concatenate.6.info_ref, bf16[1024,128]{1,0:T(8,128)(2,1)} %bitcast.26, bf16[1,2304,128]{2,1,0:T(8,128)(2,1)} %bitcast.29, bf16[1,2304,128]{2,1,0:T(8,128)(2,1)} %bitcast.30), custom_call_target="tpu_custom_call" | custom-call | flops 536870912 | bytes 524288 | tf_op jit(solution)/shard_map/pallas_call | solution.py:199
  43.4 8.9 %shard_map.75 = (f32[1024,1]{1,0:T(8,128)}, f32[1024,1]{1,0:T(8,128)}, f32[1024,128]{1,0:T(8,128)}) custom-call(s32[26]{0:T(128)} %concatenate.6.info_ref, bf16[1024,128]{1,0:T(8,128)(2,1)} %bitcast.27, f32[1024,1]{1,0:T(8,128)} %get-tuple-element.11.refs_0_, f32[1024,1]{1,0:T(8,128)} %get-tuple-element.12.refs_1_, f32[1024,128]{1,0:T(8,128)} %get-tuple-element.13.refs_2_, ...), custom_call_target="tpu_custom_call" | custom-call | flops 1073741824 | bytes 1048576 | tf_op jit(solution)/shard_map/pallas_call | solution.py:199
  52.3 0.0 copy-done.1
  52.3 0.0 collective-permute-done.4.refs_5_.refs_6_.refs_8_
  52.3 20.1 %shard_map.76 = bf16[128,1024]{1,0:T(8,128)(2,1)} custom-call(s32[26]{0:T(128)} %concatenate.6.info_ref, bf16[1024,128]{1,0:T(8,128)(2,1)} %bitcast.28, f32[1024,1]{1,0:T(8,128)} %get-tuple-element.14.refs_0_, f32[1024,1]{1,0:T(8,128)} %get-tuple-element.15.refs_1_, f32[1024,128]{1,0:T(8,128)} %get-tuple-element.16.refs_2_, bf16[4,2304,128]{2,1,0:T(8,128)(2,1)} %copy-done.1, ...), custom_call_target="tpu_custom_call" | custom-call | flops 3221225472 | bytes 3145728 | tf_op jit(solution)/shard_map/pallas_call | solution.py:199
  72.4 1.0 %copy.22 = bf16[2,4,16,1024]{3,2,0,1:T(8,128)(2,1)S(1)} copy(bf16[2,4,16,1024]{3,2,1,0:T(8,128)(2,1)} %bitcast.32) | data formatting | bytes 524288 | tf_op jit(solution)/shard_map/reshape | solution.py:281
  73.4 11.6 %all_to_all.10 = bf16[4,2,16,1024]{3,2,1,0:T(8,128)(2,1)S(1)} all-to-all(bf16[4,2,16,1024]{3,2,1,0:T(8,128)(2,1)S(1)} %bitcast.33), channel_id=1, replica_groups=mesh['req'=64,'tph'=2,'tpl'=4] {'tpl'}, dimensions={0} | all-to-all | bytes 524288 | tf_op jit(solution)/shard_map/all_to_all | solution.py:282
  85.0 10.5 %all_to_all.11 = bf16[2,4,16,1024]{3,2,1,0:T(8,128)(2,1)S(1)} all-to-all(bf16[2,4,16,1024]{3,2,1,0:T(8,128)(2,1)S(1)} %copy.17), channel_id=1, replica_groups=mesh['req'=64,'tph'=2,'tpl'=4] {'tph'}, dimensions={0} | all-to-all | bytes 524288 | tf_op jit(solution)/shard_map/all_to_all | solution.py:283
  95.5 0.2 copy.18
  95.7 0.9 reshape.15
  (11 shorter events, 0.1 us)
Async XLA Ops:
  0.0 36.8 %copy-start = (bf16[128,1024]{1,0:T(8,128)(2,1)S(1)}, bf16[128,1024]{1,0:T(8,128)(2,1)}, u32[]{:S(2)}) copy-start(bf16[128,1024]{1,0:T(8,128)(2,1)} %param.7) | copy-start | bytes 786436
  1.9 30.7 %copy-start.4 = (bf16[2304,128]{1,0:T(8,128)(2,1)S(1)}, bf16[2304,128]{1,0:T(8,128)(2,1)}, u32[]{:S(2)}) copy-start(bf16[2304,128]{1,0:T(8,128)(2,1)} %shard_map.73) | copy-start | bytes 1769476
  1.9 17.5 %collective-permute-start.1 = (bf16[2304,128]{1,0:T(8,128)(2,1)}, bf16[2304,128]{1,0:T(8,128)(2,1)S(1)}, u32[]{:S(2)}, u32[]{:S(2)}) collective-permute-start(bf16[2304,128]{1,0:T(8,128)(2,1)} %shard_map.73), channel_id=1, source_target_pairs={{0,32},{8,40},{16,48},{24,56},{32,0},{40,8},{48,16},{56,24},{64,96... | collective-permute-start | bytes 1769480 | tf_op jit(solution)/shard_map/ppermute | solution.py:23
  5.9 17.0 %collective-permute-start = (bf16[2304,128]{1,0:T(8,128)(2,1)}, bf16[2304,128]{1,0:T(8,128)(2,1)S(1)}, u32[]{:S(2)}, u32[]{:S(2)}) collective-permute-start(bf16[2304,128]{1,0:T(8,128)(2,1)} %shard_map.73), channel_id=1, source_target_pairs={{0,16},{8,24},{16,0},{24,8},{32,48},{40,56},{48,32},{56,40},{64,80... | collective-permute-start | bytes 1769480 | tf_op jit(solution)/shard_map/ppermute | solution.py:23
  19.4 13.6 %copy-start.2 = (bf16[2304,128]{1,0:T(8,128)(2,1)}, bf16[2304,128]{1,0:T(8,128)(2,1)S(1)}, u32[]{:S(2)}) copy-start(bf16[2304,128]{1,0:T(8,128)(2,1)S(1)} %collective-permute-done.1) | copy-start | bytes 1769476
  19.4 10.0 %collective-permute-start.2 = (bf16[1152,128]{1,0:T(8,128)(2,1)S(1)}, bf16[1152,128]{1,0:T(8,128)(2,1)S(1)}, u32[]{:S(2)}, u32[]{:S(2)}) collective-permute-start(bf16[1152,128]{1,0:T(8,128)(2,1)S(1)} %slice.8), channel_id=1, source_target_pairs={{0,16},{8,24},{16,0},{24,8},{32,48},{40,56},{48,32},{56,40},{64,80... | collective-permute-start | bytes 884744 | tf_op jit(solution)/shard_map/ppermute | solution.py:23
  22.9 10.1 %copy-start.3 = (bf16[2304,128]{1,0:T(8,128)(2,1)}, bf16[2304,128]{1,0:T(8,128)(2,1)S(1)}, u32[]{:S(2)}) copy-start(bf16[2304,128]{1,0:T(8,128)(2,1)S(1)} %collective-permute-done) | copy-start | bytes 1769476
  22.9 9.7 %collective-permute-start.3 = (bf16[1152,128]{1,0:T(8,128)(2,1)S(1)}, bf16[1152,128]{1,0:T(8,128)(2,1)S(1)}, u32[]{:S(2)}, u32[]{:S(2)}) collective-permute-start(bf16[1152,128]{1,0:T(8,128)(2,1)S(1)} %slice.9), channel_id=1, source_target_pairs={{0,32},{8,40},{16,48},{24,56},{32,0},{40,8},{48,16},{56,24},{64,96... | collective-permute-start | bytes 884744 | tf_op jit(solution)/shard_map/ppermute | solution.py:23
  32.6 2.3 %copy-start.6 = (s32[8]{0:T(128)S(1)}, s32[8]{0:T(128)}, u32[]{:S(2)}) copy-start(s32[8]{0:T(128)} %param.12) | copy-start | bytes 100
  32.7 2.9 %copy-start.5 = (s32[8]{0:T(128)S(1)}, s32[8]{0:T(128)}, u32[]{:S(2)}) copy-start(s32[8]{0:T(128)} %constant.43.clone) | copy-start | bytes 100
  33.0 19.3 %copy-start.1 = (bf16[4,2304,128]{2,1,0:T(8,128)(2,1)}, bf16[4,2304,128]{2,1,0:T(8,128)(2,1)S(1)}, u32[]{:S(2)}) copy-start(bf16[4,2304,128]{2,1,0:T(8,128)(2,1)S(1)} %pad_maximum_fusion.refs_3_.refs_4_.refs_7_) | copy-start | bytes 7077892
  33.0 19.3 %collective-permute-start.4 = (bf16[4,2304,128]{2,1,0:T(8,128)(2,1)S(1)}, bf16[4,2304,128]{2,1,0:T(8,128)(2,1)}, u32[]{:S(2)}, u32[]{:S(2)}) collective-permute-start(bf16[4,2304,128]{2,1,0:T(8,128)(2,1)S(1)} %pad_maximum_fusion.refs_3_.refs_4_.refs_7_), channel_id=1, source_target_pairs={{0,8},{8,0},{16,24},{24,16},{32,40},{40,32},{48,56},{56,48},{64,72... | collective-permute-start | bytes 7077896 | tf_op jit(solution)/shard_map/ppermute | solution.py:23

commit v12 on v9

--- a/solution.py
+++ b/solution.py
@@ -206,7 +206,7 @@
             scratch_shapes=scratch,
         ),
         compiler_params=pltpu.CompilerParams(
-            dimension_semantics=("arbitrary",), vmem_limit_bytes=56 * 1024 * 1024
+            dimension_semantics=("arbitrary",), vmem_limit_bytes=32 * 1024 * 1024
         ),
         cost_estimate=pl.CostEstimate(
             flops=flops, transcendentals=rows * block * n_steps,
@@ -274,8 +274,9 @@
     diag = jnp.concatenate([diag_lo, diag_hi], 0)
     local = jnp.stack([pack, from_x, from_z, diag])
     other = exchange(local, "req", 1)
-    plan = [(0, 3), (1, 0), (1, 1), (1, 2), (1, 3)]
-    attended = attention(info, 3, q_rows, [local, other], plan, state, (local, other), *size)
+    state = attention(info, 3, q_rows, [local], [(0, 3)], state, None, *size)
+    plan = [(0, 0), (0, 1), (0, 2), (0, 3)]
+    attended = attention(info, 4, q_rows, [other], plan, state, (local, other), *size)
     return lax.all_to_all(attended, "tp", split_axis=0, concat_axis=1, tiled=True)
 
 

time: 89.6 us -> 83 us (0.926)
  Pallas kernels: 36.7 us -> 30.6 us
    pallas_call x3 -> x4, Pallas kernels: 34.8 us -> 28.7 us  [attention(): pl.pallas_call(functools.partial(attn_kernel, plan, offset, first, final)...]
    unnamed x14, local copies, waits for them, and re-layouts: 0.03 us -> 1.14 us
  transfers between devices with their start and end apart: 5 -> 5, of which waited for: 3 -> 3; matrix products, arithmetic and copies ran while one was open for 3% -> 2% of each run, Pallas kernels for 16% -> 15%
where the time goes in v12:
time: 83 us; the launch traced here: 82.6 us
  Pallas kernels  30.6 us (37%)
  starting transfers between devices  16.3 us (20%)
  waiting for transfers between devices  16.2 us (20%)
  blocking collectives  15.7 us (19%)
  local copies, waits for them, and re-layouts  3.26 us (4%)
    pallas_call x4, Pallas kernels, attention(): pl.pallas_call(functools.partial(attn_kernel, plan, offset, first, final)...  28.7 us
    ppermute x5, starting transfers between devices, exchange(): return lax.ppermute(value, axis, pairs)  16.3 us
    ppermute x5, waiting for transfers between devices, exchange(): return lax.ppermute(value, axis, pairs)  16.2 us
    all_to_all x1, blocking collectives, body(): lax.all_to_all(attended, 'tp', split_axis=0, concat_axis=1, tiled=True)  15.7 us
    pallas_call x1, Pallas kernels, make_pack(): pl.pallas_call(pack_kernel, out_shape=jax.ShapeDtypeStruct((rows, HEAD_SI...  1.94 us
  transfers between devices with their start and end apart: 5, of which 3 were waited for; matrix products, arithmetic and copies ran while one was open for 2% of the time, Pallas kernels for 15%

profile of v12, /device:TPU:128, one launch (start us, length us, event | category | flops | bytes accessed | tf_op | source)
XLA Modules:
  0.0 82.6 jit_solution(16072735411827736881)
XLA Ops:
  0.0 0.0 copy-start
  0.0 1.9 %shard_map.73 = bf16[2304,128]{1,0:T(8,128)(2,1)} custom-call(bf16[1024,128]{1,0:T(8,128)(2,1)} %k_ref.1, bf16[1024,128]{1,0:T(8,128)(2,1)} %v_ref.1, bf16[128,128]{1,0:T(8,128)(2,1)} %sk_ref.1, bf16[128,128]{1,0:T(8,128)(2,1)} %sv_ref.1), custom_call_target="tpu_custom_call" | custom-call | tf_op jit(solution)/shard_map/pallas_call | solution.py:229
  2.0 3.9 %collective-permute-start.1 = (bf16[2304,128]{1,0:T(8,128)(2,1)}, bf16[2304,128]{1,0:T(8,128)(2,1)S(1)}, u32[]{:S(2)}, u32[]{:S(2)}) collective-permute-start(bf16[2304,128]{1,0:T(8,128)(2,1)} %shard_map.73), channel_id=1, source_target_pairs={{0,32},{8,40},{16,48},{24,56},{32,0},{40,8},{48,16},{56,24},{64,96... | collective-permute-start | bytes 1769480 | tf_op jit(solution)/shard_map/ppermute | solution.py:22
  5.9 3.4 %collective-permute-start = (bf16[2304,128]{1,0:T(8,128)(2,1)}, bf16[2304,128]{1,0:T(8,128)(2,1)S(1)}, u32[]{:S(2)}, u32[]{:S(2)}) collective-permute-start(bf16[2304,128]{1,0:T(8,128)(2,1)} %shard_map.73), channel_id=1, source_target_pairs={{0,16},{8,24},{16,0},{24,8},{32,48},{40,56},{48,32},{56,40},{64,80... | collective-permute-start | bytes 1769480 | tf_op jit(solution)/shard_map/ppermute | solution.py:22
  9.3 10.1 %collective-permute-done.1 = bf16[2304,128]{1,0:T(8,128)(2,1)S(1)} collective-permute-done((bf16[2304,128]{1,0:T(8,128)(2,1)}, bf16[2304,128]{1,0:T(8,128)(2,1)S(1)}, u32[]{:S(2)}, u32[]{:S(2)}) %collective-permute-start.1) | collective-permute-done | bytes 589856 | tf_op jit(solution)/shard_map/ppermute | solution.py:22
  19.4 3.4 %collective-permute-start.2 = (bf16[1152,128]{1,0:T(8,128)(2,1)S(1)}, bf16[1152,128]{1,0:T(8,128)(2,1)S(1)}, u32[]{:S(2)}, u32[]{:S(2)}) collective-permute-start(bf16[1152,128]{1,0:T(8,128)(2,1)S(1)} %slice.8), channel_id=1, source_target_pairs={{0,16},{8,24},{16,0},{24,8},{32,48},{40,56},{48,32},{56,40},{64,80... | collective-permute-start | bytes 884744 | tf_op jit(solution)/shard_map/ppermute | solution.py:22
  22.9 0.0 collective-permute-done
  22.9 0.0 copy-start.1
  22.9 3.6 %collective-permute-start.3 = (bf16[1152,128]{1,0:T(8,128)(2,1)S(1)}, bf16[1152,128]{1,0:T(8,128)(2,1)S(1)}, u32[]{:S(2)}, u32[]{:S(2)}) collective-permute-start(bf16[1152,128]{1,0:T(8,128)(2,1)S(1)} %slice.9), channel_id=1, source_target_pairs={{0,32},{8,40},{16,48},{24,56},{32,0},{40,8},{48,16},{56,24},{64,96... | collective-permute-start | bytes 884744 | tf_op jit(solution)/shard_map/ppermute | solution.py:22
  26.6 2.9 %collective-permute-done.2 = bf16[1152,128]{1,0:T(8,128)(2,1)S(1)} collective-permute-done((bf16[1152,128]{1,0:T(8,128)(2,1)S(1)}, bf16[1152,128]{1,0:T(8,128)(2,1)S(1)}, u32[]{:S(2)}, u32[]{:S(2)}) %collective-permute-start.2) | collective-permute-done | bytes 294944 | tf_op jit(solution)/shard_map/ppermute | solution.py:22
  29.4 3.2 %collective-permute-done.3 = bf16[1152,128]{1,0:T(8,128)(2,1)S(1)} collective-permute-done((bf16[1152,128]{1,0:T(8,128)(2,1)S(1)}, bf16[1152,128]{1,0:T(8,128)(2,1)S(1)}, u32[]{:S(2)}, u32[]{:S(2)}) %collective-permute-start.3) | collective-permute-done | bytes 294944 | tf_op jit(solution)/shard_map/ppermute | solution.py:22
  32.6 0.0 copy-done.3
  32.6 0.0 copy-start.6
  32.7 0.0 copy-start.5
  32.7 0.3 pad_maximum_fusion.refs_3_.refs_4_.refs_5_
  33.0 0.0 copy-done.1
  33.0 1.9 %collective-permute-start.4 = (bf16[4,2304,128]{2,1,0:T(8,128)(2,1)S(1)}, bf16[4,2304,128]{2,1,0:T(8,128)(2,1)}, u32[]{:S(2)}, u32[]{:S(2)}) collective-permute-start(bf16[4,2304,128]{2,1,0:T(8,128)(2,1)S(1)} %pad_maximum_fusion.refs_3_.refs_4_.refs_5_), channel_id=1, source_target_pairs={{0,8},{8,0},{16,24},{24,16},{32,40},{40,32},{48,56},{56,48},{64,72... | collective-permute-start | bytes 7077896 | tf_op jit(solution)/shard_map/ppermute | solution.py:22
  34.9 0.0 copy-done.6
  35.0 0.6 dynamic_slice.4
  35.5 0.0 copy-done.5
  35.6 0.7 concatenate.6.info_ref
  36.3 0.1 copy_bitcast_fusion
  36.3 0.0 copy-start.4
  36.3 1.1 %copy-done.4 = bf16[2304,128]{1,0:T(8,128)(2,1)S(1)} copy-done((bf16[2304,128]{1,0:T(8,128)(2,1)S(1)}, bf16[2304,128]{1,0:T(8,128)(2,1)}, u32[]{:S(2)}) %copy-start.4) | copy-done | bytes 589848
  37.5 3.4 %shard_map.74 = (f32[1024,1]{1,0:T(8,128)S(1)}, f32[1024,1]{1,0:T(8,128)S(1)}, f32[1024,128]{1,0:T(8,128)S(1)}) custom-call(s32[26]{0:T(128)S(1)} %concatenate.6.info_ref, bf16[1024,128]{1,0:T(8,128)(2,1)S(1)} %bitcast.24, bf16[1,2304,128]{2,1,0:T(8,128)(2,1)S(1)} %bitcast.29, bf16[1,2304,128]{2,1,0:T(8,128)(2,1)S(1)} %bitcast.30), custom_call_target="tpu_custom_call" | custom-call | flops 536870912 | bytes 524288 | tf_op jit(solution)/shard_map/pallas_call | solution.py:198
  40.9 0.0 copy-done.2
  40.9 5.8 %shard_map.75 = (f32[1024,1]{1,0:T(8,128)S(1)}, f32[1024,1]{1,0:T(8,128)S(1)}, f32[1024,128]{1,0:T(8,128)S(1)}) custom-call(s32[26]{0:T(128)S(1)} %concatenate.6.info_ref, bf16[1024,128]{1,0:T(8,128)(2,1)S(1)} %bitcast.25, f32[1024,1]{1,0:T(8,128)S(1)} %get-tuple-element.14.refs_0_, f32[1024,1]{1,0:T(8,128)S(1)} %get-tuple-element.15.refs_1_, ...), custom_call_target="tpu_custom_call" | custom-call | flops 1073741824 | bytes 1048576 | tf_op jit(solution)/shard_map/pallas_call | solution.py:198
  46.7 3.4 %shard_map.76 = (f32[1024,1]{1,0:T(8,128)S(1)}, f32[1024,1]{1,0:T(8,128)S(1)}, f32[1024,128]{1,0:T(8,128)S(1)}) custom-call(s32[26]{0:T(128)S(1)} %concatenate.6.info_ref, bf16[1024,128]{1,0:T(8,128)(2,1)S(1)} %bitcast.26, f32[1024,1]{1,0:T(8,128)S(1)} %get-tuple-element.17.refs_0_, f32[1024,1]{1,0:T(8,128)S(1)} %get-tuple-element.18.refs_1_, ...), custom_call_target="tpu_custom_call" | custom-call | flops 536870912 | bytes 524288 | tf_op jit(solution)/shard_map/pallas_call | solution.py:198
  50.1 0.0 collective-permute-done.4.refs_3_.refs_4_.refs_6_
  50.1 16.1 %shard_map.77 = bf16[128,1024]{1,0:T(8,128)(2,1)S(1)} custom-call(s32[26]{0:T(128)S(1)} %concatenate.6.info_ref, bf16[1024,128]{1,0:T(8,128)(2,1)S(1)} %bitcast.27, f32[1024,1]{1,0:T(8,128)S(1)} %get-tuple-element.20.refs_0_, f32[1024,1]{1,0:T(8,128)S(1)} %get-tuple-element.21.refs_1_, f32[1024,128]{1,0:T(8,128)S(1)} %get-tuple-element.22.refs_2_, ...), custom_call_target="tpu_custom_call" | custom-call | flops 2684354560 | bytes 2621440 | tf_op jit(solution)/shard_map/pallas_call | solution.py:198
  66.2 15.7 %all_to_all.19 = bf16[8,16,1024]{2,1,0:T(8,128)(2,1)S(1)} all-to-all(bf16[8,16,1024]{2,1,0:T(8,128)(2,1)S(1)} %bitcast.31), channel_id=1, replica_groups=mesh['req'=64,'tp'=8] {'tp'}, dimensions={0} | all-to-all | bytes 524288 | tf_op jit(solution)/shard_map/all_to_all | solution.py:280
  81.9 0.7 copy.11
  (8 shorter events, 0.1 us)
Async XLA Ops:
  0.0 36.3 %copy-start = (bf16[128,1024]{1,0:T(8,128)(2,1)S(1)}, bf16[128,1024]{1,0:T(8,128)(2,1)}, u32[]{:S(2)}) copy-start(bf16[128,1024]{1,0:T(8,128)(2,1)} %param.7) | copy-start | bytes 786436
  1.9 30.7 %copy-start.3 = (bf16[2304,128]{1,0:T(8,128)(2,1)S(1)}, bf16[2304,128]{1,0:T(8,128)(2,1)}, u32[]{:S(2)}) copy-start(bf16[2304,128]{1,0:T(8,128)(2,1)} %shard_map.73) | copy-start | bytes 1769476
  2.0 17.5 %collective-permute-start.1 = (bf16[2304,128]{1,0:T(8,128)(2,1)}, bf16[2304,128]{1,0:T(8,128)(2,1)S(1)}, u32[]{:S(2)}, u32[]{:S(2)}) collective-permute-start(bf16[2304,128]{1,0:T(8,128)(2,1)} %shard_map.73), channel_id=1, source_target_pairs={{0,32},{8,40},{16,48},{24,56},{32,0},{40,8},{48,16},{56,24},{64,96... | collective-permute-start | bytes 1769480 | tf_op jit(solution)/shard_map/ppermute | solution.py:22
  5.9 17.0 %collective-permute-start = (bf16[2304,128]{1,0:T(8,128)(2,1)}, bf16[2304,128]{1,0:T(8,128)(2,1)S(1)}, u32[]{:S(2)}, u32[]{:S(2)}) collective-permute-start(bf16[2304,128]{1,0:T(8,128)(2,1)} %shard_map.73), channel_id=1, source_target_pairs={{0,16},{8,24},{16,0},{24,8},{32,48},{40,56},{48,32},{56,40},{64,80... | collective-permute-start | bytes 1769480 | tf_op jit(solution)/shard_map/ppermute | solution.py:22
  19.4 10.0 %collective-permute-start.2 = (bf16[1152,128]{1,0:T(8,128)(2,1)S(1)}, bf16[1152,128]{1,0:T(8,128)(2,1)S(1)}, u32[]{:S(2)}, u32[]{:S(2)}) collective-permute-start(bf16[1152,128]{1,0:T(8,128)(2,1)S(1)} %slice.8), channel_id=1, source_target_pairs={{0,16},{8,24},{16,0},{24,8},{32,48},{40,56},{48,32},{56,40},{64,80... | collective-permute-start | bytes 884744 | tf_op jit(solution)/shard_map/ppermute | solution.py:22
  22.9 10.1 %copy-start.1 = (bf16[2304,128]{1,0:T(8,128)(2,1)}, bf16[2304,128]{1,0:T(8,128)(2,1)S(1)}, u32[]{:S(2)}) copy-start(bf16[2304,128]{1,0:T(8,128)(2,1)S(1)} %collective-permute-done) | copy-start | bytes 1769476
  22.9 9.7 %collective-permute-start.3 = (bf16[1152,128]{1,0:T(8,128)(2,1)S(1)}, bf16[1152,128]{1,0:T(8,128)(2,1)S(1)}, u32[]{:S(2)}, u32[]{:S(2)}) collective-permute-start(bf16[1152,128]{1,0:T(8,128)(2,1)S(1)} %slice.9), channel_id=1, source_target_pairs={{0,32},{8,40},{16,48},{24,56},{32,0},{40,8},{48,16},{56,24},{64,96... | collective-permute-start | bytes 884744 | tf_op jit(solution)/shard_map/ppermute | solution.py:22
  32.6 2.3 %copy-start.6 = (s32[8]{0:T(128)S(1)}, s32[8]{0:T(128)}, u32[]{:S(2)}) copy-start(s32[8]{0:T(128)} %param.12) | copy-start | bytes 100
  32.7 2.9 %copy-start.5 = (s32[8]{0:T(128)S(1)}, s32[8]{0:T(128)}, u32[]{:S(2)}) copy-start(s32[8]{0:T(128)} %constant.43.clone) | copy-start | bytes 100
  33.0 17.1 %collective-permute-start.4 = (bf16[4,2304,128]{2,1,0:T(8,128)(2,1)S(1)}, bf16[4,2304,128]{2,1,0:T(8,128)(2,1)}, u32[]{:S(2)}, u32[]{:S(2)}) collective-permute-start(bf16[4,2304,128]{2,1,0:T(8,128)(2,1)S(1)} %pad_maximum_fusion.refs_3_.refs_4_.refs_5_), channel_id=1, source_target_pairs={{0,8},{8,0},{16,24},{24,16},{32,40},{40,32},{48,56},{56,48},{64,72... | collective-permute-start | bytes 7077896 | tf_op jit(solution)/shard_map/ppermute | solution.py:22
  36.3 4.6 %copy-start.2 = (bf16[2304,128]{1,0:T(8,128)(2,1)S(1)}, bf16[2304,128]{1,0:T(8,128)(2,1)}, u32[]{:S(2)}) copy-start(bf16[2304,128]{1,0:T(8,128)(2,1)} %copy-done.1) | copy-start | bytes 1769476
  36.3 1.1 %copy-start.4 = (bf16[2304,128]{1,0:T(8,128)(2,1)S(1)}, bf16[2304,128]{1,0:T(8,128)(2,1)}, u32[]{:S(2)}) copy-start(bf16[2304,128]{1,0:T(8,128)(2,1)} %shard_map.73) | copy-start | bytes 1769476
